TPU v7x, 256 devices: a whole 4x4x8 slice. The times are simulated.
256 devices in a mesh: dp: 16 (over z_lo, x), tensor: 16 (over z_hi, y, core).
Axes of the slice: x: 4, y: 4, z: 8 (z_hi: 2, z_lo: 4; z = z_hi * 4 + z_lo), core: 2. Of those that a mesh axis runs over, the one named last changes fastest.
Arguments:
- cotangent: bfloat16 [8192, 4096], P(('dp', 'tensor')), may hold values from -6 to 6
- gate: bfloat16 [8192, 14336], P('dp', 'tensor'), may hold values from -8 to 8
- up: bfloat16 [8192, 14336], P('dp', 'tensor'), may hold values from -6 to 6
- w_down: bfloat16 [4, 14336, 4096], P(None, 'tensor', 'dp'), may hold values from -0.03125 to 0.03125
- language: int32 [16], replicated, may hold values from 0 to 3
Outputs:
- d_gate: bfloat16 [8192, 14336], P('dp', 'tensor')
- d_up: bfloat16 [8192, 14336], P('dp', 'tensor')
- d_weight: float32 [4, 14336, 4096], P(None, 'tensor', 'dp')
All inputs are finite; a program needn't handle non-finite values.
Results may differ from a plain program's by a relative error of at most 0.0029.
Values may be sent and summed in bfloat16 or wider, within the bound.
No kernel may reach another device: no remote copies, remote signals or barrier semaphores. Data moves between devices by JAX's collectives and lax.ppermute only.
A program may use at most 128 MiB of HBM per device.

v0:
```python
import jax
import jax.numpy as jnp
from jax import lax
from jax.sharding import PartitionSpec as P


def shards(cotangent, gate, up, w_down, language):
    groups = lax.axis_size("dp")
    variants = w_down.shape[0]
    ff_dev = w_down.shape[1]
    feat_dev = w_down.shape[2]
    out_rows = lax.all_gather(cotangent, "tensor", axis=0, tiled=True)
    gate_f = gate.astype(jnp.float32)
    up_f = up.astype(jnp.float32)
    sig = jax.nn.sigmoid(gate_f)
    act = gate_f * sig
    hidden = (act * up_f).astype(jnp.bfloat16)
    slabs = jnp.take(w_down, language, axis=0)
    received = lax.all_to_all(slabs, "dp", split_axis=0, concat_axis=2, tiled=True)
    weights = received[0]
    d_hidden = lax.dot_general(
        out_rows, weights, (((1,), (1,)), ((), ())), preferred_element_type=jnp.float32
    )
    d_up = (d_hidden * act).astype(jnp.bfloat16)
    d_gate = (d_hidden * up_f * sig * (1.0 + gate_f * (1.0 - sig))).astype(jnp.bfloat16)
    selector = (language[None, :] == jnp.arange(variants, dtype=jnp.int32)[:, None]).astype(
        jnp.float32
    )
    partial_term = lax.dot_general(
        hidden, out_rows, (((0,), (0,)), ((), ())), preferred_element_type=jnp.float32
    )
    pieces = lax.all_to_all(
        partial_term.reshape(ff_dev, groups, feat_dev),
        "dp",
        split_axis=1,
        concat_axis=1,
        tiled=True,
    )
    d_weight = jnp.einsum("lg,fgd->lfd", selector, pieces, precision=lax.Precision.HIGHEST)
    return (d_gate, d_up, d_weight)


def solution(mesh):
    return jax.shard_map(
        shards,
        mesh=mesh,
        in_specs=(
            P(("dp", "tensor"), None),
            P("dp", "tensor"),
            P("dp", "tensor"),
            P(None, "tensor", "dp"),
            P(),
        ),
        out_specs=(P("dp", "tensor"), P("dp", "tensor"), P(None, "tensor", "dp")),
        check_vma=False,
    )
```

profile of v0, /device:TPU:228, one launch (start us, length us, event | category | flops | bytes accessed | tf_op | source)
XLA Modules:
  0.0 563.7 jit_solution(13106661074899269644)
XLA Ops:
  7.2 0.0 copy-start
  7.2 0.8 compare_and_fusion
  8.0 0.7 compare_select_fusion
  8.6 0.0 copy-done
  8.7 4.0 gather_fusion
  12.7 6.9 %broadcast_select_fusion = bf16[16,896,256]{2,1,0:T(8,128)(2,1)} fusion(bf16[16,896,256]{2,1,0:T(8,128)(2,1)} %gather_fusion, pred[16]{0:T(512)(128)(4,1)S(1)} %compare_and_fusion), kind=kLoop, calls=%fused_computation.4 | loop fusion | flops 3670016 | bytes 14680080 | tf_op jit(solution)/shard_map/jit(_take)/select_n | solution.py:18
  19.6 7.7 %all-to-all-start = ((bf16[16,896,256]{2,1,0:T(8,128)(2,1)}), bf16[16,896,256]{2,1,0:T(8,128)(2,1)}, u32[]{:S(2)}, u32[]{:S(2)}) async-start(bf16[16,896,256]{2,1,0:T(8,128)(2,1)} %broadcast_select_fusion), calls=%async_computation | async-start | bytes 14680064 | tf_op jit(solution)/shard_map/all_to_all | solution.py:19
  27.2 0.0 all-gather.2.cloned.1.call-start
  27.3 0.7 all-gather.2.cloned.1.call-update
  28.0 0.0 copy-done.2
  28.0 0.5 copy.26
  28.5 0.5 copy.25
  29.1 80.8 %all-gather.2.cloned.1.call-done = bf16[512,4096]{1,0:T(8,128)(2,1)} async-done(((bf16[32,4096]{1,0:T(8,128)(2,1)}), bf16[512,4096]{1,0:T(8,128)(2,1)}) %all-gather.2.cloned.1.call-update) | async-done | bytes 4194320 | tf_op jit(solution)/shard_map/all_gather | solution.py:12
  109.9 9.5 %fusion.11 = f32[896,4096]{1,0:T(8,128)} fusion(bf16[512,4096]{1,0:T(8,128)(2,1)} %all-gather.2.cloned.1.call-done, bf16[512,896]{0,1:T(8,128)(2,1)S(1)} %copy.25, bf16[512,896]{0,1:T(8,128)(2,1)S(1)} %copy.26), kind=kOutput, calls=%fused_computation.20 | convolution fusion | flops 3761766400 | bytes 20709376 | tf_op jit(solution)/shard_map/dot_general | solution.py:29
  119.4 12.0 %copy.36 = f32[112,16,8,256]{3,2,0,1:T(8,128)} copy(f32[112,16,8,256]{3,2,1,0:T(8,128)} %bitcast.20) | data formatting | bytes 29360128 | tf_op jit(solution)/shard_map/reshape | solution.py:33
  131.4 82.3 %all-to-all-done = bf16[16,896,256]{2,1,0:T(8,128)(2,1)} async-done(((bf16[16,896,256]{2,1,0:T(8,128)(2,1)}), bf16[16,896,256]{2,1,0:T(8,128)(2,1)}, u32[]{:S(2)}, u32[]{:S(2)}) %all-to-all-start) | async-done | bytes 7340064 | tf_op jit(solution)/shard_map/all_to_all | solution.py:19
  213.7 7.5 %all-to-all-start.1 = ((f32[896,16,256]{2,0,1:T(8,128)}), f32[896,16,256]{2,0,1:T(8,128)}, u32[]{:S(2)}, u32[]{:S(2)}) async-start(f32[896,16,256]{2,0,1:T(8,128)} %bitcast.19), calls=%async_computation.1 | async-start | bytes 29360128 | tf_op jit(solution)/shard_map/all_to_all | solution.py:32
  221.2 11.1 %copy.24 = bf16[1,896,16,256]{1,3,2,0:T(8,128)(2,1)} copy(bf16[1,896,16,256]{3,1,2,0:T(8,128)(2,1)} %bitcast.1) | data formatting | bytes 14680064 | tf_op jit(solution)/shard_map/all_to_all | solution.py:19
  232.4 9.8 %fusion.10 = (bf16[512,896]{0,1:T(8,128)(2,1)}, bf16[512,896]{0,1:T(8,128)(2,1)S(1)}) fusion(bf16[512,896]{0,1:T(8,128)(2,1)S(1)} %copy.26, bf16[512,896]{0,1:T(8,128)(2,1)S(1)} %copy.25, bf16[896,4096]{0,1:T(8,128)(2,1)} %bitcast.21, bf16[512,4096]{1,0:T(8,128)(2,1)} %all-gather.2.cloned.1.call-done), kind=kOutput, calls=%fused_computation.19 | convolution fusion | flops 3764977664 | bytes 15204352 | tf_op jit(solution)/shard_map/dot_general | solution.py:21
  242.2 2.2 copy.30
  244.4 1.3 copy.29
  245.7 290.4 %all-to-all-done.1 = f32[896,16,256]{2,0,1:T(8,128)} async-done(((f32[896,16,256]{2,0,1:T(8,128)}), f32[896,16,256]{2,0,1:T(8,128)}, u32[]{:S(2)}, u32[]{:S(2)}) %all-to-all-start.1) | async-done | bytes 14680096 | tf_op jit(solution)/shard_map/all_to_all | solution.py:32
  536.1 18.3 %fusion = f32[4,896,256]{2,0,1:T(4,128)S(1)} fusion(f32[896,16,256]{2,0,1:T(8,128)} %all-to-all-done.1, s32[16]{0:T(128)S(1)} %copy-done.4), kind=kOutput, calls=%fused_computation.2 | convolution fusion | flops 176160832 | bytes 18350144 | tf_op jit(solution)/shard_map/lg,fgd->lfd/dot_general | solution.py:39
  554.4 2.5 copy.31
  (8 shorter events, 0.0 us)
Async XLA Ops:
  7.2 1.5 copy-start
  19.6 8.4 %copy-start.2 = (bf16[512,896]{1,0:T(8,128)(2,1)S(1)}, bf16[512,896]{1,0:T(8,128)(2,1)}, u32[]{:S(2)}) copy-start(bf16[512,896]{1,0:T(8,128)(2,1)} %param.6) | copy-start | bytes 2752516
  19.6 8.9 %copy-start.3 = (bf16[512,896]{1,0:T(8,128)(2,1)S(1)}, bf16[512,896]{1,0:T(8,128)(2,1)}, u32[]{:S(2)}) copy-start(bf16[512,896]{1,0:T(8,128)(2,1)} %param.7) | copy-start | bytes 2752516
  19.6 194.1 %all-to-all-start = ((bf16[16,896,256]{2,1,0:T(8,128)(2,1)}), bf16[16,896,256]{2,1,0:T(8,128)(2,1)}, u32[]{:S(2)}, u32[]{:S(2)}) async-start(bf16[16,896,256]{2,1,0:T(8,128)(2,1)} %broadcast_select_fusion), calls=%async_computation | async-start | bytes 14680064 | tf_op jit(solution)/shard_map/all_to_all | solution.py:19
  27.2 82.7 %all-gather.2.cloned.1.call-start = ((), (), s32[]{:S(2)}) async-start(), calls=%async_computation.2 | async-start | bytes 4456448 | tf_op jit(solution)/shard_map/all_gather | solution.py:12
  213.7 322.4 %all-to-all-start.1 = ((f32[896,16,256]{2,0,1:T(8,128)}), f32[896,16,256]{2,0,1:T(8,128)}, u32[]{:S(2)}, u32[]{:S(2)}) async-start(f32[896,16,256]{2,0,1:T(8,128)} %bitcast.19), calls=%async_computation.1 | async-start | bytes 29360128 | tf_op jit(solution)/shard_map/all_to_all | solution.py:32
  242.2 293.9 %copy-start.4 = (s32[16]{0:T(128)S(1)}, s32[16]{0:T(128)}, u32[]{:S(2)}) copy-start(s32[16]{0:T(128)} %param.9) | copy-start | bytes 196
  536.1 20.8 %copy-start.1 = (bf16[4,896,256]{2,1,0:T(8,128)(2,1)S(1)}, bf16[4,896,256]{2,1,0:T(8,128)(2,1)}, u32[]{:S(2)}) copy-start(bf16[4,896,256]{2,1,0:T(8,128)(2,1)} %param.8) | copy-start | bytes 5505028
Sparse Core Ops, SparseCore 0:
  30.8 79.0 all-gather.1
where the time goes:
time: 567 us; the launch traced here: 564 us
  waiting for transfers between devices  454 us (80%)
  matrix products  37.6 us (7%)
  local copies, waits for them, and re-layouts  34.2 us (6%)
  starting transfers between devices  15.2 us (3%)
  between operations  14.1 us (2%)
  other arithmetic  8.33 us (1%)
    all_to_all x1, waiting for transfers between devices, shards(): lax.all_to_all(partial_term.reshape(ff_dev, groups, feat_dev), 'dp', spli...  290 us
    all_to_all x1, waiting for transfers between devices, shards(): lax.all_to_all(slabs, 'dp', split_axis=0, concat_axis=2, tiled=True)  82.3 us
    all_gather x1, waiting for transfers between devices, shards(): out_rows = lax.all_gather(cotangent, 'tensor', axis=0, tiled=True)  80.8 us
    dot_general x1, matrix products, shards(): jnp.einsum('lg,fgd->lfd', selector, pieces, precision=lax.Precision.HIGHEST)  18.3 us
    reshape x1, local copies, waits for them, and re-layouts, shards(): partial_term.reshape(ff_dev, groups, feat_dev)  12 us
  transfers between devices with their start and end apart: 3, of which 3 were waited for; matrix products, arithmetic and copies ran while one was open for 8% of the time, Pallas kernels for 0%

commit v1 on v0

v1 whole, which is shorter than its diff:
```python
import jax
import jax.numpy as jnp
from jax import lax
from jax.sharding import Mesh
from jax.sharding import PartitionSpec as P

DP = ("zl", "x")
TP = ("zh", "y", "c")


def shards(cotangent, gate, up, w_down, language):
    groups = lax.axis_size(DP)
    variants = w_down.shape[0]
    ff_dev = w_down.shape[1]
    feat_dev = w_down.shape[2]
    rows_dev, feats = cotangent.shape
    cores = lax.axis_size("c")
    chip_rows = lax.all_gather(cotangent, ("zh", "y"), axis=0, tiled=False)
    both = lax.all_gather(chip_rows, "c", axis=0, tiled=False)
    out_rows = jnp.swapaxes(both, 0, 1).reshape(-1, feats)
    gate_f = gate.astype(jnp.float32)
    up_f = up.astype(jnp.float32)
    sig = jax.nn.sigmoid(gate_f)
    act = gate_f * sig
    hidden = (act * up_f).astype(jnp.bfloat16)
    slabs = jnp.take(w_down, language, axis=0)
    received = lax.all_to_all(slabs, DP, split_axis=0, concat_axis=2, tiled=True)
    weights = received[0]
    d_hidden = lax.dot_general(
        out_rows, weights, (((1,), (1,)), ((), ())), preferred_element_type=jnp.float32
    )
    d_up = (d_hidden * act).astype(jnp.bfloat16)
    d_gate = (d_hidden * up_f * sig * (1.0 + gate_f * (1.0 - sig))).astype(jnp.bfloat16)
    selector = (language[None, :] == jnp.arange(variants, dtype=jnp.int32)[:, None]).astype(
        jnp.bfloat16
    )
    partial_term = lax.dot_general(
        hidden, out_rows, (((0,), (0,)), ((), ())), preferred_element_type=jnp.float32
    ).astype(jnp.bfloat16)
    pieces = lax.all_to_all(
        partial_term.reshape(ff_dev, groups, feat_dev),
        DP,
        split_axis=1,
        concat_axis=1,
        tiled=True,
    )
    d_weight = jnp.einsum("lg,fgd->lfd", selector, pieces, preferred_element_type=jnp.float32)
    return (d_gate, d_up, d_weight)


def solution(mesh):
    sub = Mesh(mesh.devices.reshape(4, 4, 2, 4, 2), DP + TP)
    return jax.shard_map(
        shards,
        mesh=sub,
        in_specs=(
            P(DP + TP, None),
            P(DP, TP),
            P(DP, TP),
            P(None, TP, DP),
            P(),
        ),
        out_specs=(P(DP, TP), P(DP, TP), P(None, TP, DP)),
        check_vma=False,
    )
```

time: 567 us -> 399 us (0.70)
  waiting for transfers between devices: 454 us -> 307 us
  matrix products: 37.6 us -> 21.8 us
    all_to_all x2, waiting for transfers between devices: 373 us -> 161 us  [the longest x1 133 us: shards(): lax.all_to_all(partial_term.reshape(ff_dev, groups, feat_dev), DP, split_...]
    all_gather x1 -> x2, waiting for transfers between devices: 80.8 us -> 145 us  [the longest x1 80.8 us: shards(): chip_rows = lax.all_gather(cotangent, ('zh', 'y'), axis=0, tiled=False)]
    dot_general x1, matrix products: 18.3 us -> 7.53 us  [shards(): jnp.einsum('lg,fgd->lfd', selector, pieces, preferred_element_type=jnp.fl...]
    reshape x1, local copies, waits for them, and re-layouts: 12 us -> 3.75 us  [shards(): partial_term.reshape(ff_dev, groups, feat_dev)]
  transfers between devices with their start and end apart: 3 -> 4, of which waited for: 3 -> 4; matrix products, arithmetic and copies ran while one was open for 8% -> 9% of each run, Pallas kernels for 0% -> 0%
where the time goes in v1:
time: 399 us; the launch traced here: 395 us
  waiting for transfers between devices  307 us (77%)
  local copies, waits for them, and re-layouts  28.7 us (7%)
  matrix products  21.8 us (5%)
  starting transfers between devices  15.3 us (4%)
  between operations  14.1 us (4%)
  other arithmetic  8.24 us (2%)
    all_to_all x1, waiting for transfers between devices, shards(): lax.all_to_all(partial_term.reshape(ff_dev, groups, feat_dev), DP, split_...  133 us
    all_gather x1, waiting for transfers between devices, shards(): chip_rows = lax.all_gather(cotangent, ('zh', 'y'), axis=0, tiled=False)  80.8 us
    all_gather x1, waiting for transfers between devices, shards(): both = lax.all_gather(chip_rows, 'c', axis=0, tiled=False)  64.5 us
    all_to_all x1, waiting for transfers between devices, shards(): lax.all_to_all(slabs, DP, split_axis=0, concat_axis=2, tiled=True)  28.3 us
    all_to_all x1, local copies, waits for them, and re-layouts, shards(): lax.all_to_all(slabs, DP, split_axis=0, concat_axis=2, tiled=True)  11.2 us
    dot_general x1, matrix products, shards(): lax.dot_general(out_rows, weights, (((1,), (1,)), ((), ())), preferred_el...  9.81 us
  transfers between devices with their start and end apart: 4, of which 4 were waited for; matrix products, arithmetic and copies ran while one was open for 9% of the time, Pallas kernels for 0%

profile of v1, /device:TPU:228, one launch (start us, length us, event | category | flops | bytes accessed | tf_op | source)
XLA Modules:
  0.0 395.5 jit_solution(9383245005647268694)
XLA Ops:
  7.2 0.8 compare_select_fusion
  8.0 0.7 compare_and_fusion
  8.6 0.0 copy-done
  8.7 3.9 gather_fusion
  12.6 6.8 %broadcast_select_fusion = bf16[16,896,256]{2,1,0:T(8,128)(2,1)} fusion(bf16[16,896,256]{2,1,0:T(8,128)(2,1)} %gather_fusion, pred[16]{0:T(512)(128)(4,1)S(1)} %compare_and_fusion), kind=kLoop, calls=%fused_computation.4 | loop fusion | flops 3670016 | bytes 14680080 | tf_op jit(solution)/shard_map/jit(_take)/select_n | solution.py:26
  19.4 7.7 %all-to-all-start = ((bf16[16,896,256]{2,1,0:T(8,128)(2,1)}), bf16[16,896,256]{2,1,0:T(8,128)(2,1)}, u32[]{:S(2)}, u32[]{:S(2)}) async-start(bf16[16,896,256]{2,1,0:T(8,128)(2,1)} %broadcast_select_fusion), calls=%async_computation | async-start | bytes 14680064 | tf_op jit(solution)/shard_map/all_to_all | solution.py:27
  27.1 0.0 all-gather.5.cloned.1.call-start
  27.1 0.7 all-gather.5.cloned.1.call-update
  27.9 80.8 %all-gather.5.cloned.1.call-done = bf16[256,4096]{1,0:T(8,128)(2,1)} async-done(((bf16[32,4096]{1,0:T(8,128)(2,1)}), bf16[256,4096]{1,0:T(8,128)(2,1)}) %all-gather.5.cloned.1.call-update) | async-done | bytes 2097168 | tf_op jit(solution)/shard_map/all_gather | solution.py:18
  108.7 0.5 copy.28
  109.2 0.5 copy.27
  109.8 64.5 %all-gather.7.cloned.1.call-done = bf16[16,32,4096]{2,1,0:T(8,128)(2,1)} async-done(((bf16[8,32,4096]{2,1,0:T(8,128)(2,1)}), bf16[16,32,4096]{2,1,0:T(8,128)(2,1)}) %all-gather.7.cloned.1.call-update) | async-done | bytes 4194320 | tf_op jit(solution)/shard_map/all_gather | solution.py:19
  174.3 2.7 copy.26
  177.0 4.5 %convolution_convert_fusion = bf16[896,4096]{1,0:T(8,128)(2,1)S(1)} fusion(bf16[512,4096]{1,0:T(8,128)(2,1)S(1)} %bitcast.27, bf16[512,896]{0,1:T(8,128)(2,1)S(1)} %copy.27, bf16[512,896]{0,1:T(8,128)(2,1)S(1)} %copy.28), kind=kOutput, calls=%fused_computation.5 | convolution fusion | flops 3765436416 | bytes 13369344 | tf_op jit(solution)/shard_map/dot_general | solution.py:37
  181.5 3.8 copy.38
  185.2 28.3 %all-to-all-done = bf16[16,896,256]{2,1,0:T(8,128)(2,1)} async-done(((bf16[16,896,256]{2,1,0:T(8,128)(2,1)}), bf16[16,896,256]{2,1,0:T(8,128)(2,1)}, u32[]{:S(2)}, u32[]{:S(2)}) %all-to-all-start) | async-done | bytes 7340064 | tf_op jit(solution)/shard_map/all_to_all | solution.py:27
  213.5 7.5 %all-to-all-start.1 = ((bf16[896,16,256]{2,0,1:T(8,128)(2,1)}), bf16[896,16,256]{2,0,1:T(8,128)(2,1)}, u32[]{:S(2)}, u32[]{:S(2)}) async-start(bf16[896,16,256]{2,0,1:T(8,128)(2,1)} %bitcast.24), calls=%async_computation.1 | async-start | bytes 14680064 | tf_op jit(solution)/shard_map/all_to_all | solution.py:40
  221.1 11.2 %copy.25 = bf16[1,896,16,256]{1,3,2,0:T(8,128)(2,1)} copy(bf16[1,896,16,256]{3,1,2,0:T(8,128)(2,1)} %bitcast.1) | data formatting | bytes 14680064 | tf_op jit(solution)/shard_map/all_to_all | solution.py:27
  232.2 9.8 %fusion.10 = (bf16[512,896]{0,1:T(8,128)(2,1)S(1)}, bf16[512,896]{0,1:T(8,128)(2,1)}) fusion(bf16[512,896]{0,1:T(8,128)(2,1)S(1)} %copy.28, bf16[512,896]{0,1:T(8,128)(2,1)S(1)} %copy.27, bf16[896,4096]{0,1:T(8,128)(2,1)} %bitcast.25, bf16[512,4096]{1,0:T(8,128)(2,1)} %bitcast.28), kind=kOutput, calls=%fused_computation.20 | convolution fusion | flops 3764977664 | bytes 15204352 | tf_op jit(solution)/shard_map/dot_general | solution.py:29
  242.1 2.2 copy.31
  244.3 1.3 copy.32
  245.5 133.0 %all-to-all-done.1 = bf16[896,16,256]{2,0,1:T(8,128)(2,1)} async-done(((bf16[896,16,256]{2,0,1:T(8,128)(2,1)}), bf16[896,16,256]{2,0,1:T(8,128)(2,1)}, u32[]{:S(2)}, u32[]{:S(2)}) %all-to-all-start.1) | async-done | bytes 7340064 | tf_op jit(solution)/shard_map/all_to_all | solution.py:40
  378.6 7.5 %fusion = f32[4,896,256]{2,0,1:T(4,128)S(1)} fusion(bf16[896,16,256]{2,0,1:T(8,128)(2,1)} %all-to-all-done.1, s32[16]{0:T(128)S(1)} %copy-done.5), kind=kOutput, calls=%fused_computation.2 | convolution fusion | flops 29360192 | bytes 11010112 | tf_op jit(solution)/shard_map/lg,fgd->lfd/dot_general | solution.py:47
  386.1 2.5 copy.33
  (14 shorter events, 0.1 us)
Async XLA Ops:
  7.2 1.5 copy-start
  19.4 89.3 %copy-start.3 = (bf16[512,896]{1,0:T(8,128)(2,1)S(1)}, bf16[512,896]{1,0:T(8,128)(2,1)}, u32[]{:S(2)}) copy-start(bf16[512,896]{1,0:T(8,128)(2,1)} %param.6) | copy-start | bytes 2752516
  19.4 194.1 %all-to-all-start = ((bf16[16,896,256]{2,1,0:T(8,128)(2,1)}), bf16[16,896,256]{2,1,0:T(8,128)(2,1)}, u32[]{:S(2)}, u32[]{:S(2)}) async-start(bf16[16,896,256]{2,1,0:T(8,128)(2,1)} %broadcast_select_fusion), calls=%async_computation | async-start | bytes 14680064 | tf_op jit(solution)/shard_map/all_to_all | solution.py:27
  27.1 82.2 %copy-start.4 = (bf16[512,896]{1,0:T(8,128)(2,1)S(1)}, bf16[512,896]{1,0:T(8,128)(2,1)}, u32[]{:S(2)}) copy-start(bf16[512,896]{1,0:T(8,128)(2,1)} %param.7) | copy-start | bytes 2752516
  27.1 81.6 %all-gather.5.cloned.1.call-start = ((), (), s32[]{:S(2)}) async-start(), calls=%async_computation.2 | async-start | bytes 2359296 | tf_op jit(solution)/shard_map/all_gather | solution.py:18
  27.8 146.5 %all-gather.7.cloned.1.call-start = ((), (), s32[]{:S(2)}) async-start(), calls=%async_computation.3 | async-start | bytes 6291456 | tf_op jit(solution)/shard_map/all_gather | solution.py:19
  177.0 4.5 %copy-start.2 = (bf16[8,2,32,4096]{3,2,1,0:T(8,128)(2,1)}, bf16[8,2,32,4096]{3,2,1,0:T(8,128)(2,1)S(1)}, u32[]{:S(2)}) copy-start(bf16[8,2,32,4096]{3,2,1,0:T(8,128)(2,1)S(1)} %copy.26) | copy-start | bytes 12582916
  213.5 165.1 %all-to-all-start.1 = ((bf16[896,16,256]{2,0,1:T(8,128)(2,1)}), bf16[896,16,256]{2,0,1:T(8,128)(2,1)}, u32[]{:S(2)}, u32[]{:S(2)}) async-start(bf16[896,16,256]{2,0,1:T(8,128)(2,1)} %bitcast.24), calls=%async_computation.1 | async-start | bytes 14680064 | tf_op jit(solution)/shard_map/all_to_all | solution.py:40
  242.1 136.5 %copy-start.5 = (s32[16]{0:T(128)S(1)}, s32[16]{0:T(128)}, u32[]{:S(2)}) copy-start(s32[16]{0:T(128)} %param.9) | copy-start | bytes 196
  378.6 10.0 %copy-start.1 = (bf16[4,896,256]{2,1,0:T(8,128)(2,1)S(1)}, bf16[4,896,256]{2,1,0:T(8,128)(2,1)}, u32[]{:S(2)}) copy-start(bf16[4,896,256]{2,1,0:T(8,128)(2,1)} %param.8) | copy-start | bytes 5505028
Sparse Core Ops, SparseCore 0:
  30.5 78.0 all-gather.4
  110.4 63.8 all-gather.6

commit v2 on v1

--- a/solution.py
+++ b/solution.py
@@ -15,15 +15,27 @@
     feat_dev = w_down.shape[2]
     rows_dev, feats = cotangent.shape
     cores = lax.axis_size("c")
-    chip_rows = lax.all_gather(cotangent, ("zh", "y"), axis=0, tiled=False)
-    both = lax.all_gather(chip_rows, "c", axis=0, tiled=False)
-    out_rows = jnp.swapaxes(both, 0, 1).reshape(-1, feats)
+    partner = lax.ppermute(cotangent, "zh", [(0, 1), (1, 0)])
+    first = lax.axis_index("zh") == 0
+    pair = jnp.where(first, jnp.stack([cotangent, partner]), jnp.stack([partner, cotangent]))
+    ring = lax.axis_size("y")
+    me_y = lax.axis_index("y")
+    got = [pair]
+    for shift in range(1, ring):
+        got.append(lax.ppermute(pair, "y", [(i, (i + shift) % ring) for i in range(ring)]))
+    by_y = jnp.stack(got)
+    order = (me_y - jnp.arange(ring)) % ring
+    by_y = jnp.take(by_y, jnp.argsort(order), axis=0, mode="clip")
+    other = lax.ppermute(by_y, "c", [(0, 1), (1, 0)])
+    first_c = lax.axis_index("c") == 0
+    both = jnp.where(first_c, jnp.stack([by_y, other]), jnp.stack([other, by_y]))
+    out_rows = jnp.transpose(both, (2, 1, 0, 3, 4)).reshape(-1, feats)
     gate_f = gate.astype(jnp.float32)
     up_f = up.astype(jnp.float32)
     sig = jax.nn.sigmoid(gate_f)
     act = gate_f * sig
     hidden = (act * up_f).astype(jnp.bfloat16)
-    slabs = jnp.take(w_down, language, axis=0)
+    slabs = jnp.take(w_down, language, axis=0, mode="clip")
     received = lax.all_to_all(slabs, DP, split_axis=0, concat_axis=2, tiled=True)
     weights = received[0]
     d_hidden = lax.dot_general(

time: 399 us -> 380 us (0.952)
  between operations: 14.1 us -> 0.72 us
  waiting for transfers between devices: 307 us -> 294 us
  starting transfers between devices: 15.3 us -> 21.5 us
    ppermute x0 -> x5, waiting for transfers between devices: none -> 157 us  [the longest x1 129 us: shards(): partner = lax.ppermute(cotangent, 'zh', [(0, 1), (1, 0)])]
    all_gather x2 -> x0, waiting for transfers between devices: 145 us -> none  [the longest x1 80.8 us: shards(): chip_rows = lax.all_gather(cotangent, ('zh', 'y'), axis=0, tiled=False)]
    all_to_all x1, waiting for transfers between devices: 28.3 us -> 0.01 us  [shards(): lax.all_to_all(slabs, DP, split_axis=0, concat_axis=2, tiled=True)]
    select_n x2 -> x3, other arithmetic: 7.58 us -> 0.16 us  [the longest x2 0.15 us: shards(): jnp.where(first, jnp.stack([cotangent, partner]), jnp.stack([partner, cot...]
    ppermute x0 -> x5, starting transfers between devices: none -> 6.34 us  [the longest x3 4.69 us: shards(): lax.ppermute(pair, 'y', [(i, (i + shift) % ring) for i in range(ring)])]
    transpose x0 -> x1, other arithmetic: none -> 4.17 us  [shards(): out_rows = jnp.transpose(both, (2, 1, 0, 3, 4)).reshape(-1, feats)]
  transfers between devices with their start and end apart: 4 -> 7, of which waited for: 4 -> 5; matrix products, arithmetic and copies ran while one was open for 9% -> 11% of each run, Pallas kernels for 0% -> 0%
where the time goes in v2:
time: 380 us; the launch traced here: 374 us
  waiting for transfers between devices  294 us (77%)
  local copies, waits for them, and re-layouts  27.6 us (7%)
  matrix products  22.6 us (6%)
  starting transfers between devices  21.5 us (6%)
  other arithmetic  7.46 us (2%)
    all_to_all x1, waiting for transfers between devices, shards(): lax.all_to_all(partial_term.reshape(ff_dev, groups, feat_dev), DP, split_...  137 us
    ppermute x1, waiting for transfers between devices, shards(): partner = lax.ppermute(cotangent, 'zh', [(0, 1), (1, 0)])  129 us
    ppermute x3, waiting for transfers between devices, shards(): lax.ppermute(pair, 'y', [(i, (i + shift) % ring) for i in range(ring)])  23.4 us
    all_to_all x1, local copies, waits for them, and re-layouts, shards(): lax.all_to_all(slabs, DP, split_axis=0, concat_axis=2, tiled=True)  11.1 us
    dot_general x1, matrix products, shards(): lax.dot_general(out_rows, weights, (((1,), (1,)), ((), ())), preferred_el...  10.5 us
    all_to_all x1, starting transfers between devices, shards(): lax.all_to_all(slabs, DP, split_axis=0, concat_axis=2, tiled=True)  7.65 us
  transfers between devices with their start and end apart: 7, of which 5 were waited for; matrix products, arithmetic and copies ran while one was open for 11% of the time, Pallas kernels for 0%

profile of v2, /device:TPU:228, one launch (start us, length us, event | category | flops | bytes accessed | tf_op | source)
XLA Modules:
  0.0 373.7 jit_solution(2548591933414283584)
XLA Ops:
  0.6 0.8 pad_clamp_fusion
  2.2 4.0 %gather_fusion.1 = bf16[16,896,256]{2,1,0:T(8,128)(2,1)} fusion(bf16[4,896,256]{2,1,0:T(8,128)(2,1)S(1)} %copy-done, s32[1024]{0:T(1024)S(1)} %pad_clamp_fusion), kind=kCustom, calls=%fused_computation.1 | custom fusion | bytes 14680128 | tf_op jit(solution)/shard_map/jit(_take)/gather | solution.py:38
  6.2 7.7 %all-to-all-start = ((bf16[16,896,256]{2,1,0:T(8,128)(2,1)}), bf16[16,896,256]{2,1,0:T(8,128)(2,1)}, u32[]{:S(2)}, u32[]{:S(2)}) async-start(bf16[16,896,256]{2,1,0:T(8,128)(2,1)} %gather_fusion.1), calls=%async_computation | async-start | bytes 14680064 | tf_op jit(solution)/shard_map/all_to_all | solution.py:39
  13.8 1.5 collective-permute-start
  15.4 0.7 sort.17
  16.1 129.1 %collective-permute-done = bf16[32,4096]{1,0:T(8,128)(2,1)S(1)} collective-permute-done((bf16[32,4096]{1,0:T(8,128)(2,1)S(1)}, bf16[32,4096]{1,0:T(8,128)(2,1)S(1)}, u32[]{:S(2)}, u32[]{:S(2)}) %collective-permute-start) | collective-permute-done | bytes 262176 | tf_op jit(solution)/shard_map/ppermute | solution.py:18
  145.3 3.1 collective-permute-start.3
  149.0 1.0 collective-permute-start.1
  150.1 19.7 %collective-permute-done.3 = bf16[2,32,4096]{2,1,0:T(8,128)(2,1)S(1)} collective-permute-done((bf16[2,32,4096]{2,1,0:T(8,128)(2,1)S(1)}, bf16[2,32,4096]{2,1,0:T(8,128)(2,1)S(1)}, u32[]{:S(2)}, u32[]{:S(2)}) %collective-permute-start.3) | collective-permute-done | bytes 524320 | tf_op jit(solution)/shard_map/ppermute | solution.py:25
  169.7 3.7 collective-permute-done.1
  173.4 1.6 pad_maximum_fusion
  175.0 3.6 gather_fusion
  178.7 4.4 %collective-permute-done.4 = bf16[4,2,32,4096]{3,2,1,0:T(8,128)(2,1)} collective-permute-done((bf16[4,2,32,4096]{3,2,1,0:T(8,128)(2,1)}, bf16[4,2,32,4096]{3,2,1,0:T(8,128)(2,1)}, u32[]{:S(2)}, u32[]{:S(2)}) %collective-permute-start.4) | collective-permute-done | bytes 2097184 | tf_op jit(solution)/shard_map/ppermute | solution.py:29
  183.1 4.2 %fusion.2 = bf16[2,4,2,32,4096]{4,3,0,1,2:T(8,128)(2,1)S(1)} fusion(bf16[1,4,2,32,4096]{4,3,2,1,0:T(8,128)(2,1)} %bitcast.8, bf16[1,4,2,32,4096]{4,3,2,1,0:T(8,128)(2,1)} %bitcast.27, pred[]{:T(512)S(6)} %eq.21), kind=kLoop, calls=%fused_computation.7 | loop fusion | flops 6291456 | bytes 8388609 | tf_op jit(solution)/shard_map/transpose | solution.py:32
  187.6 0.9 copy-done.5
  188.4 0.9 copy-done.6
  189.3 4.5 %convolution_convert_fusion = bf16[896,4096]{1,0:T(8,128)(2,1)S(1)} fusion(bf16[512,4096]{1,0:T(8,128)(2,1)S(1)} %bitcast.30, bf16[512,896]{1,0:T(8,128)(2,1)S(1)} %copy-done.6, bf16[512,896]{1,0:T(8,128)(2,1)S(1)} %copy-done.5), kind=kOutput, calls=%fused_computation.5 | convolution fusion | flops 3765436416 | bytes 13369344 | tf_op jit(solution)/shard_map/dot_general | solution.py:49
  193.8 3.7 copy.22
  197.5 7.5 %all-to-all-start.1 = ((bf16[896,16,256]{2,0,1:T(8,128)(2,1)}), bf16[896,16,256]{2,0,1:T(8,128)(2,1)}, u32[]{:S(2)}, u32[]{:S(2)}) async-start(bf16[896,16,256]{2,0,1:T(8,128)(2,1)} %bitcast.26), calls=%async_computation.1 | async-start | bytes 14680064 | tf_op jit(solution)/shard_map/all_to_all | solution.py:52
  205.0 11.1 %copy.14 = bf16[1,896,16,256]{1,3,2,0:T(8,128)(2,1)} copy(bf16[1,896,16,256]{3,1,2,0:T(8,128)(2,1)} %bitcast.12) | data formatting | bytes 14680064 | tf_op jit(solution)/shard_map/all_to_all | solution.py:39
  216.2 10.5 %multiply_convert_fusion = (bf16[512,896]{1,0:T(8,128)(2,1)}, bf16[512,896]{1,0:T(8,128)(2,1)}) fusion(bf16[512,896]{1,0:T(8,128)(2,1)S(1)} %copy-done.5, bf16[512,896]{1,0:T(8,128)(2,1)S(1)} %copy-done.6, bf16[512,4096]{1,0:T(8,128)(2,1)} %bitcast.31, bf16[896,4096]{0,1:T(8,128)(2,1)} %bitcast.28), kind=kOutput, calls=%fused_computation.22 | convolution fusion | flops 3764977664 | bytes 15204352 | tf_op jit(solution)/shard_map/dot_general | solution.py:41
  226.7 137.0 %all-to-all-done.1 = bf16[896,16,256]{2,0,1:T(8,128)(2,1)} async-done(((bf16[896,16,256]{2,0,1:T(8,128)(2,1)}), bf16[896,16,256]{2,0,1:T(8,128)(2,1)}, u32[]{:S(2)}, u32[]{:S(2)}) %all-to-all-start.1) | async-done | bytes 7340064 | tf_op jit(solution)/shard_map/all_to_all | solution.py:52
  363.7 7.5 %fusion = f32[4,896,256]{2,0,1:T(4,128)S(1)} fusion(bf16[896,16,256]{2,0,1:T(8,128)(2,1)} %all-to-all-done.1, s32[16]{0:T(128)S(1)} %copy-done.4), kind=kOutput, calls=%fused_computation.3 | convolution fusion | flops 29360192 | bytes 11010112 | tf_op jit(solution)/shard_map/lg,fgd->lfd/dot_general | solution.py:59
  371.2 2.5 copy.17
  (22 shorter events, 1.9 us)
Async XLA Ops:
  0.6 1.5 copy-start
  6.2 7.7 %copy-start.3 = (bf16[32,4096]{1,0:T(8,128)(2,1)S(1)}, bf16[32,4096]{1,0:T(8,128)(2,1)}, u32[]{:S(2)}) copy-start(bf16[32,4096]{1,0:T(8,128)(2,1)} %param.5) | copy-start | bytes 786436
  6.2 191.3 %all-to-all-start = ((bf16[16,896,256]{2,1,0:T(8,128)(2,1)}), bf16[16,896,256]{2,1,0:T(8,128)(2,1)}, u32[]{:S(2)}, u32[]{:S(2)}) async-start(bf16[16,896,256]{2,1,0:T(8,128)(2,1)} %gather_fusion.1), calls=%async_computation | async-start | bytes 14680064 | tf_op jit(solution)/shard_map/all_to_all | solution.py:39
  13.8 131.3 %collective-permute-start = (bf16[32,4096]{1,0:T(8,128)(2,1)S(1)}, bf16[32,4096]{1,0:T(8,128)(2,1)S(1)}, u32[]{:S(2)}, u32[]{:S(2)}) collective-permute-start(bf16[32,4096]{1,0:T(8,128)(2,1)S(1)} %copy-done.3), channel_id=1, source_target_pairs={{0,8},{8,0},{1,9},{9,1},{2,10},{10,2},{3,11},{11,3},{4,12},{12,4},... | collective-permute-start | bytes 786440 | tf_op jit(solution)/shard_map/ppermute | solution.py:18
  145.3 24.4 %collective-permute-start.3 = (bf16[2,32,4096]{2,1,0:T(8,128)(2,1)S(1)}, bf16[2,32,4096]{2,1,0:T(8,128)(2,1)S(1)}, u32[]{:S(2)}, u32[]{:S(2)}) collective-permute-start(bf16[2,32,4096]{2,1,0:T(8,128)(2,1)S(1)} %maximum_select_fusion.2), channel_id=1, source_target_pairs={{0,6},{2,0},{4,2},{6,4},{1,7},{3,1},{5,3},{7,5},{8,14},{10,8},{12,... | collective-permute-start | bytes 1572872 | tf_op jit(solution)/shard_map/ppermute | solution.py:25
  148.4 21.4 %collective-permute-start.2 = (bf16[2,32,4096]{2,1,0:T(8,128)(2,1)S(1)}, bf16[2,32,4096]{2,1,0:T(8,128)(2,1)S(1)}, u32[]{:S(2)}, u32[]{:S(2)}) collective-permute-start(bf16[2,32,4096]{2,1,0:T(8,128)(2,1)S(1)} %maximum_select_fusion.2), channel_id=1, source_target_pairs={{0,4},{2,6},{4,0},{6,2},{1,5},{3,7},{5,1},{7,3},{8,12},{10,14},{12... | collective-permute-start | bytes 1572872 | tf_op jit(solution)/shard_map/ppermute | solution.py:25
  149.0 24.4 %collective-permute-start.1 = (bf16[2,32,4096]{2,1,0:T(8,128)(2,1)S(1)}, bf16[2,32,4096]{2,1,0:T(8,128)(2,1)S(1)}, u32[]{:S(2)}, u32[]{:S(2)}) collective-permute-start(bf16[2,32,4096]{2,1,0:T(8,128)(2,1)S(1)} %maximum_select_fusion.2), channel_id=1, source_target_pairs={{0,2},{2,4},{4,6},{6,0},{1,3},{3,5},{5,7},{7,1},{8,10},{10,12},{12... | collective-permute-start | bytes 1572872 | tf_op jit(solution)/shard_map/ppermute | solution.py:25
  178.6 4.5 %collective-permute-start.4 = (bf16[4,2,32,4096]{3,2,1,0:T(8,128)(2,1)}, bf16[4,2,32,4096]{3,2,1,0:T(8,128)(2,1)}, u32[]{:S(2)}, u32[]{:S(2)}) collective-permute-start(bf16[4,2,32,4096]{3,2,1,0:T(8,128)(2,1)} %gather_fusion), channel_id=1, source_target_pairs={{0,1},{1,0},{2,3},{3,2},{4,5},{5,4},{6,7},{7,6},{8,9},{9,8},{10,11... | collective-permute-start | bytes 6291464 | tf_op jit(solution)/shard_map/ppermute | solution.py:29
  187.3 1.2 copy-start.5
  187.3 2.0 copy-start.6
  187.6 6.3 %copy-start.2 = (bf16[2,4,2,32,4096]{4,3,2,1,0:T(8,128)(2,1)}, bf16[2,4,2,32,4096]{4,3,2,1,0:T(8,128)(2,1)S(1)}, u32[]{:S(2)}) copy-start(bf16[2,4,2,32,4096]{4,3,2,1,0:T(8,128)(2,1)S(1)} %copy.13) | copy-start | bytes 12582916
  197.5 166.2 %all-to-all-start.1 = ((bf16[896,16,256]{2,0,1:T(8,128)(2,1)}), bf16[896,16,256]{2,0,1:T(8,128)(2,1)}, u32[]{:S(2)}, u32[]{:S(2)}) async-start(bf16[896,16,256]{2,0,1:T(8,128)(2,1)} %bitcast.26), calls=%async_computation.1 | async-start | bytes 14680064 | tf_op jit(solution)/shard_map/all_to_all | solution.py:52
  216.2 147.6 %copy-start.4 = (s32[16]{0:T(128)S(1)}, s32[16]{0:T(128)}, u32[]{:S(2)}) copy-start(s32[16]{0:T(128)} %param.9) | copy-start | bytes 196
  363.7 10.0 %copy-start.1 = (bf16[4,896,256]{2,1,0:T(8,128)(2,1)S(1)}, bf16[4,896,256]{2,1,0:T(8,128)(2,1)}, u32[]{:S(2)}) copy-start(bf16[4,896,256]{2,1,0:T(8,128)(2,1)} %param.8) | copy-start | bytes 5505028

commit v3 on v2

--- a/solution.py
+++ b/solution.py
@@ -16,6 +16,8 @@
     rows_dev, feats = cotangent.shape
     cores = lax.axis_size("c")
     partner = lax.ppermute(cotangent, "zh", [(0, 1), (1, 0)])
+    slabs = jnp.take(w_down, language, axis=0, mode="clip")
+    partner, slabs = lax.optimization_barrier((partner, slabs))
     first = lax.axis_index("zh") == 0
     pair = jnp.where(first, jnp.stack([cotangent, partner]), jnp.stack([partner, cotangent]))
     ring = lax.axis_size("y")
@@ -35,7 +37,6 @@
     sig = jax.nn.sigmoid(gate_f)
     act = gate_f * sig
     hidden = (act * up_f).astype(jnp.bfloat16)
-    slabs = jnp.take(w_down, language, axis=0, mode="clip")
     received = lax.all_to_all(slabs, DP, split_axis=0, concat_axis=2, tiled=True)
     weights = received[0]
     d_hidden = lax.dot_general(

time: 380 us -> 361 us (0.950)
  waiting for transfers between devices: 294 us -> 277 us
    ppermute x1, waiting for transfers between devices: 129 us -> 9.08 us  [shards(): partner = lax.ppermute(cotangent, 'zh', [(0, 1), (1, 0)])]
    all_to_all x1, waiting for transfers between devices: 0.01 us -> 105 us  [shards(): lax.all_to_all(slabs, DP, split_axis=0, concat_axis=2, tiled=True)]
  transfers between devices with their start and end apart: 7 -> 7, of which waited for: 5 -> 6; matrix products, arithmetic and copies ran while one was open for 11% -> 13% of each run, Pallas kernels for 0% -> 0%
where the time goes in v3:
time: 361 us; the launch traced here: 358 us
  waiting for transfers between devices  277 us (77%)
  local copies, waits for them, and re-layouts  26.9 us (7%)
  starting transfers between devices  23.3 us (6%)
  matrix products  22.6 us (6%)
  other arithmetic  7.32 us (2%)
    all_to_all x1, waiting for transfers between devices, shards(): lax.all_to_all(partial_term.reshape(ff_dev, groups, feat_dev), DP, split_...  136 us
    all_to_all x1, waiting for transfers between devices, shards(): lax.all_to_all(slabs, DP, split_axis=0, concat_axis=2, tiled=True)  105 us
    ppermute x3, waiting for transfers between devices, shards(): lax.ppermute(pair, 'y', [(i, (i + shift) % ring) for i in range(ring)])  23.2 us
    all_to_all x1, local copies, waits for them, and re-layouts, shards(): lax.all_to_all(slabs, DP, split_axis=0, concat_axis=2, tiled=True)  11.1 us
    dot_general x1, matrix products, shards(): lax.dot_general(out_rows, weights, (((1,), (1,)), ((), ())), preferred_el...  10.6 us
    all_to_all x1, starting transfers between devices, shards(): lax.all_to_all(slabs, DP, split_axis=0, concat_axis=2, tiled=True)  9.56 us
    ppermute x1, waiting for transfers between devices, shards(): partner = lax.ppermute(cotangent, 'zh', [(0, 1), (1, 0)])  9.08 us
    dot_general x1, matrix products, shards(): jnp.einsum('lg,fgd->lfd', selector, pieces, preferred_element_type=jnp.fl...  7.53 us
  transfers between devices with their start and end apart: 7, of which 6 were waited for; matrix products, arithmetic and copies ran while one was open for 13% of the time, Pallas kernels for 0%

profile of v3, /device:TPU:228, one launch (start us, length us, event | category | flops | bytes accessed | tf_op | source)
XLA Modules:
  0.0 358.2 jit_solution(10707687449354510474)
XLA Ops:
  0.6 1.5 collective-permute-start
  2.8 4.0 %gather_fusion = bf16[16,896,256]{2,1,0:T(8,128)(2,1)} fusion(bf16[4,896,256]{2,1,0:T(8,128)(2,1)S(1)} %copy-done, s32[1024]{0:T(1024)S(1)} %pad_clamp_fusion.1), kind=kCustom, calls=%fused_computation | custom fusion | bytes 14680128 | tf_op jit(solution)/shard_map/jit(_take)/gather | solution.py:19
  6.9 9.1 %collective-permute-done = bf16[32,4096]{1,0:T(8,128)(2,1)S(1)} collective-permute-done((bf16[32,4096]{1,0:T(8,128)(2,1)}, bf16[32,4096]{1,0:T(8,128)(2,1)S(1)}, u32[]{:S(2)}, u32[]{:S(2)}) %collective-permute-start) | collective-permute-done | bytes 262176 | tf_op jit(solution)/shard_map/ppermute | solution.py:18
  15.9 9.6 %all-to-all-start = ((bf16[16,896,256]{2,1,0:T(8,128)(2,1)}), bf16[16,896,256]{2,1,0:T(8,128)(2,1)}, u32[]{:S(2)}, u32[]{:S(2)}) async-start(bf16[16,896,256]{2,1,0:T(8,128)(2,1)} %gather_fusion), calls=%async_computation | async-start | bytes 14680064 | tf_op jit(solution)/shard_map/all_to_all | solution.py:40
  25.5 0.7 sort.17
  26.4 3.1 collective-permute-start.3
  30.1 1.0 collective-permute-start.1
  31.1 19.4 %collective-permute-done.3 = bf16[2,32,4096]{2,1,0:T(8,128)(2,1)S(1)} collective-permute-done((bf16[2,32,4096]{2,1,0:T(8,128)(2,1)S(1)}, bf16[2,32,4096]{2,1,0:T(8,128)(2,1)S(1)}, u32[]{:S(2)}, u32[]{:S(2)}) %collective-permute-start.3) | collective-permute-done | bytes 524320 | tf_op jit(solution)/shard_map/ppermute | solution.py:27
  50.6 3.7 %collective-permute-done.1 = bf16[2,32,4096]{2,1,0:T(8,128)(2,1)S(1)} collective-permute-done((bf16[2,32,4096]{2,1,0:T(8,128)(2,1)S(1)}, bf16[2,32,4096]{2,1,0:T(8,128)(2,1)S(1)}, u32[]{:S(2)}, u32[]{:S(2)}) %collective-permute-start.1) | collective-permute-done | bytes 524320 | tf_op jit(solution)/shard_map/ppermute | solution.py:27
  54.3 1.6 pad_maximum_fusion
  55.9 3.6 gather_fusion.1
  59.5 4.5 %collective-permute-done.4 = bf16[4,2,32,4096]{3,2,1,0:T(8,128)(2,1)} collective-permute-done((bf16[4,2,32,4096]{3,2,1,0:T(8,128)(2,1)}, bf16[4,2,32,4096]{3,2,1,0:T(8,128)(2,1)}, u32[]{:S(2)}, u32[]{:S(2)}) %collective-permute-start.4) | collective-permute-done | bytes 2097184 | tf_op jit(solution)/shard_map/ppermute | solution.py:31
  63.9 4.2 %fusion.2 = bf16[2,4,2,32,4096]{4,3,0,1,2:T(8,128)(2,1)S(1)} fusion(bf16[1,4,2,32,4096]{4,3,2,1,0:T(8,128)(2,1)} %bitcast.8, bf16[1,4,2,32,4096]{4,3,2,1,0:T(8,128)(2,1)} %bitcast.27, pred[]{:T(512)S(6)} %eq.21), kind=kLoop, calls=%fused_computation.7 | loop fusion | flops 6291456 | bytes 8388609 | tf_op jit(solution)/shard_map/transpose | solution.py:34
  68.4 0.9 copy-done.5
  69.3 0.9 copy-done.6
  70.2 4.5 %convolution_convert_fusion = bf16[896,4096]{1,0:T(8,128)(2,1)S(1)} fusion(bf16[512,4096]{1,0:T(8,128)(2,1)S(1)} %bitcast.30, bf16[512,896]{1,0:T(8,128)(2,1)S(1)} %copy-done.6, bf16[512,896]{1,0:T(8,128)(2,1)S(1)} %copy-done.5), kind=kOutput, calls=%fused_computation.5 | convolution fusion | flops 3765436416 | bytes 13369344 | tf_op jit(solution)/shard_map/dot_general | solution.py:50
  74.7 3.7 %copy.22 = bf16[112,16,8,256]{3,2,0,1:T(8,128)(2,1)} copy(bf16[112,16,8,256]{3,2,1,0:T(8,128)(2,1)S(1)} %bitcast.29) | data formatting | bytes 14680064 | tf_op jit(solution)/shard_map/reshape | solution.py:54
  78.4 104.8 %all-to-all-done = bf16[16,896,256]{2,1,0:T(8,128)(2,1)} async-done(((bf16[16,896,256]{2,1,0:T(8,128)(2,1)}), bf16[16,896,256]{2,1,0:T(8,128)(2,1)}, u32[]{:S(2)}, u32[]{:S(2)}) %all-to-all-start) | async-done | bytes 7340064 | tf_op jit(solution)/shard_map/all_to_all | solution.py:40
  183.2 7.5 %all-to-all-start.1 = ((bf16[896,16,256]{2,0,1:T(8,128)(2,1)}), bf16[896,16,256]{2,0,1:T(8,128)(2,1)}, u32[]{:S(2)}, u32[]{:S(2)}) async-start(bf16[896,16,256]{2,0,1:T(8,128)(2,1)} %bitcast.26), calls=%async_computation.1 | async-start | bytes 14680064 | tf_op jit(solution)/shard_map/all_to_all | solution.py:53
  190.7 11.1 %copy.14 = bf16[1,896,16,256]{1,3,2,0:T(8,128)(2,1)} copy(bf16[1,896,16,256]{3,1,2,0:T(8,128)(2,1)} %bitcast.12) | data formatting | bytes 14680064 | tf_op jit(solution)/shard_map/all_to_all | solution.py:40
  201.8 10.6 %multiply_convert_fusion = (bf16[512,896]{1,0:T(8,128)(2,1)}, bf16[512,896]{1,0:T(8,128)(2,1)}) fusion(bf16[512,896]{1,0:T(8,128)(2,1)S(1)} %copy-done.5, bf16[512,896]{1,0:T(8,128)(2,1)S(1)} %copy-done.6, bf16[512,4096]{1,0:T(8,128)(2,1)} %bitcast.31, bf16[896,4096]{0,1:T(8,128)(2,1)} %bitcast.28), kind=kOutput, calls=%fused_computation.22 | convolution fusion | flops 3764977664 | bytes 15204352 | tf_op jit(solution)/shard_map/dot_general | solution.py:42
  212.4 135.8 %all-to-all-done.1 = bf16[896,16,256]{2,0,1:T(8,128)(2,1)} async-done(((bf16[896,16,256]{2,0,1:T(8,128)(2,1)}), bf16[896,16,256]{2,0,1:T(8,128)(2,1)}, u32[]{:S(2)}, u32[]{:S(2)}) %all-to-all-start.1) | async-done | bytes 7340064 | tf_op jit(solution)/shard_map/all_to_all | solution.py:53
  348.2 7.5 %fusion = f32[4,896,256]{2,0,1:T(4,128)S(1)} fusion(bf16[896,16,256]{2,0,1:T(8,128)(2,1)} %all-to-all-done.1, s32[16]{0:T(128)S(1)} %copy-done.4), kind=kOutput, calls=%fused_computation.3 | convolution fusion | flops 29360192 | bytes 11010112 | tf_op jit(solution)/shard_map/lg,fgd->lfd/dot_general | solution.py:60
  355.7 2.5 copy.17
  (22 shorter events, 1.8 us)
Async XLA Ops:
  0.6 2.2 copy-start
  0.6 15.3 %collective-permute-start = (bf16[32,4096]{1,0:T(8,128)(2,1)}, bf16[32,4096]{1,0:T(8,128)(2,1)S(1)}, u32[]{:S(2)}, u32[]{:S(2)}) collective-permute-start(bf16[32,4096]{1,0:T(8,128)(2,1)} %param.5), channel_id=1, source_target_pairs={{0,8},{8,0},{1,9},{9,1},{2,10},{10,2},{3,11},{11,3},{4,12},{12,4},... | collective-permute-start | bytes 786440 | tf_op jit(solution)/shard_map/ppermute | solution.py:18
  6.9 19.4 %copy-start.3 = (bf16[32,4096]{1,0:T(8,128)(2,1)S(1)}, bf16[32,4096]{1,0:T(8,128)(2,1)}, u32[]{:S(2)}) copy-start(bf16[32,4096]{1,0:T(8,128)(2,1)} %param.5) | copy-start | bytes 786436
  15.9 167.2 %all-to-all-start = ((bf16[16,896,256]{2,1,0:T(8,128)(2,1)}), bf16[16,896,256]{2,1,0:T(8,128)(2,1)}, u32[]{:S(2)}, u32[]{:S(2)}) async-start(bf16[16,896,256]{2,1,0:T(8,128)(2,1)} %gather_fusion), calls=%async_computation | async-start | bytes 14680064 | tf_op jit(solution)/shard_map/all_to_all | solution.py:40
  26.4 24.2 %collective-permute-start.3 = (bf16[2,32,4096]{2,1,0:T(8,128)(2,1)S(1)}, bf16[2,32,4096]{2,1,0:T(8,128)(2,1)S(1)}, u32[]{:S(2)}, u32[]{:S(2)}) collective-permute-start(bf16[2,32,4096]{2,1,0:T(8,128)(2,1)S(1)} %maximum_select_fusion.2), channel_id=1, source_target_pairs={{0,6},{2,0},{4,2},{6,4},{1,7},{3,1},{5,3},{7,5},{8,14},{10,8},{12,... | collective-permute-start | bytes 1572872 | tf_op jit(solution)/shard_map/ppermute | solution.py:27
  29.5 21.1 %collective-permute-start.2 = (bf16[2,32,4096]{2,1,0:T(8,128)(2,1)S(1)}, bf16[2,32,4096]{2,1,0:T(8,128)(2,1)S(1)}, u32[]{:S(2)}, u32[]{:S(2)}) collective-permute-start(bf16[2,32,4096]{2,1,0:T(8,128)(2,1)S(1)} %maximum_select_fusion.2), channel_id=1, source_target_pairs={{0,4},{2,6},{4,0},{6,2},{1,5},{3,7},{5,1},{7,3},{8,12},{10,14},{12... | collective-permute-start | bytes 1572872 | tf_op jit(solution)/shard_map/ppermute | solution.py:27
  30.1 24.2 %collective-permute-start.1 = (bf16[2,32,4096]{2,1,0:T(8,128)(2,1)S(1)}, bf16[2,32,4096]{2,1,0:T(8,128)(2,1)S(1)}, u32[]{:S(2)}, u32[]{:S(2)}) collective-permute-start(bf16[2,32,4096]{2,1,0:T(8,128)(2,1)S(1)} %maximum_select_fusion.2), channel_id=1, source_target_pairs={{0,2},{2,4},{4,6},{6,0},{1,3},{3,5},{5,7},{7,1},{8,10},{10,12},{12... | collective-permute-start | bytes 1572872 | tf_op jit(solution)/shard_map/ppermute | solution.py:27
  59.4 4.5 %collective-permute-start.4 = (bf16[4,2,32,4096]{3,2,1,0:T(8,128)(2,1)}, bf16[4,2,32,4096]{3,2,1,0:T(8,128)(2,1)}, u32[]{:S(2)}, u32[]{:S(2)}) collective-permute-start(bf16[4,2,32,4096]{3,2,1,0:T(8,128)(2,1)} %gather_fusion.1), channel_id=1, source_target_pairs={{0,1},{1,0},{2,3},{3,2},{4,5},{5,4},{6,7},{7,6},{8,9},{9,8},{10,11... | collective-permute-start | bytes 6291464 | tf_op jit(solution)/shard_map/ppermute | solution.py:31
  68.1 1.2 copy-start.5
  68.1 2.0 copy-start.6
  68.4 6.3 %copy-start.2 = (bf16[2,4,2,32,4096]{4,3,2,1,0:T(8,128)(2,1)}, bf16[2,4,2,32,4096]{4,3,2,1,0:T(8,128)(2,1)S(1)}, u32[]{:S(2)}) copy-start(bf16[2,4,2,32,4096]{4,3,2,1,0:T(8,128)(2,1)S(1)} %copy.13) | copy-start | bytes 12582916
  183.2 165.1 %all-to-all-start.1 = ((bf16[896,16,256]{2,0,1:T(8,128)(2,1)}), bf16[896,16,256]{2,0,1:T(8,128)(2,1)}, u32[]{:S(2)}, u32[]{:S(2)}) async-start(bf16[896,16,256]{2,0,1:T(8,128)(2,1)} %bitcast.26), calls=%async_computation.1 | async-start | bytes 14680064 | tf_op jit(solution)/shard_map/all_to_all | solution.py:53
  201.8 146.4 %copy-start.4 = (s32[16]{0:T(128)S(1)}, s32[16]{0:T(128)}, u32[]{:S(2)}) copy-start(s32[16]{0:T(128)} %param.9) | copy-start | bytes 196
  348.2 10.0 %copy-start.1 = (bf16[4,896,256]{2,1,0:T(8,128)(2,1)S(1)}, bf16[4,896,256]{2,1,0:T(8,128)(2,1)}, u32[]{:S(2)}) copy-start(bf16[4,896,256]{2,1,0:T(8,128)(2,1)} %param.8) | copy-start | bytes 5505028

commit v4 on v2

--- a/solution.py
+++ b/solution.py
@@ -4,7 +4,8 @@
 from jax.sharding import Mesh
 from jax.sharding import PartitionSpec as P
 
-DP = ("zl", "x")
+DP = ("zh2", "zl2", "x")
+HALF = ("zl2", "x")
 TP = ("zh", "y", "c")
 
 
@@ -16,6 +17,16 @@
     rows_dev, feats = cotangent.shape
     cores = lax.axis_size("c")
     partner = lax.ppermute(cotangent, "zh", [(0, 1), (1, 0)])
+    half = lax.axis_size(HALF)
+    side = lax.axis_index("zh2")
+    lang = language.reshape(2, half)
+    own_langs = jnp.take(lang, side, axis=0, mode="clip")
+    own_slabs = jnp.take(w_down, own_langs, axis=0, mode="clip")
+    partner, own_slabs = lax.optimization_barrier((partner, own_slabs))
+    near = lax.all_to_all(own_slabs, HALF, split_axis=0, concat_axis=0, tiled=True)
+    block = lax.ppermute(w_down, "zh2", [(0, 1), (1, 0)])
+    relay = jnp.take(block, own_langs, axis=0, mode="clip")
+    far = lax.all_to_all(relay, HALF, split_axis=0, concat_axis=0, tiled=True)
     first = lax.axis_index("zh") == 0
     pair = jnp.where(first, jnp.stack([cotangent, partner]), jnp.stack([partner, cotangent]))
     ring = lax.axis_size("y")
@@ -35,12 +46,12 @@
     sig = jax.nn.sigmoid(gate_f)
     act = gate_f * sig
     hidden = (act * up_f).astype(jnp.bfloat16)
-    slabs = jnp.take(w_down, language, axis=0, mode="clip")
-    received = lax.all_to_all(slabs, DP, split_axis=0, concat_axis=2, tiled=True)
-    weights = received[0]
-    d_hidden = lax.dot_general(
-        out_rows, weights, (((1,), (1,)), ((), ())), preferred_element_type=jnp.float32
-    )
+    rows3 = out_rows.reshape(out_rows.shape[0], 2, half, feat_dev)
+    cot_near = jnp.take(rows3, side, axis=1, mode="clip")
+    cot_far = jnp.take(rows3, 1 - side, axis=1, mode="clip")
+    d_hidden = jnp.einsum(
+        "tsd,sfd->tf", cot_near, near, preferred_element_type=jnp.float32
+    ) + jnp.einsum("tsd,sfd->tf", cot_far, far, preferred_element_type=jnp.float32)
     d_up = (d_hidden * act).astype(jnp.bfloat16)
     d_gate = (d_hidden * up_f * sig * (1.0 + gate_f * (1.0 - sig))).astype(jnp.bfloat16)
     selector = (language[None, :] == jnp.arange(variants, dtype=jnp.int32)[:, None]).astype(
@@ -61,7 +72,7 @@
 
 
 def solution(mesh):
-    sub = Mesh(mesh.devices.reshape(4, 4, 2, 4, 2), DP + TP)
+    sub = Mesh(mesh.devices.reshape(2, 2, 4, 2, 4, 2), DP + TP)
     return jax.shard_map(
         shards,
         mesh=sub,

time: 380 us -> 340 us (0.89)
  waiting for transfers between devices: 294 us -> 257 us
  starting transfers between devices: 21.5 us -> 29.3 us
  local copies, waits for them, and re-layouts: 27.6 us -> 23.1 us
    ppermute x1, waiting for transfers between devices: 129 us -> 8.94 us  [shards(): partner = lax.ppermute(cotangent, 'zh', [(0, 1), (1, 0)])]
    ppermute x0 -> x1, waiting for transfers between devices: none -> 79.3 us  [shards(): block = lax.ppermute(w_down, 'zh2', [(0, 1), (1, 0)])]
    all_to_all x1 -> x0, local copies, waits for them, and re-layouts: 11.1 us -> none  [shards(): lax.all_to_all(slabs, DP, split_axis=0, concat_axis=2, tiled=True)]
    all_to_all x1, waiting for transfers between devices: 137 us -> 144 us  [shards(): lax.all_to_all(partial_term.reshape(ff_dev, groups, feat_dev), DP, split_...]
    all_to_all x1 -> x2, starting transfers between devices: 7.65 us -> 13.7 us  [the longest x1 7.86 us: shards(): lax.all_to_all(own_slabs, HALF, split_axis=0, concat_axis=0, tiled=True)]
    gather x1 -> x2, local copies, waits for them, and re-layouts: 4.03 us -> 8.19 us  [the longest x1 4.12 us: shards(): relay = jnp.take(block, own_langs, axis=0, mode='clip')]
    unnamed x15 -> x14, local copies, waits for them, and re-layouts: 4.98 us -> 7.86 us
    dot_general x1 -> x2, matrix products: 10.5 us -> 10.7 us  [the longest x1 6.3 us: shards(): jnp.einsum('tsd,sfd->tf', cot_far, far, preferred_element_type=jnp.float32)]
  transfers between devices with their start and end apart: 7 -> 9, of which waited for: 5 -> 6; matrix products, arithmetic and copies ran while one was open for 11% -> 11% of each run, Pallas kernels for 0% -> 0%
where the time goes in v4:
time: 340 us; the launch traced here: 337 us
  waiting for transfers between devices  257 us (76%)
  starting transfers between devices  29.3 us (9%)
  local copies, waits for them, and re-layouts  23.1 us (7%)
  matrix products  22.6 us (7%)
  other arithmetic  4.01 us (1%)
    all_to_all x1, waiting for transfers between devices, shards(): lax.all_to_all(partial_term.reshape(ff_dev, groups, feat_dev), DP, split_...  144 us
    ppermute x1, waiting for transfers between devices, shards(): block = lax.ppermute(w_down, 'zh2', [(0, 1), (1, 0)])  79.3 us
    ppermute x3, waiting for transfers between devices, shards(): lax.ppermute(pair, 'y', [(i, (i + shift) % ring) for i in range(ring)])  20.5 us
    ppermute x1, waiting for transfers between devices, shards(): partner = lax.ppermute(cotangent, 'zh', [(0, 1), (1, 0)])  8.94 us
    all_to_all x1, starting transfers between devices, shards(): lax.all_to_all(own_slabs, HALF, split_axis=0, concat_axis=0, tiled=True)  7.86 us
    unnamed x14, local copies, waits for them, and re-layouts  7.86 us
    all_to_all x1, starting transfers between devices, shards(): lax.all_to_all(partial_term.reshape(ff_dev, groups, feat_dev), DP, split_...  7.53 us
    dot_general x1, matrix products, shards(): jnp.einsum('lg,fgd->lfd', selector, pieces, preferred_element_type=jnp.fl...  7.39 us
  transfers between devices with their start and end apart: 9, of which 6 were waited for; matrix products, arithmetic and copies ran while one was open for 11% of the time, Pallas kernels for 0%

profile of v4, /device:TPU:228, one launch (start us, length us, event | category | flops | bytes accessed | tf_op | source)
XLA Modules:
  0.0 336.9 jit_solution(18185441324595208929)
XLA Ops:
  0.6 1.5 collective-permute-start
  2.9 4.1 %gather_fusion = bf16[8,896,256]{2,1,0:T(8,128)(2,1)} fusion(bf16[4,896,256]{2,1,0:T(8,128)(2,1)} %param.8, s32[1024]{0:T(1024)S(1)} %pad_clamp_fusion.1), kind=kCustom, calls=%fused_computation | custom fusion | bytes 7340064 | tf_op jit(solution)/shard_map/jit(_take)/gather | solution.py:24
  7.0 8.9 %collective-permute-done = bf16[32,4096]{1,0:T(8,128)(2,1)S(1)} collective-permute-done((bf16[32,4096]{1,0:T(8,128)(2,1)}, bf16[32,4096]{1,0:T(8,128)(2,1)S(1)}, u32[]{:S(2)}, u32[]{:S(2)}) %collective-permute-start) | collective-permute-done | bytes 262176 | tf_op jit(solution)/shard_map/ppermute | solution.py:19
  15.9 7.9 %all-to-all-start = ((bf16[8,896,256]{2,1,0:T(8,128)(2,1)}), bf16[8,896,256]{2,1,0:T(8,128)(2,1)}, u32[]{:S(2)}, u32[]{:S(2)}) async-start(bf16[8,896,256]{2,1,0:T(8,128)(2,1)} %gather_fusion), calls=%async_computation | async-start | bytes 7340032 | tf_op jit(solution)/shard_map/all_to_all | solution.py:26
  23.8 1.9 collective-permute-start.5
  25.7 79.3 %collective-permute-done.5 = bf16[4,896,256]{2,1,0:T(8,128)(2,1)} collective-permute-done((bf16[4,896,256]{2,1,0:T(8,128)(2,1)S(1)}, bf16[4,896,256]{2,1,0:T(8,128)(2,1)}, u32[]{:S(2)}, u32[]{:S(2)}) %collective-permute-start.5) | collective-permute-done | bytes 1835040 | tf_op jit(solution)/shard_map/ppermute | solution.py:27
  104.9 4.1 %gather_fusion.2 = bf16[8,896,256]{2,1,0:T(8,128)(2,1)} fusion(bf16[4,896,256]{2,1,0:T(8,128)(2,1)} %collective-permute-done.5, s32[1024]{0:T(1024)S(1)} %pad_clamp_fusion.1), kind=kCustom, calls=%fused_computation.2 | custom fusion | bytes 7340064 | tf_op jit(solution)/shard_map/jit(_take)/gather | solution.py:28
  109.0 5.8 %all-to-all-start.1 = ((bf16[8,896,256]{2,1,0:T(8,128)(2,1)}), bf16[8,896,256]{2,1,0:T(8,128)(2,1)}, u32[]{:S(2)}, u32[]{:S(2)}) async-start(bf16[8,896,256]{2,1,0:T(8,128)(2,1)} %gather_fusion.2), calls=%async_computation.1 | async-start | bytes 7340032 | tf_op jit(solution)/shard_map/all_to_all | solution.py:29
  115.7 3.1 collective-permute-start.3
  119.4 1.0 collective-permute-start.1
  120.5 16.8 %collective-permute-done.3 = bf16[2,32,4096]{2,1,0:T(8,128)(2,1)S(1)} collective-permute-done((bf16[2,32,4096]{2,1,0:T(8,128)(2,1)S(1)}, bf16[2,32,4096]{2,1,0:T(8,128)(2,1)S(1)}, u32[]{:S(2)}, u32[]{:S(2)}) %collective-permute-start.3) | collective-permute-done | bytes 524320 | tf_op jit(solution)/shard_map/ppermute | solution.py:36
  137.3 3.7 %collective-permute-done.1 = bf16[2,32,4096]{2,1,0:T(8,128)(2,1)S(1)} collective-permute-done((bf16[2,32,4096]{2,1,0:T(8,128)(2,1)S(1)}, bf16[2,32,4096]{2,1,0:T(8,128)(2,1)S(1)}, u32[]{:S(2)}, u32[]{:S(2)}) %collective-permute-start.1) | collective-permute-done | bytes 524320 | tf_op jit(solution)/shard_map/ppermute | solution.py:36
  141.3 2.0 gather_fusion.1
  143.3 4.4 %collective-permute-done.4 = bf16[4,2,32,4096]{3,2,1,0:T(8,128)(2,1)S(1)} collective-permute-done((bf16[4,2,32,4096]{3,2,1,0:T(8,128)(2,1)}, bf16[4,2,32,4096]{3,2,1,0:T(8,128)(2,1)S(1)}, u32[]{:S(2)}, u32[]{:S(2)}) %collective-permute-start.4) | collective-permute-done | bytes 2097184 | tf_op jit(solution)/shard_map/ppermute | solution.py:40
  147.6 2.8 fusion.2
  152.5 4.5 %convolution_convert_fusion = bf16[896,4096]{1,0:T(8,128)(2,1)S(1)} fusion(bf16[512,4096]{1,0:T(8,128)(2,1)S(1)} %bitcast.44, bf16[512,896]{1,0:T(8,128)(2,1)S(1)} %copy-done.5, bf16[512,896]{1,0:T(8,128)(2,1)S(1)} %copy-done.4), kind=kOutput, calls=%fused_computation.6 | convolution fusion | flops 3765436416 | bytes 13369344 | tf_op jit(solution)/shard_map/dot_general | solution.py:60
  157.1 3.7 %copy.41 = bf16[112,16,8,256]{3,2,0,1:T(8,128)(2,1)} copy(bf16[112,16,8,256]{3,2,1,0:T(8,128)(2,1)S(1)} %bitcast.48) | data formatting | bytes 14680064 | tf_op jit(solution)/shard_map/reshape | solution.py:64
  160.8 7.5 %all-to-all-start.2 = ((bf16[896,16,256]{2,0,1:T(8,128)(2,1)}), bf16[896,16,256]{2,0,1:T(8,128)(2,1)}, u32[]{:S(2)}, u32[]{:S(2)}) async-start(bf16[896,16,256]{2,0,1:T(8,128)(2,1)} %bitcast.43), calls=%async_computation.2 | async-start | bytes 14680064 | tf_op jit(solution)/shard_map/all_to_all | solution.py:63
  168.3 3.6 %copy.25 = bf16[64,8,16,256]{3,2,1,0:T(8,128)(2,1)S(1)} copy(bf16[64,8,16,256]{3,1,2,0:T(8,128)(2,1)} %bitcast.45) | data formatting | bytes 8388608
  172.2 4.4 %fusion.5 = f32[512,896,1]{1,0,2:T(8,128)S(1)} fusion(bf16[8,896,256]{2,1,0:T(8,128)(2,1)} %all-to-all-done, bf16[512,1,8,256]{3,2,1,0:T(8,128)(2,1)S(1)} %get-tuple-element.55), kind=kOutput, calls=%fused_computation.17 | convolution fusion | flops 1879048192 | bytes 7602176 | tf_op jit(solution)/shard_map/tsd,sfd->tf/dot_general | solution.py:52
  176.7 6.3 %multiply_convert_fusion = (bf16[512,896]{1,0:T(8,128)(2,1)}, bf16[512,896]{1,0:T(8,128)(2,1)}) fusion(bf16[512,896]{1,0:T(8,128)(2,1)S(1)} %copy-done.4, bf16[512,896]{1,0:T(8,128)(2,1)S(1)} %copy-done.5, bf16[8,896,256]{2,1,0:T(8,128)(2,1)} %all-to-all-done.1, bf16[512,1,8,256]{3,2,1,0:T(8,128)(2,1)S(1)} %get-tuple-element.54, f32[512,896,1]{1,0,2:T(8,128)S(1)} %fusion.5), kind=kOutput, calls=%fused_computation.30 | convolution fusion | flops 1886388224 | bytes 11272192 | tf_op jit(solution)/shard_map/tsd,sfd->tf/dot_general | solution.py:54
  183.0 144.1 %all-to-all-done.2 = bf16[896,16,256]{2,0,1:T(8,128)(2,1)} async-done(((bf16[896,16,256]{2,0,1:T(8,128)(2,1)}), bf16[896,16,256]{2,0,1:T(8,128)(2,1)}, u32[]{:S(2)}, u32[]{:S(2)}) %all-to-all-start.2) | async-done | bytes 7340064 | tf_op jit(solution)/shard_map/all_to_all | solution.py:63
  327.0 7.4 %fusion = f32[4,896,256]{2,0,1:T(4,128)S(1)} fusion(bf16[896,16,256]{2,0,1:T(8,128)(2,1)} %all-to-all-done.2, s32[16]{0:T(128)S(1)} %copy-done.3), kind=kOutput, calls=%fused_computation.4 | convolution fusion | flops 29360192 | bytes 11010112 | tf_op jit(solution)/shard_map/lg,fgd->lfd/dot_general | solution.py:70
  334.4 2.5 copy.23
  (29 shorter events, 4.9 us)
Async XLA Ops:
  0.6 15.3 %collective-permute-start = (bf16[32,4096]{1,0:T(8,128)(2,1)}, bf16[32,4096]{1,0:T(8,128)(2,1)S(1)}, u32[]{:S(2)}, u32[]{:S(2)}) collective-permute-start(bf16[32,4096]{1,0:T(8,128)(2,1)} %param.5), channel_id=1, source_target_pairs={{0,8},{8,0},{1,9},{9,1},{2,10},{10,2},{3,11},{11,3},{4,12},{12,4},... | collective-permute-start | bytes 786440 | tf_op jit(solution)/shard_map/ppermute | solution.py:19
  7.0 16.8 %copy-start.1 = (bf16[4,896,256]{2,1,0:T(8,128)(2,1)S(1)}, bf16[4,896,256]{2,1,0:T(8,128)(2,1)}, u32[]{:S(2)}) copy-start(bf16[4,896,256]{2,1,0:T(8,128)(2,1)} %param.8) | copy-start | bytes 5505028
  15.9 93.1 %all-to-all-start = ((bf16[8,896,256]{2,1,0:T(8,128)(2,1)}), bf16[8,896,256]{2,1,0:T(8,128)(2,1)}, u32[]{:S(2)}, u32[]{:S(2)}) async-start(bf16[8,896,256]{2,1,0:T(8,128)(2,1)} %gather_fusion), calls=%async_computation | async-start | bytes 7340032 | tf_op jit(solution)/shard_map/all_to_all | solution.py:26
  23.8 81.1 %collective-permute-start.5 = (bf16[4,896,256]{2,1,0:T(8,128)(2,1)S(1)}, bf16[4,896,256]{2,1,0:T(8,128)(2,1)}, u32[]{:S(2)}, u32[]{:S(2)}) collective-permute-start(bf16[4,896,256]{2,1,0:T(8,128)(2,1)S(1)} %copy-done.1), channel_id=1, source_target_pairs={{0,128},{128,0},{1,129},{129,1},{2,130},{130,2},{3,131},{131,3},{4... | collective-permute-start | bytes 5505032 | tf_op jit(solution)/shard_map/ppermute | solution.py:27
  109.0 6.6 %copy-start.2 = (bf16[32,4096]{1,0:T(8,128)(2,1)S(1)}, bf16[32,4096]{1,0:T(8,128)(2,1)}, u32[]{:S(2)}) copy-start(bf16[32,4096]{1,0:T(8,128)(2,1)} %param.5) | copy-start | bytes 786436
  109.0 51.8 %all-to-all-start.1 = ((bf16[8,896,256]{2,1,0:T(8,128)(2,1)}), bf16[8,896,256]{2,1,0:T(8,128)(2,1)}, u32[]{:S(2)}, u32[]{:S(2)}) async-start(bf16[8,896,256]{2,1,0:T(8,128)(2,1)} %gather_fusion.2), calls=%async_computation.1 | async-start | bytes 7340032 | tf_op jit(solution)/shard_map/all_to_all | solution.py:29
  115.7 21.6 %collective-permute-start.3 = (bf16[2,32,4096]{2,1,0:T(8,128)(2,1)S(1)}, bf16[2,32,4096]{2,1,0:T(8,128)(2,1)S(1)}, u32[]{:S(2)}, u32[]{:S(2)}) collective-permute-start(bf16[2,32,4096]{2,1,0:T(8,128)(2,1)S(1)} %maximum_select_fusion.2), channel_id=1, source_target_pairs={{0,6},{2,0},{4,2},{6,4},{1,7},{3,1},{5,3},{7,5},{8,14},{10,8},{12,... | collective-permute-start | bytes 1572872 | tf_op jit(solution)/shard_map/ppermute | solution.py:36
  118.8 18.5 %collective-permute-start.2 = (bf16[2,32,4096]{2,1,0:T(8,128)(2,1)S(1)}, bf16[2,32,4096]{2,1,0:T(8,128)(2,1)S(1)}, u32[]{:S(2)}, u32[]{:S(2)}) collective-permute-start(bf16[2,32,4096]{2,1,0:T(8,128)(2,1)S(1)} %maximum_select_fusion.2), channel_id=1, source_target_pairs={{0,4},{2,6},{4,0},{6,2},{1,5},{3,7},{5,1},{7,3},{8,12},{10,14},{12... | collective-permute-start | bytes 1572872 | tf_op jit(solution)/shard_map/ppermute | solution.py:36
  119.4 21.5 %collective-permute-start.1 = (bf16[2,32,4096]{2,1,0:T(8,128)(2,1)S(1)}, bf16[2,32,4096]{2,1,0:T(8,128)(2,1)S(1)}, u32[]{:S(2)}, u32[]{:S(2)}) collective-permute-start(bf16[2,32,4096]{2,1,0:T(8,128)(2,1)S(1)} %maximum_select_fusion.2), channel_id=1, source_target_pairs={{0,2},{2,4},{4,6},{6,0},{1,3},{3,5},{5,7},{7,1},{8,10},{10,12},{12... | collective-permute-start | bytes 1572872 | tf_op jit(solution)/shard_map/ppermute | solution.py:36
  143.3 4.4 %collective-permute-start.4 = (bf16[4,2,32,4096]{3,2,1,0:T(8,128)(2,1)}, bf16[4,2,32,4096]{3,2,1,0:T(8,128)(2,1)S(1)}, u32[]{:S(2)}, u32[]{:S(2)}) collective-permute-start(bf16[4,2,32,4096]{3,2,1,0:T(8,128)(2,1)} %gather_fusion.1), channel_id=1, source_target_pairs={{0,1},{1,0},{2,3},{3,2},{4,5},{5,4},{6,7},{7,6},{8,9},{9,8},{10,11... | collective-permute-start | bytes 6291464 | tf_op jit(solution)/shard_map/ppermute | solution.py:40
  150.5 1.2 copy-start.4
  150.5 2.0 copy-start.5
  150.8 6.3 %copy-start = (bf16[2,4,2,32,4096]{4,3,2,1,0:T(8,128)(2,1)}, bf16[2,4,2,32,4096]{4,3,2,1,0:T(8,128)(2,1)S(1)}, u32[]{:S(2)}) copy-start(bf16[2,4,2,32,4096]{4,3,2,1,0:T(8,128)(2,1)S(1)} %copy.17) | copy-start | bytes 12582916
  160.8 166.2 %all-to-all-start.2 = ((bf16[896,16,256]{2,0,1:T(8,128)(2,1)}), bf16[896,16,256]{2,0,1:T(8,128)(2,1)}, u32[]{:S(2)}, u32[]{:S(2)}) async-start(bf16[896,16,256]{2,0,1:T(8,128)(2,1)} %bitcast.43), calls=%async_computation.2 | async-start | bytes 14680064 | tf_op jit(solution)/shard_map/all_to_all | solution.py:63
  176.6 150.4 %copy-start.3 = (s32[16]{0:T(128)S(1)}, s32[16]{0:T(128)}, u32[]{:S(2)}) copy-start(s32[16]{0:T(128)} %param.9) | copy-start | bytes 196

commit v5 on v4

--- a/solution.py
+++ b/solution.py
@@ -54,20 +54,25 @@
     ) + jnp.einsum("tsd,sfd->tf", cot_far, far, preferred_element_type=jnp.float32)
     d_up = (d_hidden * act).astype(jnp.bfloat16)
     d_gate = (d_hidden * up_f * sig * (1.0 + gate_f * (1.0 - sig))).astype(jnp.bfloat16)
-    selector = (language[None, :] == jnp.arange(variants, dtype=jnp.int32)[:, None]).astype(
-        jnp.bfloat16
+    rows_g = out_rows.reshape(out_rows.shape[0], groups, feat_dev)
+    pieces = jnp.einsum(
+        "tf,tgd->gfd", hidden, rows_g, preferred_element_type=jnp.float32
+    ).astype(jnp.bfloat16)
+    me = lax.axis_index(DP)
+    got = [jnp.take(pieces, me, axis=0, mode="clip")]
+    for shift in range(1, groups):
+        piece = jnp.take(pieces, (me + shift) % groups, axis=0, mode="clip")
+        got.append(
+            lax.ppermute(piece, DP, [(i, (i + shift) % groups) for i in range(groups)])
+        )
+    source = (me - jnp.arange(groups)) % groups
+    selector = (
+        jnp.take(language, source, mode="clip")[None, :]
+        == jnp.arange(variants, dtype=jnp.int32)[:, None]
+    ).astype(jnp.bfloat16)
+    d_weight = jnp.einsum(
+        "lk,kfd->lfd", selector, jnp.stack(got), preferred_element_type=jnp.float32
     )
-    partial_term = lax.dot_general(
-        hidden, out_rows, (((0,), (0,)), ((), ())), preferred_element_type=jnp.float32
-    ).astype(jnp.bfloat16)
-    pieces = lax.all_to_all(
-        partial_term.reshape(ff_dev, groups, feat_dev),
-        DP,
-        split_axis=1,
-        concat_axis=1,
-        tiled=True,
-    )
-    d_weight = jnp.einsum("lg,fgd->lfd", selector, pieces, preferred_element_type=jnp.float32)
     return (d_gate, d_up, d_weight)
 
 

time: 340 us -> 443 us (1.30)
  waiting for transfers between devices: 257 us -> 299 us
  local copies, waits for them, and re-layouts: 23.1 us -> 53.3 us
  starting transfers between devices: 29.3 us -> 57.6 us
  matrix products: 22.6 us -> 27.2 us
    ppermute x0 -> x15, waiting for transfers between devices: none -> 186 us  [shards(): lax.ppermute(piece, DP, [(i, (i + shift) % groups) for i in range(groups)])]
    all_to_all x1 -> x0, waiting for transfers between devices: 144 us -> none  [shards(): lax.all_to_all(partial_term.reshape(ff_dev, groups, feat_dev), DP, split_...]
    ppermute x0 -> x15, starting transfers between devices: none -> 36.3 us  [shards(): lax.ppermute(piece, DP, [(i, (i + shift) % groups) for i in range(groups)])]
    unnamed x14 -> x53, local copies, waits for them, and re-layouts: 7.86 us -> 21.4 us
    another operation x0 -> x2, local copies, waits for them, and re-layouts: none -> 13 us  [shards(): jnp.stack(got)]
    all_to_all x1 -> x0, starting transfers between devices: 7.53 us -> none  [shards(): lax.all_to_all(partial_term.reshape(ff_dev, groups, feat_dev), DP, split_...]
  transfers between devices with their start and end apart: 9 -> 23, of which waited for: 6 -> 14; matrix products, arithmetic and copies ran while one was open for 11% -> 17% of each run, Pallas kernels for 0% -> 0%
where the time goes in v5:
time: 443 us; the launch traced here: 442 us
  waiting for transfers between devices  299 us (67%)
  starting transfers between devices  57.6 us (13%)
  local copies, waits for them, and re-layouts  53.3 us (12%)
  matrix products  27.2 us (6%)
    ppermute x15, waiting for transfers between devices, shards(): lax.ppermute(piece, DP, [(i, (i + shift) % groups) for i in range(groups)])  186 us
    ppermute x1, waiting for transfers between devices, shards(): block = lax.ppermute(w_down, 'zh2', [(0, 1), (1, 0)])  81.5 us
    ppermute x15, starting transfers between devices, shards(): lax.ppermute(piece, DP, [(i, (i + shift) % groups) for i in range(groups)])  36.3 us
    ppermute x3, waiting for transfers between devices, shards(): lax.ppermute(pair, 'y', [(i, (i + shift) % ring) for i in range(ring)])  23.4 us
    unnamed x53, local copies, waits for them, and re-layouts  21.4 us
    another operation x2, local copies, waits for them, and re-layouts, shards(): jnp.stack(got)  13 us
    dot_general x1, matrix products, shards(): jnp.einsum('tf,tgd->gfd', hidden, rows_g, preferred_element_type=jnp.floa...  10.2 us
    ppermute x1, waiting for transfers between devices, shards(): partner = lax.ppermute(cotangent, 'zh', [(0, 1), (1, 0)])  8.9 us
  transfers between devices with their start and end apart: 23, of which 14 were waited for; matrix products, arithmetic and copies ran while one was open for 17% of the time, Pallas kernels for 0%

profile of v5, /device:TPU:228, one launch (start us, length us, event | category | flops | bytes accessed | tf_op | source)
XLA Modules:
  0.0 442.4 jit_solution(1930768132155159867)
XLA Ops:
  7.0 8.9 %collective-permute-done = bf16[32,4096]{1,0:T(8,128)(2,1)S(1)} collective-permute-done((bf16[32,4096]{1,0:T(8,128)(2,1)}, bf16[32,4096]{1,0:T(8,128)(2,1)S(1)}, u32[]{:S(2)}, u32[]{:S(2)}) %collective-permute-start) | collective-permute-done | bytes 262176 | tf_op jit(solution)/shard_map/ppermute | solution.py:19
  15.9 7.9 %all-to-all-start = ((bf16[8,896,256]{2,1,0:T(8,128)(2,1)}), bf16[8,896,256]{2,1,0:T(8,128)(2,1)}, u32[]{:S(2)}, u32[]{:S(2)}) async-start(bf16[8,896,256]{2,1,0:T(8,128)(2,1)} %gather_fusion), calls=%async_computation | async-start | bytes 7340032 | tf_op jit(solution)/shard_map/all_to_all | solution.py:26
  29.4 19.7 %collective-permute-done.3 = bf16[2,32,4096]{2,1,0:T(8,128)(2,1)S(1)} collective-permute-done((bf16[2,32,4096]{2,1,0:T(8,128)(2,1)S(1)}, bf16[2,32,4096]{2,1,0:T(8,128)(2,1)S(1)}, u32[]{:S(2)}, u32[]{:S(2)}) %collective-permute-start.3) | collective-permute-done | bytes 524320 | tf_op jit(solution)/shard_map/ppermute | solution.py:36
  56.6 81.5 %collective-permute-done.5 = bf16[4,896,256]{2,1,0:T(8,128)(2,1)} collective-permute-done((bf16[4,896,256]{2,1,0:T(8,128)(2,1)}, bf16[4,896,256]{2,1,0:T(8,128)(2,1)}, u32[]{:S(2)}, u32[]{:S(2)}) %collective-permute-start.5) | collective-permute-done | bytes 1835040 | tf_op jit(solution)/shard_map/ppermute | solution.py:27
  138.2 4.1 gather_fusion.2
  149.0 5.8 %all-to-all-start.1 = ((bf16[8,896,256]{2,1,0:T(8,128)(2,1)}), bf16[8,896,256]{2,1,0:T(8,128)(2,1)}, u32[]{:S(2)}, u32[]{:S(2)}) async-start(bf16[8,896,256]{2,1,0:T(8,128)(2,1)} %gather_fusion.2), calls=%async_computation.1 | async-start | bytes 7340032 | tf_op jit(solution)/shard_map/all_to_all | solution.py:29
  154.9 10.2 %convolution_convert_fusion = bf16[16,256,896]{2,1,0:T(8,128)(2,1)S(1)} fusion(bf16[512,16,256]{2,1,0:T(8,128)(2,1)} %bitcast.139, bf16[512,896]{1,0:T(8,128)(2,1)S(1)} %copy-done.17, bf16[512,896]{1,0:T(8,128)(2,1)S(1)} %copy-done.15), kind=kOutput, calls=%fused_computation.4 | convolution fusion | flops 3765436416 | bytes 13369344 | tf_op jit(solution)/shard_map/tf,tgd->gfd/dot_general | solution.py:58
  175.2 4.1 collective-permute-start.7
  185.2 40.0 %collective-permute-done.6 = bf16[896,256]{0,1:T(8,128)(2,1)S(1)} collective-permute-done((bf16[896,256]{0,1:T(8,128)(2,1)}, bf16[896,256]{0,1:T(8,128)(2,1)S(1)}, u32[]{:S(2)}, u32[]{:S(2)}) %collective-permute-start.6) | collective-permute-done | bytes 458784 | tf_op jit(solution)/shard_map/ppermute | solution.py:66
  226.0 16.3 %collective-permute-done.7 = bf16[896,256]{0,1:T(8,128)(2,1)S(1)} collective-permute-done((bf16[896,256]{0,1:T(8,128)(2,1)}, bf16[896,256]{0,1:T(8,128)(2,1)S(1)}, u32[]{:S(2)}, u32[]{:S(2)}) %collective-permute-start.7) | collective-permute-done | bytes 458784 | tf_op jit(solution)/shard_map/ppermute | solution.py:66
  243.6 5.9 %collective-permute-done.8 = bf16[896,256]{0,1:T(8,128)(2,1)S(1)} collective-permute-done((bf16[896,256]{0,1:T(8,128)(2,1)S(1)}, bf16[896,256]{0,1:T(8,128)(2,1)S(1)}, u32[]{:S(2)}, u32[]{:S(2)}) %collective-permute-start.8) | collective-permute-done | bytes 458784 | tf_op jit(solution)/shard_map/ppermute | solution.py:66
  250.3 9.1 %collective-permute-done.9 = bf16[896,256]{0,1:T(8,128)(2,1)S(1)} collective-permute-done((bf16[896,256]{0,1:T(8,128)(2,1)S(1)}, bf16[896,256]{0,1:T(8,128)(2,1)S(1)}, u32[]{:S(2)}, u32[]{:S(2)}) %collective-permute-start.9) | collective-permute-done | bytes 458784 | tf_op jit(solution)/shard_map/ppermute | solution.py:66
  260.3 9.0 %collective-permute-done.10 = bf16[896,256]{0,1:T(8,128)(2,1)S(1)} collective-permute-done((bf16[896,256]{0,1:T(8,128)(2,1)S(1)}, bf16[896,256]{0,1:T(8,128)(2,1)S(1)}, u32[]{:S(2)}, u32[]{:S(2)}) %collective-permute-start.10) | collective-permute-done | bytes 458784 | tf_op jit(solution)/shard_map/ppermute | solution.py:66
  269.3 20.5 %collective-permute-start.12 = (bf16[896,256]{0,1:T(8,128)(2,1)S(1)}, bf16[896,256]{0,1:T(8,128)(2,1)S(1)}, u32[]{:S(2)}, u32[]{:S(2)}) collective-permute-start(bf16[896,256]{0,1:T(8,128)(2,1)S(1)} %copy-done.10), channel_id=1, source_target_pairs={{0,112},{16,128},{32,144},{48,160},{64,176},{80,192},{96,208},{112... | collective-permute-start | bytes 1376264 | tf_op jit(solution)/shard_map/ppermute | solution.py:66
  290.6 6.4 %collective-permute-start.13 = (bf16[896,256]{0,1:T(8,128)(2,1)S(1)}, bf16[896,256]{0,1:T(8,128)(2,1)S(1)}, u32[]{:S(2)}, u32[]{:S(2)}) collective-permute-start(bf16[896,256]{0,1:T(8,128)(2,1)S(1)} %copy-done.9), channel_id=1, source_target_pairs={{0,128},{16,144},{32,160},{48,176},{64,192},{80,208},{96,224},{112... | collective-permute-start | bytes 1376264 | tf_op jit(solution)/shard_map/ppermute | solution.py:66
  297.9 47.5 %collective-permute-done.12 = bf16[896,256]{0,1:T(8,128)(2,1)S(1)} collective-permute-done((bf16[896,256]{0,1:T(8,128)(2,1)S(1)}, bf16[896,256]{0,1:T(8,128)(2,1)S(1)}, u32[]{:S(2)}, u32[]{:S(2)}) %collective-permute-start.12) | collective-permute-done | bytes 458784 | tf_op jit(solution)/shard_map/ppermute | solution.py:66
  347.0 38.6 %collective-permute-done.14 = bf16[896,256]{0,1:T(8,128)(2,1)S(1)} collective-permute-done((bf16[896,256]{0,1:T(8,128)(2,1)S(1)}, bf16[896,256]{0,1:T(8,128)(2,1)S(1)}, u32[]{:S(2)}, u32[]{:S(2)}) %collective-permute-start.14) | collective-permute-done | bytes 458784 | tf_op jit(solution)/shard_map/ppermute | solution.py:66
  386.4 8.7 %collective-permute-done.15 = bf16[896,256]{0,1:T(8,128)(2,1)S(1)} collective-permute-done((bf16[896,256]{0,1:T(8,128)(2,1)S(1)}, bf16[896,256]{0,1:T(8,128)(2,1)S(1)}, u32[]{:S(2)}, u32[]{:S(2)}) %collective-permute-start.15) | collective-permute-done | bytes 458784 | tf_op jit(solution)/shard_map/ppermute | solution.py:66
  396.0 5.6 %collective-permute-done.16 = bf16[896,256]{0,1:T(8,128)(2,1)S(1)} collective-permute-done((bf16[896,256]{0,1:T(8,128)(2,1)S(1)}, bf16[896,256]{0,1:T(8,128)(2,1)S(1)}, u32[]{:S(2)}, u32[]{:S(2)}) %collective-permute-start.16) | collective-permute-done | bytes 458784 | tf_op jit(solution)/shard_map/ppermute | solution.py:66
  402.4 5.0 %collective-permute-done.17 = bf16[896,256]{0,1:T(8,128)(2,1)S(1)} collective-permute-done((bf16[896,256]{0,1:T(8,128)(2,1)S(1)}, bf16[896,256]{0,1:T(8,128)(2,1)S(1)}, u32[]{:S(2)}, u32[]{:S(2)}) %collective-permute-start.17) | collective-permute-done | bytes 458784 | tf_op jit(solution)/shard_map/ppermute | solution.py:66
  410.6 12.2 %copy.15 = bf16[16,896,256]{2,0,1:T(8,128)(2,1)} copy(bf16[16,896,256]{1,2,0:T(8,128)(2,1)} %bitcast_dynamic-update-slice_fusion) | data formatting | bytes 14680064 | tf_op jit(solution)/shard_map/stack | solution.py:74
  422.8 4.2 fusion.21
  429.6 5.7 %fusion.4 = f32[512,896,1]{1,0,2:T(8,128)} fusion(bf16[8,896,256]{2,1,0:T(8,128)(2,1)} %all-to-all-done, bf16[512,1,8,256]{3,2,1,0:T(8,128)(2,1)S(1)} %copy-done.3), kind=kOutput, calls=%fused_computation.16 | convolution fusion | flops 1879048192 | bytes 7602176 | tf_op jit(solution)/shard_map/tsd,sfd->tf/dot_general | solution.py:52
  435.3 7.1 %multiply_convert_fusion = (bf16[512,896]{1,0:T(8,128)(2,1)}, bf16[512,896]{1,0:T(8,128)(2,1)}) fusion(bf16[512,896]{1,0:T(8,128)(2,1)S(1)} %copy-done.16, bf16[512,896]{1,0:T(8,128)(2,1)} %param.7, bf16[8,896,256]{2,1,0:T(8,128)(2,1)} %all-to-all-done.1, bf16[512,1,8,256]{3,2,1,0:T(8,128)(2,1)S(1)} %get-tuple-element.239, f32[512,896,1]{1,0,2:T(8,128)} %fusion.4), kind=kOutput, calls=%fused_computation.29 | convolution fusion | flops 1886388224 | bytes 11272192 | tf_op jit(solution)/shard_map/tsd,sfd->tf/dot_general | solution.py:54
  (101 shorter events, 57.5 us)
Async XLA Ops:
  0.6 15.3 %collective-permute-start = (bf16[32,4096]{1,0:T(8,128)(2,1)}, bf16[32,4096]{1,0:T(8,128)(2,1)S(1)}, u32[]{:S(2)}, u32[]{:S(2)}) collective-permute-start(bf16[32,4096]{1,0:T(8,128)(2,1)} %param.5), channel_id=1, source_target_pairs={{0,8},{8,0},{1,9},{9,1},{2,10},{10,2},{3,11},{11,3},{4,12},{12,4},... | collective-permute-start | bytes 786440 | tf_op jit(solution)/shard_map/ppermute | solution.py:19
  15.9 133.1 %all-to-all-start = ((bf16[8,896,256]{2,1,0:T(8,128)(2,1)}), bf16[8,896,256]{2,1,0:T(8,128)(2,1)}, u32[]{:S(2)}, u32[]{:S(2)}) async-start(bf16[8,896,256]{2,1,0:T(8,128)(2,1)} %gather_fusion), calls=%async_computation | async-start | bytes 7340032 | tf_op jit(solution)/shard_map/all_to_all | solution.py:26
  24.6 24.5 %collective-permute-start.3 = (bf16[2,32,4096]{2,1,0:T(8,128)(2,1)S(1)}, bf16[2,32,4096]{2,1,0:T(8,128)(2,1)S(1)}, u32[]{:S(2)}, u32[]{:S(2)}) collective-permute-start(bf16[2,32,4096]{2,1,0:T(8,128)(2,1)S(1)} %maximum_select_fusion.2), channel_id=1, source_target_pairs={{0,6},{2,0},{4,2},{6,4},{1,7},{3,1},{5,3},{7,5},{8,14},{10,8},{12,... | collective-permute-start | bytes 1572872 | tf_op jit(solution)/shard_map/ppermute | solution.py:36
  27.7 21.4 %collective-permute-start.2 = (bf16[2,32,4096]{2,1,0:T(8,128)(2,1)S(1)}, bf16[2,32,4096]{2,1,0:T(8,128)(2,1)S(1)}, u32[]{:S(2)}, u32[]{:S(2)}) collective-permute-start(bf16[2,32,4096]{2,1,0:T(8,128)(2,1)S(1)} %maximum_select_fusion.2), channel_id=1, source_target_pairs={{0,4},{2,6},{4,0},{6,2},{1,5},{3,7},{5,1},{7,3},{8,12},{10,14},{12... | collective-permute-start | bytes 1572872 | tf_op jit(solution)/shard_map/ppermute | solution.py:36
  28.4 24.5 %collective-permute-start.1 = (bf16[2,32,4096]{2,1,0:T(8,128)(2,1)S(1)}, bf16[2,32,4096]{2,1,0:T(8,128)(2,1)S(1)}, u32[]{:S(2)}, u32[]{:S(2)}) collective-permute-start(bf16[2,32,4096]{2,1,0:T(8,128)(2,1)S(1)} %maximum_select_fusion.2), channel_id=1, source_target_pairs={{0,2},{2,4},{4,6},{6,0},{1,3},{3,5},{5,7},{7,1},{8,10},{10,12},{12... | collective-permute-start | bytes 1572872 | tf_op jit(solution)/shard_map/ppermute | solution.py:36
  55.2 87.2 %collective-permute-start.4 = (bf16[4,2,32,4096]{3,2,1,0:T(8,128)(2,1)}, bf16[4,2,32,4096]{3,2,1,0:T(8,128)(2,1)}, u32[]{:S(2)}, u32[]{:S(2)}) collective-permute-start(bf16[4,2,32,4096]{3,2,1,0:T(8,128)(2,1)} %gather_fusion.1), channel_id=1, source_target_pairs={{0,1},{1,0},{2,3},{3,2},{4,5},{5,4},{6,7},{7,6},{8,9},{9,8},{10,11... | collective-permute-start | bytes 6291464 | tf_op jit(solution)/shard_map/ppermute | solution.py:40
  55.2 83.0 %collective-permute-start.5 = (bf16[4,896,256]{2,1,0:T(8,128)(2,1)}, bf16[4,896,256]{2,1,0:T(8,128)(2,1)}, u32[]{:S(2)}, u32[]{:S(2)}) collective-permute-start(bf16[4,896,256]{2,1,0:T(8,128)(2,1)} %param.8), channel_id=1, source_target_pairs={{0,128},{128,0},{1,129},{129,1},{2,130},{130,2},{3,131},{131,3},{4... | collective-permute-start | bytes 5505032 | tf_op jit(solution)/shard_map/ppermute | solution.py:27
  149.0 286.3 %all-to-all-start.1 = ((bf16[8,896,256]{2,1,0:T(8,128)(2,1)}), bf16[8,896,256]{2,1,0:T(8,128)(2,1)}, u32[]{:S(2)}, u32[]{:S(2)}) async-start(bf16[8,896,256]{2,1,0:T(8,128)(2,1)} %gather_fusion.2), calls=%async_computation.1 | async-start | bytes 7340032 | tf_op jit(solution)/shard_map/all_to_all | solution.py:29
  169.8 55.4 %collective-permute-start.6 = (bf16[896,256]{0,1:T(8,128)(2,1)}, bf16[896,256]{0,1:T(8,128)(2,1)S(1)}, u32[]{:S(2)}, u32[]{:S(2)}) collective-permute-start(bf16[896,256]{0,1:T(8,128)(2,1)} %get-tuple-element.238), channel_id=1, source_target_pairs={{0,16},{16,32},{32,48},{48,64},{64,80},{80,96},{96,112},{112,128},... | collective-permute-start | bytes 1376264 | tf_op jit(solution)/shard_map/ppermute | solution.py:66
  171.6 238.2 %collective-permute-start.20 = (bf16[896,256]{0,1:T(8,128)(2,1)S(1)}, bf16[896,256]{0,1:T(8,128)(2,1)S(1)}, u32[]{:S(2)}, u32[]{:S(2)}) collective-permute-start(bf16[896,256]{0,1:T(8,128)(2,1)S(1)} %get-tuple-element.224), channel_id=1, source_target_pairs={{0,240},{16,0},{32,16},{48,32},{64,48},{80,64},{96,80},{112,96},{1... | collective-permute-start | bytes 1376264 | tf_op jit(solution)/shard_map/ppermute | solution.py:66
  172.6 236.4 %collective-permute-start.19 = (bf16[896,256]{0,1:T(8,128)(2,1)S(1)}, bf16[896,256]{0,1:T(8,128)(2,1)S(1)}, u32[]{:S(2)}, u32[]{:S(2)}) collective-permute-start(bf16[896,256]{0,1:T(8,128)(2,1)S(1)} %get-tuple-element.225), channel_id=1, source_target_pairs={{0,224},{16,240},{32,0},{48,16},{64,32},{80,48},{96,64},{112,80},{... | collective-permute-start | bytes 1376264 | tf_op jit(solution)/shard_map/ppermute | solution.py:66
  175.2 232.9 %collective-permute-start.18 = (bf16[896,256]{0,1:T(8,128)(2,1)}, bf16[896,256]{0,1:T(8,128)(2,1)S(1)}, u32[]{:S(2)}, u32[]{:S(2)}) collective-permute-start(bf16[896,256]{0,1:T(8,128)(2,1)} %get-tuple-element.226), channel_id=1, source_target_pairs={{0,208},{16,224},{32,240},{48,0},{64,16},{80,32},{96,48},{112,64},... | collective-permute-start | bytes 1376264 | tf_op jit(solution)/shard_map/ppermute | solution.py:66
  175.2 67.1 %collective-permute-start.7 = (bf16[896,256]{0,1:T(8,128)(2,1)}, bf16[896,256]{0,1:T(8,128)(2,1)S(1)}, u32[]{:S(2)}, u32[]{:S(2)}) collective-permute-start(bf16[896,256]{0,1:T(8,128)(2,1)} %get-tuple-element.237), channel_id=1, source_target_pairs={{0,32},{16,48},{32,64},{48,80},{64,96},{80,112},{96,128},{112,144}... | collective-permute-start | bytes 1376264 | tf_op jit(solution)/shard_map/ppermute | solution.py:66
  185.2 161.0 %copy-start.7 = (bf16[896,256]{0,1:T(8,128)(2,1)S(1)}, bf16[896,256]{0,1:T(8,128)(2,1)}, u32[]{:S(2)}) copy-start(bf16[896,256]{0,1:T(8,128)(2,1)} %get-tuple-element.229) | copy-start | bytes 1376260
  225.2 24.3 %collective-permute-start.8 = (bf16[896,256]{0,1:T(8,128)(2,1)S(1)}, bf16[896,256]{0,1:T(8,128)(2,1)S(1)}, u32[]{:S(2)}, u32[]{:S(2)}) collective-permute-start(bf16[896,256]{0,1:T(8,128)(2,1)S(1)} %copy-done.14), channel_id=1, source_target_pairs={{0,48},{16,64},{32,80},{48,96},{64,112},{80,128},{96,144},{112,160... | collective-permute-start | bytes 1376264 | tf_op jit(solution)/shard_map/ppermute | solution.py:66
  242.3 17.1 %collective-permute-start.9 = (bf16[896,256]{0,1:T(8,128)(2,1)S(1)}, bf16[896,256]{0,1:T(8,128)(2,1)S(1)}, u32[]{:S(2)}, u32[]{:S(2)}) collective-permute-start(bf16[896,256]{0,1:T(8,128)(2,1)S(1)} %copy-done.13), channel_id=1, source_target_pairs={{0,64},{16,80},{32,96},{48,112},{64,128},{80,144},{96,160},{112,17... | collective-permute-start | bytes 1376264 | tf_op jit(solution)/shard_map/ppermute | solution.py:66
  249.5 19.8 %collective-permute-start.10 = (bf16[896,256]{0,1:T(8,128)(2,1)S(1)}, bf16[896,256]{0,1:T(8,128)(2,1)S(1)}, u32[]{:S(2)}, u32[]{:S(2)}) collective-permute-start(bf16[896,256]{0,1:T(8,128)(2,1)S(1)} %copy-done.12), channel_id=1, source_target_pairs={{0,80},{16,96},{32,112},{48,128},{64,144},{80,160},{96,176},{112,1... | collective-permute-start | bytes 1376264 | tf_op jit(solution)/shard_map/ppermute | solution.py:66
  259.4 31.2 %collective-permute-start.11 = (bf16[896,256]{0,1:T(8,128)(2,1)S(1)}, bf16[896,256]{0,1:T(8,128)(2,1)S(1)}, u32[]{:S(2)}, u32[]{:S(2)}) collective-permute-start(bf16[896,256]{0,1:T(8,128)(2,1)S(1)} %copy-done.11), channel_id=1, source_target_pairs={{0,96},{16,112},{32,128},{48,144},{64,160},{80,176},{96,192},{112,... | collective-permute-start | bytes 1376264 | tf_op jit(solution)/shard_map/ppermute | solution.py:66
  269.3 76.1 %collective-permute-start.12 = (bf16[896,256]{0,1:T(8,128)(2,1)S(1)}, bf16[896,256]{0,1:T(8,128)(2,1)S(1)}, u32[]{:S(2)}, u32[]{:S(2)}) collective-permute-start(bf16[896,256]{0,1:T(8,128)(2,1)S(1)} %copy-done.10), channel_id=1, source_target_pairs={{0,112},{16,128},{32,144},{48,160},{64,176},{80,192},{96,208},{112... | collective-permute-start | bytes 1376264 | tf_op jit(solution)/shard_map/ppermute | solution.py:66
  290.6 55.5 %collective-permute-start.13 = (bf16[896,256]{0,1:T(8,128)(2,1)S(1)}, bf16[896,256]{0,1:T(8,128)(2,1)S(1)}, u32[]{:S(2)}, u32[]{:S(2)}) collective-permute-start(bf16[896,256]{0,1:T(8,128)(2,1)S(1)} %copy-done.9), channel_id=1, source_target_pairs={{0,128},{16,144},{32,160},{48,176},{64,192},{80,208},{96,224},{112... | collective-permute-start | bytes 1376264 | tf_op jit(solution)/shard_map/ppermute | solution.py:66
  345.3 40.3 %collective-permute-start.14 = (bf16[896,256]{0,1:T(8,128)(2,1)S(1)}, bf16[896,256]{0,1:T(8,128)(2,1)S(1)}, u32[]{:S(2)}, u32[]{:S(2)}) collective-permute-start(bf16[896,256]{0,1:T(8,128)(2,1)S(1)} %copy-done.8), channel_id=1, source_target_pairs={{0,144},{16,160},{32,176},{48,192},{64,208},{80,224},{96,240},{112... | collective-permute-start | bytes 1376264 | tf_op jit(solution)/shard_map/ppermute | solution.py:66
  346.2 49.0 %collective-permute-start.15 = (bf16[896,256]{0,1:T(8,128)(2,1)S(1)}, bf16[896,256]{0,1:T(8,128)(2,1)S(1)}, u32[]{:S(2)}, u32[]{:S(2)}) collective-permute-start(bf16[896,256]{0,1:T(8,128)(2,1)S(1)} %copy-done.7), channel_id=1, source_target_pairs={{0,160},{16,176},{32,192},{48,208},{64,224},{80,240},{96,0},{112,1... | collective-permute-start | bytes 1376264 | tf_op jit(solution)/shard_map/ppermute | solution.py:66
  385.6 15.9 %collective-permute-start.16 = (bf16[896,256]{0,1:T(8,128)(2,1)S(1)}, bf16[896,256]{0,1:T(8,128)(2,1)S(1)}, u32[]{:S(2)}, u32[]{:S(2)}) collective-permute-start(bf16[896,256]{0,1:T(8,128)(2,1)S(1)} %copy-done.6), channel_id=1, source_target_pairs={{0,176},{16,192},{32,208},{48,224},{64,240},{80,0},{96,16},{112,32... | collective-permute-start | bytes 1376264 | tf_op jit(solution)/shard_map/ppermute | solution.py:66
  395.1 12.2 %collective-permute-start.17 = (bf16[896,256]{0,1:T(8,128)(2,1)S(1)}, bf16[896,256]{0,1:T(8,128)(2,1)S(1)}, u32[]{:S(2)}, u32[]{:S(2)}) collective-permute-start(bf16[896,256]{0,1:T(8,128)(2,1)S(1)} %copy-done.5), channel_id=1, source_target_pairs={{0,192},{16,208},{32,224},{48,240},{64,0},{80,16},{96,32},{112,48}... | collective-permute-start | bytes 1376264 | tf_op jit(solution)/shard_map/ppermute | solution.py:66
  (17 other events, 1048.2 us)

commit v6 on v4

--- a/solution.py
+++ b/solution.py
@@ -26,7 +26,13 @@
     near = lax.all_to_all(own_slabs, HALF, split_axis=0, concat_axis=0, tiled=True)
     block = lax.ppermute(w_down, "zh2", [(0, 1), (1, 0)])
     relay = jnp.take(block, own_langs, axis=0, mode="clip")
-    far = lax.all_to_all(relay, HALF, split_axis=0, concat_axis=0, tiled=True)
+    me_h = lax.axis_index(HALF)
+    far = [jnp.take(relay, me_h, axis=0, mode="clip")]
+    for shift in range(1, half):
+        slab = jnp.take(relay, (me_h + shift) % half, axis=0, mode="clip")
+        far.append(lax.ppermute(slab, HALF, [(i, (i + shift) % half) for i in range(half)]))
+    far = jnp.stack(far)
+    far_src = (me_h - jnp.arange(half)) % half
     first = lax.axis_index("zh") == 0
     pair = jnp.where(first, jnp.stack([cotangent, partner]), jnp.stack([partner, cotangent]))
     ring = lax.axis_size("y")
@@ -49,6 +55,7 @@
     rows3 = out_rows.reshape(out_rows.shape[0], 2, half, feat_dev)
     cot_near = jnp.take(rows3, side, axis=1, mode="clip")
     cot_far = jnp.take(rows3, 1 - side, axis=1, mode="clip")
+    cot_far = jnp.take(cot_far, far_src, axis=1, mode="clip")
     d_hidden = jnp.einsum(
         "tsd,sfd->tf", cot_near, near, preferred_element_type=jnp.float32
     ) + jnp.einsum("tsd,sfd->tf", cot_far, far, preferred_element_type=jnp.float32)

time: 340 us -> 416 us (1.22)
  waiting for transfers between devices: 257 us -> 316 us
  local copies, waits for them, and re-layouts: 23.1 us -> 34.5 us
  starting transfers between devices: 29.3 us -> 34.1 us
    ppermute x1, waiting for transfers between devices: 79.3 us -> 237 us  [shards(): block = lax.ppermute(w_down, 'zh2', [(0, 1), (1, 0)])]
    all_to_all x1, waiting for transfers between devices: 144 us -> 0.01 us  [shards(): lax.all_to_all(partial_term.reshape(ff_dev, groups, feat_dev), DP, split_...]
    ppermute x0 -> x7, waiting for transfers between devices: none -> 46 us  [shards(): lax.ppermute(slab, HALF, [(i, (i + shift) % half) for i in range(half)])]
    ppermute x0 -> x7, starting transfers between devices: none -> 10.5 us  [shards(): lax.ppermute(slab, HALF, [(i, (i + shift) % half) for i in range(half)])]
    all_to_all x1 -> x0, starting transfers between devices: 5.84 us -> none  [shards(): far = lax.all_to_all(relay, HALF, split_axis=0, concat_axis=0, tiled=True)]
    gather x0 -> x2, local copies, waits for them, and re-layouts: none -> 5.02 us  [the longest x1 3.01 us: shards(): slab = jnp.take(relay, (me_h + shift) % half, axis=0, mode='clip')]
    unnamed x14 -> x30, local copies, waits for them, and re-layouts: 7.86 us -> 11.7 us
  transfers between devices with their start and end apart: 9 -> 15, of which waited for: 6 -> 9; matrix products, arithmetic and copies ran while one was open for 11% -> 12% of each run, Pallas kernels for 0% -> 0%
where the time goes in v6:
time: 416 us; the launch traced here: 411 us
  waiting for transfers between devices  316 us (76%)
  local copies, waits for them, and re-layouts  34.5 us (8%)
  starting transfers between devices  34.1 us (8%)
  matrix products  21.3 us (5%)
    ppermute x1, waiting for transfers between devices, shards(): block = lax.ppermute(w_down, 'zh2', [(0, 1), (1, 0)])  237 us
    ppermute x7, waiting for transfers between devices, shards(): lax.ppermute(slab, HALF, [(i, (i + shift) % half) for i in range(half)])  46 us
    ppermute x3, waiting for transfers between devices, shards(): lax.ppermute(pair, 'y', [(i, (i + shift) % ring) for i in range(ring)])  20.4 us
    unnamed x30, local copies, waits for them, and re-layouts  11.7 us
    ppermute x7, starting transfers between devices, shards(): lax.ppermute(slab, HALF, [(i, (i + shift) % half) for i in range(half)])  10.5 us
    ppermute x1, waiting for transfers between devices, shards(): partner = lax.ppermute(cotangent, 'zh', [(0, 1), (1, 0)])  8.9 us
  transfers between devices with their start and end apart: 15, of which 9 were waited for; matrix products, arithmetic and copies ran while one was open for 12% of the time, Pallas kernels for 0%

profile of v6, /device:TPU:228, one launch (start us, length us, event | category | flops | bytes accessed | tf_op | source)
XLA Modules:
  0.0 411.1 jit_solution(823895534836827795)
XLA Ops:
  2.9 4.1 %gather_fusion = bf16[8,896,256]{2,1,0:T(8,128)(2,1)} fusion(bf16[4,896,256]{2,1,0:T(8,128)(2,1)} %param.8, s32[1024]{0:T(1024)S(1)} %pad_clamp_fusion.2), kind=kCustom, calls=%fused_computation | custom fusion | bytes 7340064 | tf_op jit(solution)/shard_map/jit(_take)/gather | solution.py:24
  7.0 8.9 %collective-permute-done = bf16[32,4096]{1,0:T(8,128)(2,1)S(1)} collective-permute-done((bf16[32,4096]{1,0:T(8,128)(2,1)}, bf16[32,4096]{1,0:T(8,128)(2,1)S(1)}, u32[]{:S(2)}, u32[]{:S(2)}) %collective-permute-start) | collective-permute-done | bytes 262176 | tf_op jit(solution)/shard_map/ppermute | solution.py:19
  15.9 7.9 %all-to-all-start = ((bf16[8,896,256]{2,1,0:T(8,128)(2,1)}), bf16[8,896,256]{2,1,0:T(8,128)(2,1)}, u32[]{:S(2)}, u32[]{:S(2)}) async-start(bf16[8,896,256]{2,1,0:T(8,128)(2,1)} %gather_fusion), calls=%async_computation | async-start | bytes 7340032 | tf_op jit(solution)/shard_map/all_to_all | solution.py:26
  26.3 2.9 collective-permute-start.2
  30.6 9.0 %collective-permute-done.1 = bf16[2,32,4096]{2,1,0:T(8,128)(2,1)S(1)} collective-permute-done((bf16[2,32,4096]{2,1,0:T(8,128)(2,1)S(1)}, bf16[2,32,4096]{2,1,0:T(8,128)(2,1)S(1)}, u32[]{:S(2)}, u32[]{:S(2)}) %collective-permute-start.1) | collective-permute-done | bytes 524320 | tf_op jit(solution)/shard_map/ppermute | solution.py:42
  39.7 11.4 %collective-permute-done.2 = bf16[2,32,4096]{2,1,0:T(8,128)(2,1)S(1)} collective-permute-done((bf16[2,32,4096]{2,1,0:T(8,128)(2,1)S(1)}, bf16[2,32,4096]{2,1,0:T(8,128)(2,1)S(1)}, u32[]{:S(2)}, u32[]{:S(2)}) %collective-permute-start.2) | collective-permute-done | bytes 524320 | tf_op jit(solution)/shard_map/ppermute | solution.py:42
  53.3 4.4 %collective-permute-done.4 = bf16[4,2,32,4096]{3,2,1,0:T(8,128)(2,1)S(1)} collective-permute-done((bf16[4,2,32,4096]{3,2,1,0:T(8,128)(2,1)}, bf16[4,2,32,4096]{3,2,1,0:T(8,128)(2,1)S(1)}, u32[]{:S(2)}, u32[]{:S(2)}) %collective-permute-start.4) | collective-permute-done | bytes 2097184 | tf_op jit(solution)/shard_map/ppermute | solution.py:46
  57.7 2.8 fusion.2
  62.6 4.5 %convolution_convert_fusion = bf16[896,4096]{1,0:T(8,128)(2,1)S(1)} fusion(bf16[512,4096]{1,0:T(8,128)(2,1)S(1)} %bitcast.77, bf16[512,896]{1,0:T(8,128)(2,1)S(1)} %copy-done.9, bf16[512,896]{1,0:T(8,128)(2,1)S(1)} %copy-done.7), kind=kOutput, calls=%fused_computation.7 | convolution fusion | flops 3765436416 | bytes 13369344 | tf_op jit(solution)/shard_map/dot_general | solution.py:67
  67.1 3.8 copy.33
  70.9 7.7 %all-to-all-start.1 = ((bf16[896,16,256]{2,0,1:T(8,128)(2,1)}), bf16[896,16,256]{2,0,1:T(8,128)(2,1)}, u32[]{:S(2)}, u32[]{:S(2)}) async-start(bf16[896,16,256]{2,0,1:T(8,128)(2,1)} %bitcast.76), calls=%async_computation.1 | async-start | bytes 14680064 | tf_op jit(solution)/shard_map/all_to_all | solution.py:70
  79.2 236.6 %collective-permute-done.5 = bf16[4,896,256]{2,1,0:T(8,128)(2,1)} collective-permute-done((bf16[4,896,256]{2,1,0:T(8,128)(2,1)S(1)}, bf16[4,896,256]{2,1,0:T(8,128)(2,1)}, u32[]{:S(2)}, u32[]{:S(2)}) %collective-permute-start.5) | collective-permute-done | bytes 1835040 | tf_op jit(solution)/shard_map/ppermute | solution.py:27
  315.8 4.1 %gather_fusion.3 = bf16[8,896,256]{2,1,0:T(8,128)(2,1)} fusion(bf16[4,896,256]{2,1,0:T(8,128)(2,1)} %collective-permute-done.5, s32[1024]{0:T(1024)S(1)} %pad_clamp_fusion.2), kind=kCustom, calls=%fused_computation.3 | custom fusion | bytes 7340064 | tf_op jit(solution)/shard_map/jit(_take)/gather | solution.py:28
  320.0 3.0 dynamic-slice_bitcast_fusion
  324.2 3.0 collective-permute-start.8
  327.2 2.4 collective-permute-start.10
  329.5 13.6 %collective-permute-done.6 = bf16[896,256]{1,0:T(8,128)(2,1)} collective-permute-done((bf16[896,256]{1,0:T(8,128)(2,1)S(1)}, bf16[896,256]{1,0:T(8,128)(2,1)}, u32[]{:S(2)}, u32[]{:S(2)}) %collective-permute-start.6) | collective-permute-done | bytes 458784 | tf_op jit(solution)/shard_map/ppermute | solution.py:33
  343.1 4.0 collective-permute-start.11
  348.9 21.8 %collective-permute-done.7 = bf16[896,256]{1,0:T(8,128)(2,1)S(1)} collective-permute-done((bf16[896,256]{1,0:T(8,128)(2,1)S(1)}, bf16[896,256]{1,0:T(8,128)(2,1)S(1)}, u32[]{:S(2)}, u32[]{:S(2)}) %collective-permute-start.7) | collective-permute-done | bytes 458784 | tf_op jit(solution)/shard_map/ppermute | solution.py:33
  375.4 10.1 %collective-permute-done.12 = bf16[896,256]{1,0:T(8,128)(2,1)S(1)} collective-permute-done((bf16[896,256]{1,0:T(8,128)(2,1)S(1)}, bf16[896,256]{1,0:T(8,128)(2,1)S(1)}, u32[]{:S(2)}, u32[]{:S(2)}) %collective-permute-start.12) | collective-permute-done | bytes 458784 | tf_op jit(solution)/shard_map/ppermute | solution.py:33
  391.8 5.2 %fusion.5 = f32[512,896,1]{1,0,2:T(8,128)S(1)} fusion(bf16[8,896,256]{2,1,0:T(8,128)(2,1)} %all-to-all-done, bf16[512,1,8,256]{3,2,1,0:T(8,128)(2,1)} %get-tuple-element.143), kind=kOutput, calls=%fused_computation.18 | convolution fusion | flops 1879048192 | bytes 7602176 | tf_op jit(solution)/shard_map/tsd,sfd->tf/dot_general | solution.py:59
  397.0 4.2 %multiply_convert_fusion = (bf16[512,896]{1,0:T(8,128)(2,1)}, bf16[512,896]{1,0:T(8,128)(2,1)}) fusion(bf16[512,896]{1,0:T(8,128)(2,1)S(1)} %copy-done.8, bf16[512,896]{1,0:T(8,128)(2,1)S(1)} %copy-done.10, bf16[8,896,256]{2,1,0:T(8,128)(2,1)S(1)} %copy-done.5, bf16[8,512,256]{2,1,0:T(8,128)(2,1)S(1)} %copy-done.3, f32[512,896,1]{1,0,2:T(8,128)S(1)} %fusion.5), kind=kOutput, calls=%fused_computation.31 | convolution fusion | flops 1886388224 | bytes 11272192 | tf_op jit(solution)/shard_map/tsd,sfd->tf/dot_general | solution.py:61
  401.2 7.4 %fusion = f32[4,896,256]{2,0,1:T(4,128)S(1)} fusion(bf16[896,16,256]{2,0,1:T(8,128)(2,1)} %all-to-all-done.1, s32[16]{0:T(128)S(1)} %copy-done.6), kind=kOutput, calls=%fused_computation.5 | convolution fusion | flops 29360192 | bytes 11010112 | tf_op jit(solution)/shard_map/lg,fgd->lfd/dot_general | solution.py:77
  408.6 2.5 copy.22
  (63 shorter events, 25.1 us)
Async XLA Ops:
  0.6 15.3 %collective-permute-start = (bf16[32,4096]{1,0:T(8,128)(2,1)}, bf16[32,4096]{1,0:T(8,128)(2,1)S(1)}, u32[]{:S(2)}, u32[]{:S(2)}) collective-permute-start(bf16[32,4096]{1,0:T(8,128)(2,1)} %param.5), channel_id=1, source_target_pairs={{0,8},{8,0},{1,9},{9,1},{2,10},{10,2},{3,11},{11,3},{4,12},{12,4},... | collective-permute-start | bytes 786440 | tf_op jit(solution)/shard_map/ppermute | solution.py:19
  7.0 17.5 %copy-start.4 = (bf16[32,4096]{1,0:T(8,128)(2,1)S(1)}, bf16[32,4096]{1,0:T(8,128)(2,1)}, u32[]{:S(2)}) copy-start(bf16[32,4096]{1,0:T(8,128)(2,1)} %param.5) | copy-start | bytes 786436
  15.9 55.0 %all-to-all-start = ((bf16[8,896,256]{2,1,0:T(8,128)(2,1)}), bf16[8,896,256]{2,1,0:T(8,128)(2,1)}, u32[]{:S(2)}, u32[]{:S(2)}) async-start(bf16[8,896,256]{2,1,0:T(8,128)(2,1)} %gather_fusion), calls=%async_computation | async-start | bytes 7340032 | tf_op jit(solution)/shard_map/all_to_all | solution.py:26
  24.6 15.0 %collective-permute-start.1 = (bf16[2,32,4096]{2,1,0:T(8,128)(2,1)S(1)}, bf16[2,32,4096]{2,1,0:T(8,128)(2,1)S(1)}, u32[]{:S(2)}, u32[]{:S(2)}) collective-permute-start(bf16[2,32,4096]{2,1,0:T(8,128)(2,1)S(1)} %maximum_select_fusion.2), channel_id=1, source_target_pairs={{0,2},{2,4},{4,6},{6,0},{1,3},{3,5},{5,7},{7,1},{8,10},{10,12},{12... | collective-permute-start | bytes 1572872 | tf_op jit(solution)/shard_map/ppermute | solution.py:42
  26.3 24.8 %collective-permute-start.2 = (bf16[2,32,4096]{2,1,0:T(8,128)(2,1)S(1)}, bf16[2,32,4096]{2,1,0:T(8,128)(2,1)S(1)}, u32[]{:S(2)}, u32[]{:S(2)}) collective-permute-start(bf16[2,32,4096]{2,1,0:T(8,128)(2,1)S(1)} %maximum_select_fusion.2), channel_id=1, source_target_pairs={{0,4},{2,6},{4,0},{6,2},{1,5},{3,7},{5,1},{7,3},{8,12},{10,14},{12... | collective-permute-start | bytes 1572872 | tf_op jit(solution)/shard_map/ppermute | solution.py:42
  29.2 21.9 %collective-permute-start.3 = (bf16[2,32,4096]{2,1,0:T(8,128)(2,1)S(1)}, bf16[2,32,4096]{2,1,0:T(8,128)(2,1)S(1)}, u32[]{:S(2)}, u32[]{:S(2)}) collective-permute-start(bf16[2,32,4096]{2,1,0:T(8,128)(2,1)S(1)} %maximum_select_fusion.2), channel_id=1, source_target_pairs={{0,6},{2,0},{4,2},{6,4},{1,7},{3,1},{5,3},{7,5},{8,14},{10,8},{12,... | collective-permute-start | bytes 1572872 | tf_op jit(solution)/shard_map/ppermute | solution.py:42
  53.3 4.4 %collective-permute-start.4 = (bf16[4,2,32,4096]{3,2,1,0:T(8,128)(2,1)}, bf16[4,2,32,4096]{3,2,1,0:T(8,128)(2,1)S(1)}, u32[]{:S(2)}, u32[]{:S(2)}) collective-permute-start(bf16[4,2,32,4096]{3,2,1,0:T(8,128)(2,1)} %gather_fusion.1), channel_id=1, source_target_pairs={{0,1},{1,0},{2,3},{3,2},{4,5},{5,4},{6,7},{7,6},{8,9},{9,8},{10,11... | collective-permute-start | bytes 6291464 | tf_op jit(solution)/shard_map/ppermute | solution.py:46
  60.9 6.3 %copy-start = (bf16[2,4,2,32,4096]{4,3,2,1,0:T(8,128)(2,1)}, bf16[2,4,2,32,4096]{4,3,2,1,0:T(8,128)(2,1)S(1)}, u32[]{:S(2)}) copy-start(bf16[2,4,2,32,4096]{4,3,2,1,0:T(8,128)(2,1)S(1)} %copy.16) | copy-start | bytes 12582916
  70.9 7.7 %copy-start.2 = (bf16[4,896,256]{2,1,0:T(8,128)(2,1)S(1)}, bf16[4,896,256]{2,1,0:T(8,128)(2,1)}, u32[]{:S(2)}) copy-start(bf16[4,896,256]{2,1,0:T(8,128)(2,1)} %param.8) | copy-start | bytes 5505028
  70.9 330.3 %all-to-all-start.1 = ((bf16[896,16,256]{2,0,1:T(8,128)(2,1)}), bf16[896,16,256]{2,0,1:T(8,128)(2,1)}, u32[]{:S(2)}, u32[]{:S(2)}) async-start(bf16[896,16,256]{2,0,1:T(8,128)(2,1)} %bitcast.76), calls=%async_computation.1 | async-start | bytes 14680064 | tf_op jit(solution)/shard_map/all_to_all | solution.py:70
  78.6 237.3 %collective-permute-start.5 = (bf16[4,896,256]{2,1,0:T(8,128)(2,1)S(1)}, bf16[4,896,256]{2,1,0:T(8,128)(2,1)}, u32[]{:S(2)}, u32[]{:S(2)}) collective-permute-start(bf16[4,896,256]{2,1,0:T(8,128)(2,1)S(1)} %copy-done.2), channel_id=1, source_target_pairs={{0,128},{128,0},{1,129},{129,1},{2,130},{130,2},{3,131},{131,3},{4... | collective-permute-start | bytes 5505032 | tf_op jit(solution)/shard_map/ppermute | solution.py:27
  323.0 20.1 %collective-permute-start.6 = (bf16[896,256]{1,0:T(8,128)(2,1)S(1)}, bf16[896,256]{1,0:T(8,128)(2,1)}, u32[]{:S(2)}, u32[]{:S(2)}) collective-permute-start(bf16[896,256]{1,0:T(8,128)(2,1)S(1)} %get-tuple-element.150), channel_id=1, source_target_pairs={{0,16},{16,32},{32,48},{48,64},{64,80},{80,96},{96,112},{112,0},{1... | collective-permute-start | bytes 1376264 | tf_op jit(solution)/shard_map/ppermute | solution.py:33
  324.1 46.6 %collective-permute-start.7 = (bf16[896,256]{1,0:T(8,128)(2,1)S(1)}, bf16[896,256]{1,0:T(8,128)(2,1)S(1)}, u32[]{:S(2)}, u32[]{:S(2)}) collective-permute-start(bf16[896,256]{1,0:T(8,128)(2,1)S(1)} %get-tuple-element.149), channel_id=1, source_target_pairs={{0,32},{16,48},{32,64},{48,80},{64,96},{80,112},{96,0},{112,16},{1... | collective-permute-start | bytes 1376264 | tf_op jit(solution)/shard_map/ppermute | solution.py:33
  324.2 47.3 %collective-permute-start.8 = (bf16[896,256]{1,0:T(8,128)(2,1)S(1)}, bf16[896,256]{1,0:T(8,128)(2,1)S(1)}, u32[]{:S(2)}, u32[]{:S(2)}) collective-permute-start(bf16[896,256]{1,0:T(8,128)(2,1)S(1)} %get-tuple-element.148), channel_id=1, source_target_pairs={{0,48},{16,64},{32,80},{48,96},{64,112},{80,0},{96,16},{112,32},{1... | collective-permute-start | bytes 1376264 | tf_op jit(solution)/shard_map/ppermute | solution.py:33
  327.2 45.1 %collective-permute-start.9 = (bf16[896,256]{1,0:T(8,128)(2,1)S(1)}, bf16[896,256]{1,0:T(8,128)(2,1)S(1)}, u32[]{:S(2)}, u32[]{:S(2)}) collective-permute-start(bf16[896,256]{1,0:T(8,128)(2,1)S(1)} %get-tuple-element.147), channel_id=1, source_target_pairs={{0,64},{16,80},{32,96},{48,112},{64,0},{80,16},{96,32},{112,48},{1... | collective-permute-start | bytes 1376264 | tf_op jit(solution)/shard_map/ppermute | solution.py:33
  327.2 46.5 %collective-permute-start.10 = (bf16[896,256]{1,0:T(8,128)(2,1)S(1)}, bf16[896,256]{1,0:T(8,128)(2,1)S(1)}, u32[]{:S(2)}, u32[]{:S(2)}) collective-permute-start(bf16[896,256]{1,0:T(8,128)(2,1)S(1)} %get-tuple-element.146), channel_id=1, source_target_pairs={{0,80},{16,96},{32,112},{48,0},{64,16},{80,32},{96,48},{112,64},{1... | collective-permute-start | bytes 1376264 | tf_op jit(solution)/shard_map/ppermute | solution.py:33
  343.1 31.4 %collective-permute-start.11 = (bf16[896,256]{1,0:T(8,128)(2,1)S(1)}, bf16[896,256]{1,0:T(8,128)(2,1)S(1)}, u32[]{:S(2)}, u32[]{:S(2)}) collective-permute-start(bf16[896,256]{1,0:T(8,128)(2,1)S(1)} %get-tuple-element.145), channel_id=1, source_target_pairs={{0,96},{16,112},{32,0},{48,16},{64,32},{80,48},{96,64},{112,80},{1... | collective-permute-start | bytes 1376264 | tf_op jit(solution)/shard_map/ppermute | solution.py:33
  370.7 14.8 %collective-permute-start.12 = (bf16[896,256]{1,0:T(8,128)(2,1)S(1)}, bf16[896,256]{1,0:T(8,128)(2,1)S(1)}, u32[]{:S(2)}, u32[]{:S(2)}) collective-permute-start(bf16[896,256]{1,0:T(8,128)(2,1)S(1)} %get-tuple-element.144), channel_id=1, source_target_pairs={{0,112},{16,0},{32,16},{48,32},{64,48},{80,64},{96,80},{112,96},{1... | collective-permute-start | bytes 1376264 | tf_op jit(solution)/shard_map/ppermute | solution.py:33
  371.5 14.8 %copy-start.1 = (bf16[2,4,2,32,4096]{4,3,2,1,0:T(8,128)(2,1)S(1)}, bf16[2,4,2,32,4096]{4,3,2,1,0:T(8,128)(2,1)}, u32[]{:S(2)}) copy-start(bf16[2,4,2,32,4096]{4,3,2,1,0:T(8,128)(2,1)} %copy-done) | copy-start | bytes 12582916
  391.7 5.2 %copy-start.3 = (bf16[8,512,256]{2,1,0:T(8,128)(2,1)S(1)}, bf16[8,512,256]{2,1,0:T(8,128)(2,1)}, u32[]{:S(2)}) copy-start(bf16[8,512,256]{2,1,0:T(8,128)(2,1)} %gather_fusion.2) | copy-start | bytes 6291460
  391.8 5.2 %copy-start.5 = (bf16[8,896,256]{2,1,0:T(8,128)(2,1)S(1)}, bf16[8,896,256]{2,1,0:T(8,128)(2,1)}, u32[]{:S(2)}) copy-start(bf16[8,896,256]{2,1,0:T(8,128)(2,1)} %bitcast_dynamic-update-slice_fusion) | copy-start | bytes 11010052
  391.8 5.2 %copy-start.8 = (bf16[512,896]{1,0:T(8,128)(2,1)S(1)}, bf16[512,896]{1,0:T(8,128)(2,1)}, u32[]{:S(2)}) copy-start(bf16[512,896]{1,0:T(8,128)(2,1)} %param.6) | copy-start | bytes 2752516
  391.8 5.2 %copy-start.10 = (bf16[512,896]{1,0:T(8,128)(2,1)S(1)}, bf16[512,896]{1,0:T(8,128)(2,1)}, u32[]{:S(2)}) copy-start(bf16[512,896]{1,0:T(8,128)(2,1)} %param.7) | copy-start | bytes 2752516
  397.0 4.2 %copy-start.6 = (s32[16]{0:T(128)S(1)}, s32[16]{0:T(128)}, u32[]{:S(2)}) copy-start(s32[16]{0:T(128)} %param.9) | copy-start | bytes 196
  (2 other events, 3.2 us)

commit v7 on v4

--- a/solution.py
+++ b/solution.py
@@ -1,12 +1,42 @@
 import jax
 import jax.numpy as jnp
 from jax import lax
+from jax.experimental import pallas as pl
+from jax.experimental.pallas import tpu as pltpu
 from jax.sharding import Mesh
 from jax.sharding import PartitionSpec as P
 
 DP = ("zh2", "zl2", "x")
 HALF = ("zl2", "x")
 TP = ("zh", "y", "c")
+
+
+def _combine_kernel(lang_ref, x_ref, o_ref):
+    o_ref[...] = jnp.zeros_like(o_ref)
+    top = o_ref.shape[0] - 1
+    for g in range(x_ref.shape[0]):
+        lang = jnp.minimum(jnp.maximum(lang_ref[g], 0), top)
+        o_ref[lang] += x_ref[g].astype(jnp.float32)
+
+
+def combine(language, pieces, variants):
+    groups, ff_dev, feat_dev = pieces.shape
+    tile = 128
+    return pl.pallas_call(
+        _combine_kernel,
+        out_shape=jax.ShapeDtypeStruct((variants, ff_dev, feat_dev), jnp.float32),
+        grid_spec=pltpu.PrefetchScalarGridSpec(
+            num_scalar_prefetch=1,
+            grid=(ff_dev // tile,),
+            in_specs=[pl.BlockSpec((groups, tile, feat_dev), lambda i, lang: (0, i, 0))],
+            out_specs=pl.BlockSpec((variants, tile, feat_dev), lambda i, lang: (0, i, 0)),
+        ),
+        cost_estimate=pl.CostEstimate(
+            flops=groups * ff_dev * feat_dev,
+            transcendentals=0,
+            bytes_accessed=pieces.size * 2 + variants * ff_dev * feat_dev * 4,
+        ),
+    )(language, pieces)
 
 
 def shards(cotangent, gate, up, w_down, language):
@@ -54,20 +84,12 @@
     ) + jnp.einsum("tsd,sfd->tf", cot_far, far, preferred_element_type=jnp.float32)
     d_up = (d_hidden * act).astype(jnp.bfloat16)
     d_gate = (d_hidden * up_f * sig * (1.0 + gate_f * (1.0 - sig))).astype(jnp.bfloat16)
-    selector = (language[None, :] == jnp.arange(variants, dtype=jnp.int32)[:, None]).astype(
-        jnp.bfloat16
-    )
     partial_term = lax.dot_general(
         hidden, out_rows, (((0,), (0,)), ((), ())), preferred_element_type=jnp.float32
     ).astype(jnp.bfloat16)
-    pieces = lax.all_to_all(
-        partial_term.reshape(ff_dev, groups, feat_dev),
-        DP,
-        split_axis=1,
-        concat_axis=1,
-        tiled=True,
-    )
-    d_weight = jnp.einsum("lg,fgd->lfd", selector, pieces, preferred_element_type=jnp.float32)
+    pieces = jnp.transpose(partial_term.reshape(ff_dev, groups, feat_dev), (1, 0, 2))
+    pieces = lax.all_to_all(pieces, DP, split_axis=0, concat_axis=0, tiled=True)
+    d_weight = combine(language, pieces, variants)
     return (d_gate, d_up, d_weight)
 
 

time: 340 us -> 359 us (1.056)
  local copies, waits for them, and re-layouts: 23.1 us -> 39 us
  Pallas kernels: 0 us -> 8.43 us
  matrix products: 22.6 us -> 17 us
    convert_element_type x0 -> x1, local copies, waits for them, and re-layouts: none -> 10.8 us  [shards(): partial_term = lax.dot_general(hidden, out_rows, (((0,), (0,)), ((), ()))...]
    pallas_call x0 -> x1, Pallas kernels: none -> 8.43 us  [combine(): pl.pallas_call(_combine_kernel, out_shape=jax.ShapeDtypeStruct((variants,...]
    reshape x1, local copies, waits for them, and re-layouts: 3.74 us -> 11.1 us  [shards(): partial_term.reshape(ff_dev, groups, feat_dev)]
    dot_general x1 -> x0, matrix products: 7.39 us -> none  [shards(): jnp.einsum('lg,fgd->lfd', selector, pieces, preferred_element_type=jnp.fl...]
    unnamed x14 -> x11, local copies, waits for them, and re-layouts: 7.86 us -> 5.57 us
  transfers between devices with their start and end apart: 9 -> 9, of which waited for: 6 -> 6; matrix products, arithmetic and copies ran while one was open for 11% -> 16% of each run, Pallas kernels for 0% -> 0%
where the time goes in v7:
time: 359 us; the launch traced here: 356 us
  waiting for transfers between devices  257 us (72%)
  local copies, waits for them, and re-layouts  39 us (11%)
  starting transfers between devices  29.3 us (8%)
  matrix products  17 us (5%)
  Pallas kernels  8.43 us (2%)
  other arithmetic  3.99 us (1%)
    all_to_all x1, waiting for transfers between devices, shards(): pieces = lax.all_to_all(pieces, DP, split_axis=0, concat_axis=0, tiled=True)  144 us
    ppermute x1, waiting for transfers between devices, shards(): block = lax.ppermute(w_down, 'zh2', [(0, 1), (1, 0)])  79.3 us
    ppermute x3, waiting for transfers between devices, shards(): lax.ppermute(pair, 'y', [(i, (i + shift) % ring) for i in range(ring)])  20.5 us
    reshape x1, local copies, waits for them, and re-layouts, shards(): partial_term.reshape(ff_dev, groups, feat_dev)  11.1 us
    convert_element_type x1, local copies, waits for them, and re-layouts, shards(): partial_term = lax.dot_general(hidden, out_rows, (((0,), (0,)), ((), ()))...  10.8 us
    ppermute x1, waiting for transfers between devices, shards(): partner = lax.ppermute(cotangent, 'zh', [(0, 1), (1, 0)])  8.94 us
    pallas_call x1, Pallas kernels, combine(): pl.pallas_call(_combine_kernel, out_shape=jax.ShapeDtypeStruct((variants,...  8.43 us
    all_to_all x1, starting transfers between devices, shards(): lax.all_to_all(own_slabs, HALF, split_axis=0, concat_axis=0, tiled=True)  7.85 us
  transfers between devices with their start and end apart: 9, of which 6 were waited for; matrix products, arithmetic and copies ran while one was open for 16% of the time, Pallas kernels for 0%

profile of v7, /device:TPU:228, one launch (start us, length us, event | category | flops | bytes accessed | tf_op | source)
XLA Modules:
  0.0 355.6 jit_solution(11607385459592978065)
XLA Ops:
  0.6 1.5 collective-permute-start
  2.9 4.1 %gather_fusion = bf16[8,896,256]{2,1,0:T(8,128)(2,1)} fusion(bf16[4,896,256]{2,1,0:T(8,128)(2,1)} %param.8, s32[1024]{0:T(1024)S(1)} %pad_clamp_fusion.1), kind=kCustom, calls=%fused_computation | custom fusion | bytes 7340064 | tf_op jit(solution)/shard_map/jit(_take)/gather | solution.py:54
  7.0 8.9 %collective-permute-done = bf16[32,4096]{1,0:T(8,128)(2,1)S(1)} collective-permute-done((bf16[32,4096]{1,0:T(8,128)(2,1)}, bf16[32,4096]{1,0:T(8,128)(2,1)S(1)}, u32[]{:S(2)}, u32[]{:S(2)}) %collective-permute-start) | collective-permute-done | bytes 262176 | tf_op jit(solution)/shard_map/ppermute | solution.py:49
  15.9 7.8 %all-to-all-start = ((bf16[8,896,256]{2,1,0:T(8,128)(2,1)}), bf16[8,896,256]{2,1,0:T(8,128)(2,1)}, u32[]{:S(2)}, u32[]{:S(2)}) async-start(bf16[8,896,256]{2,1,0:T(8,128)(2,1)} %gather_fusion), calls=%async_computation | async-start | bytes 7340032 | tf_op jit(solution)/shard_map/all_to_all | solution.py:56
  23.8 1.9 collective-permute-start.5
  25.7 79.3 %collective-permute-done.5 = bf16[4,896,256]{2,1,0:T(8,128)(2,1)} collective-permute-done((bf16[4,896,256]{2,1,0:T(8,128)(2,1)S(1)}, bf16[4,896,256]{2,1,0:T(8,128)(2,1)}, u32[]{:S(2)}, u32[]{:S(2)}) %collective-permute-start.5) | collective-permute-done | bytes 1835040 | tf_op jit(solution)/shard_map/ppermute | solution.py:57
  104.9 4.1 %gather_fusion.2 = bf16[8,896,256]{2,1,0:T(8,128)(2,1)} fusion(bf16[4,896,256]{2,1,0:T(8,128)(2,1)} %collective-permute-done.5, s32[1024]{0:T(1024)S(1)} %pad_clamp_fusion.1), kind=kCustom, calls=%fused_computation.2 | custom fusion | bytes 7340064 | tf_op jit(solution)/shard_map/jit(_take)/gather | solution.py:58
  109.0 5.8 %all-to-all-start.1 = ((bf16[8,896,256]{2,1,0:T(8,128)(2,1)}), bf16[8,896,256]{2,1,0:T(8,128)(2,1)}, u32[]{:S(2)}, u32[]{:S(2)}) async-start(bf16[8,896,256]{2,1,0:T(8,128)(2,1)} %gather_fusion.2), calls=%async_computation.1 | async-start | bytes 7340032 | tf_op jit(solution)/shard_map/all_to_all | solution.py:59
  115.7 3.1 collective-permute-start.3
  120.5 16.8 %collective-permute-done.3 = bf16[2,32,4096]{2,1,0:T(8,128)(2,1)S(1)} collective-permute-done((bf16[2,32,4096]{2,1,0:T(8,128)(2,1)S(1)}, bf16[2,32,4096]{2,1,0:T(8,128)(2,1)S(1)}, u32[]{:S(2)}, u32[]{:S(2)}) %collective-permute-start.3) | collective-permute-done | bytes 524320 | tf_op jit(solution)/shard_map/ppermute | solution.py:66
  137.3 3.7 %collective-permute-done.1 = bf16[2,32,4096]{2,1,0:T(8,128)(2,1)S(1)} collective-permute-done((bf16[2,32,4096]{2,1,0:T(8,128)(2,1)S(1)}, bf16[2,32,4096]{2,1,0:T(8,128)(2,1)S(1)}, u32[]{:S(2)}, u32[]{:S(2)}) %collective-permute-start.1) | collective-permute-done | bytes 524320 | tf_op jit(solution)/shard_map/ppermute | solution.py:66
  141.3 2.0 gather_fusion.1
  143.3 4.4 %collective-permute-done.4 = bf16[4,2,32,4096]{3,2,1,0:T(8,128)(2,1)S(1)} collective-permute-done((bf16[4,2,32,4096]{3,2,1,0:T(8,128)(2,1)}, bf16[4,2,32,4096]{3,2,1,0:T(8,128)(2,1)S(1)}, u32[]{:S(2)}, u32[]{:S(2)}) %collective-permute-start.4) | collective-permute-done | bytes 2097184 | tf_op jit(solution)/shard_map/ppermute | solution.py:70
  147.6 2.8 fusion
  150.8 2.0 copy-done
  152.7 6.3 %convolution_convert_fusion = bf16[896,4096]{1,0:T(8,128)(2,1)} fusion(bf16[512,4096]{1,0:T(8,128)(2,1)S(1)} %bitcast.40, bf16[512,896]{1,0:T(8,128)(2,1)S(1)} %copy-done.4, bf16[512,896]{1,0:T(8,128)(2,1)S(1)} %copy-done.3), kind=kOutput, calls=%fused_computation.3 | convolution fusion | flops 3765436416 | bytes 13369344 | tf_op jit(solution)/shard_map/dot_general | solution.py:87
  159.0 10.8 %copy.16 = bf16[896,4096]{0,1:T(8,128)(2,1)} copy(bf16[896,4096]{1,0:T(8,128)(2,1)} %convolution_convert_fusion) | data formatting | bytes 14680064 | tf_op jit(solution)/shard_map/convert_element_type | solution.py:89
  169.8 11.1 %copy.17 = bf16[896,16,256]{2,0,1:T(8,128)(2,1)} copy(bf16[896,16,256]{0,2,1:T(8,128)(2,1)} %bitcast.39) | data formatting | bytes 14680064 | tf_op jit(solution)/shard_map/reshape | solution.py:90
  180.9 7.5 %all-to-all-start.2 = ((bf16[16,896,256]{2,1,0:T(8,128)(2,1)}), bf16[16,896,256]{2,1,0:T(8,128)(2,1)}, u32[]{:S(2)}, u32[]{:S(2)}) async-start(bf16[16,896,256]{2,1,0:T(8,128)(2,1)} %bitcast.38), calls=%async_computation.2 | async-start | bytes 14680064 | tf_op jit(solution)/shard_map/all_to_all | solution.py:91
  188.5 3.6 %copy.18 = bf16[64,8,16,256]{3,2,1,0:T(8,128)(2,1)S(1)} copy(bf16[64,8,16,256]{3,1,2,0:T(8,128)(2,1)} %bitcast.41) | data formatting | bytes 8388608
  192.4 4.4 %fusion.3 = f32[512,896,1]{1,0,2:T(8,128)S(1)} fusion(bf16[8,896,256]{2,1,0:T(8,128)(2,1)} %all-to-all-done, bf16[512,1,8,256]{3,2,1,0:T(8,128)(2,1)S(1)} %get-tuple-element.43), kind=kOutput, calls=%fused_computation.14 | convolution fusion | flops 1879048192 | bytes 7602176 | tf_op jit(solution)/shard_map/tsd,sfd->tf/dot_general | solution.py:82
  196.8 6.3 %multiply_convert_fusion = (bf16[512,896]{1,0:T(8,128)(2,1)}, bf16[512,896]{1,0:T(8,128)(2,1)}) fusion(bf16[512,896]{1,0:T(8,128)(2,1)S(1)} %copy-done.3, bf16[512,896]{1,0:T(8,128)(2,1)S(1)} %copy-done.4, bf16[8,896,256]{2,1,0:T(8,128)(2,1)} %all-to-all-done.1, bf16[512,1,8,256]{3,2,1,0:T(8,128)(2,1)S(1)} %get-tuple-element.42, f32[512,896,1]{1,0,2:T(8,128)S(1)} %fusion.3), kind=kOutput, calls=%fused_computation.27 | convolution fusion | flops 1886388224 | bytes 11272192 | tf_op jit(solution)/shard_map/tsd,sfd->tf/dot_general | solution.py:84
  203.0 144.1 %all-to-all-done.2.x_ref = bf16[16,896,256]{2,1,0:T(8,128)(2,1)} async-done(((bf16[16,896,256]{2,1,0:T(8,128)(2,1)}), bf16[16,896,256]{2,1,0:T(8,128)(2,1)}, u32[]{:S(2)}, u32[]{:S(2)}) %all-to-all-start.2) | async-done | bytes 7340064 | tf_op jit(solution)/shard_map/all_to_all | solution.py:91
  347.1 8.4 %shard_map.76 = f32[4,896,256]{2,1,0:T(8,128)} custom-call(s32[16]{0:T(128)} %lang_ref.1, bf16[16,896,256]{2,1,0:T(8,128)(2,1)} %all-to-all-done.2.x_ref), custom_call_target="tpu_custom_call" | custom-call | flops 3670016 | bytes 11010048 | tf_op jit(solution)/shard_map/pallas_call | solution.py:25
  (27 shorter events, 4.1 us)
Async XLA Ops:
  0.6 15.3 %collective-permute-start = (bf16[32,4096]{1,0:T(8,128)(2,1)}, bf16[32,4096]{1,0:T(8,128)(2,1)S(1)}, u32[]{:S(2)}, u32[]{:S(2)}) collective-permute-start(bf16[32,4096]{1,0:T(8,128)(2,1)} %param.5), channel_id=1, source_target_pairs={{0,8},{8,0},{1,9},{9,1},{2,10},{10,2},{3,11},{11,3},{4,12},{12,4},... | collective-permute-start | bytes 786440 | tf_op jit(solution)/shard_map/ppermute | solution.py:49
  7.0 16.8 %copy-start.1 = (bf16[4,896,256]{2,1,0:T(8,128)(2,1)S(1)}, bf16[4,896,256]{2,1,0:T(8,128)(2,1)}, u32[]{:S(2)}) copy-start(bf16[4,896,256]{2,1,0:T(8,128)(2,1)} %param.8) | copy-start | bytes 5505028
  15.9 93.1 %all-to-all-start = ((bf16[8,896,256]{2,1,0:T(8,128)(2,1)}), bf16[8,896,256]{2,1,0:T(8,128)(2,1)}, u32[]{:S(2)}, u32[]{:S(2)}) async-start(bf16[8,896,256]{2,1,0:T(8,128)(2,1)} %gather_fusion), calls=%async_computation | async-start | bytes 7340032 | tf_op jit(solution)/shard_map/all_to_all | solution.py:56
  23.8 81.1 %collective-permute-start.5 = (bf16[4,896,256]{2,1,0:T(8,128)(2,1)S(1)}, bf16[4,896,256]{2,1,0:T(8,128)(2,1)}, u32[]{:S(2)}, u32[]{:S(2)}) collective-permute-start(bf16[4,896,256]{2,1,0:T(8,128)(2,1)S(1)} %copy-done.1), channel_id=1, source_target_pairs={{0,128},{128,0},{1,129},{129,1},{2,130},{130,2},{3,131},{131,3},{4... | collective-permute-start | bytes 5505032 | tf_op jit(solution)/shard_map/ppermute | solution.py:57
  109.0 6.6 %copy-start.2 = (bf16[32,4096]{1,0:T(8,128)(2,1)S(1)}, bf16[32,4096]{1,0:T(8,128)(2,1)}, u32[]{:S(2)}) copy-start(bf16[32,4096]{1,0:T(8,128)(2,1)} %param.5) | copy-start | bytes 786436
  109.0 71.9 %all-to-all-start.1 = ((bf16[8,896,256]{2,1,0:T(8,128)(2,1)}), bf16[8,896,256]{2,1,0:T(8,128)(2,1)}, u32[]{:S(2)}, u32[]{:S(2)}) async-start(bf16[8,896,256]{2,1,0:T(8,128)(2,1)} %gather_fusion.2), calls=%async_computation.1 | async-start | bytes 7340032 | tf_op jit(solution)/shard_map/all_to_all | solution.py:59
  115.7 21.6 %collective-permute-start.3 = (bf16[2,32,4096]{2,1,0:T(8,128)(2,1)S(1)}, bf16[2,32,4096]{2,1,0:T(8,128)(2,1)S(1)}, u32[]{:S(2)}, u32[]{:S(2)}) collective-permute-start(bf16[2,32,4096]{2,1,0:T(8,128)(2,1)S(1)} %maximum_select_fusion.2), channel_id=1, source_target_pairs={{0,6},{2,0},{4,2},{6,4},{1,7},{3,1},{5,3},{7,5},{8,14},{10,8},{12,... | collective-permute-start | bytes 1572872 | tf_op jit(solution)/shard_map/ppermute | solution.py:66
  118.8 18.5 %collective-permute-start.2 = (bf16[2,32,4096]{2,1,0:T(8,128)(2,1)S(1)}, bf16[2,32,4096]{2,1,0:T(8,128)(2,1)S(1)}, u32[]{:S(2)}, u32[]{:S(2)}) collective-permute-start(bf16[2,32,4096]{2,1,0:T(8,128)(2,1)S(1)} %maximum_select_fusion.2), channel_id=1, source_target_pairs={{0,4},{2,6},{4,0},{6,2},{1,5},{3,7},{5,1},{7,3},{8,12},{10,14},{12... | collective-permute-start | bytes 1572872 | tf_op jit(solution)/shard_map/ppermute | solution.py:66
  119.4 21.6 %collective-permute-start.1 = (bf16[2,32,4096]{2,1,0:T(8,128)(2,1)S(1)}, bf16[2,32,4096]{2,1,0:T(8,128)(2,1)S(1)}, u32[]{:S(2)}, u32[]{:S(2)}) collective-permute-start(bf16[2,32,4096]{2,1,0:T(8,128)(2,1)S(1)} %maximum_select_fusion.2), channel_id=1, source_target_pairs={{0,2},{2,4},{4,6},{6,0},{1,3},{3,5},{5,7},{7,1},{8,10},{10,12},{12... | collective-permute-start | bytes 1572872 | tf_op jit(solution)/shard_map/ppermute | solution.py:66
  143.3 4.4 %collective-permute-start.4 = (bf16[4,2,32,4096]{3,2,1,0:T(8,128)(2,1)}, bf16[4,2,32,4096]{3,2,1,0:T(8,128)(2,1)S(1)}, u32[]{:S(2)}, u32[]{:S(2)}) collective-permute-start(bf16[4,2,32,4096]{3,2,1,0:T(8,128)(2,1)} %gather_fusion.1), channel_id=1, source_target_pairs={{0,1},{1,0},{2,3},{3,2},{4,5},{5,4},{6,7},{7,6},{8,9},{9,8},{10,11... | collective-permute-start | bytes 6291464 | tf_op jit(solution)/shard_map/ppermute | solution.py:70
  150.5 2.3 copy-start.3
  150.5 2.3 copy-start.4
  150.8 2.0 copy-start
  180.9 166.2 %all-to-all-start.2 = ((bf16[16,896,256]{2,1,0:T(8,128)(2,1)}), bf16[16,896,256]{2,1,0:T(8,128)(2,1)}, u32[]{:S(2)}, u32[]{:S(2)}) async-start(bf16[16,896,256]{2,1,0:T(8,128)(2,1)} %bitcast.38), calls=%async_computation.2 | async-start | bytes 14680064 | tf_op jit(solution)/shard_map/all_to_all | solution.py:91

commit v8 on v4

--- a/solution.py
+++ b/solution.py
@@ -22,7 +22,6 @@
     lang = language.reshape(2, half)
     own_langs = jnp.take(lang, side, axis=0, mode="clip")
     own_slabs = jnp.take(w_down, own_langs, axis=0, mode="clip")
-    partner, own_slabs = lax.optimization_barrier((partner, own_slabs))
     near = lax.all_to_all(own_slabs, HALF, split_axis=0, concat_axis=0, tiled=True)
     block = lax.ppermute(w_down, "zh2", [(0, 1), (1, 0)])
     relay = jnp.take(block, own_langs, axis=0, mode="clip")

time: 340 us -> 378 us (1.11)
  waiting for transfers between devices: 257 us -> 291 us
    ppermute x1, waiting for transfers between devices: 8.94 us -> 46.1 us  [shards(): partner = lax.ppermute(cotangent, 'zh', [(0, 1), (1, 0)])]
    ppermute x3, waiting for transfers between devices: 20.5 us -> 16.7 us  [shards(): lax.ppermute(pair, 'y', [(i, (i + shift) % ring) for i in range(ring)])]
  transfers between devices with their start and end apart: 9 -> 9, of which waited for: 6 -> 6; matrix products, arithmetic and copies ran while one was open for 11% -> 9% of each run, Pallas kernels for 0% -> 0%
where the time goes in v8:
time: 378 us; the launch traced here: 372 us
  waiting for transfers between devices  291 us (77%)
  starting transfers between devices  30.1 us (8%)
  local copies, waits for them, and re-layouts  23.1 us (6%)
  matrix products  22.6 us (6%)
  other arithmetic  4.01 us (1%)
    all_to_all x1, waiting for transfers between devices, shards(): lax.all_to_all(partial_term.reshape(ff_dev, groups, feat_dev), DP, split_...  144 us
    ppermute x1, waiting for transfers between devices, shards(): block = lax.ppermute(w_down, 'zh2', [(0, 1), (1, 0)])  80.1 us
    ppermute x1, waiting for transfers between devices, shards(): partner = lax.ppermute(cotangent, 'zh', [(0, 1), (1, 0)])  46.1 us
    ppermute x3, waiting for transfers between devices, shards(): lax.ppermute(pair, 'y', [(i, (i + shift) % ring) for i in range(ring)])  16.7 us
    all_to_all x1, starting transfers between devices, shards(): lax.all_to_all(partial_term.reshape(ff_dev, groups, feat_dev), DP, split_...  9.66 us
    unnamed x14, local copies, waits for them, and re-layouts  7.86 us
  transfers between devices with their start and end apart: 9, of which 6 were waited for; matrix products, arithmetic and copies ran while one was open for 9% of the time, Pallas kernels for 0%

profile of v8, /device:TPU:228, one launch (start us, length us, event | category | flops | bytes accessed | tf_op | source)
XLA Modules:
  0.0 371.9 jit_solution(14241853938697057446)
XLA Ops:
  1.4 4.1 %gather_fusion.1 = bf16[8,896,256]{2,1,0:T(8,128)(2,1)} fusion(bf16[4,896,256]{2,1,0:T(8,128)(2,1)} %param.8, s32[1024]{0:T(1024)S(1)} %pad_clamp_fusion), kind=kCustom, calls=%fused_computation.1 | custom fusion | bytes 7340064 | tf_op jit(solution)/shard_map/jit(_take)/gather | solution.py:24
  5.5 5.8 %all-to-all-start = ((bf16[8,896,256]{2,1,0:T(8,128)(2,1)}), bf16[8,896,256]{2,1,0:T(8,128)(2,1)}, u32[]{:S(2)}, u32[]{:S(2)}) async-start(bf16[8,896,256]{2,1,0:T(8,128)(2,1)} %gather_fusion.1), calls=%async_computation | async-start | bytes 7340032 | tf_op jit(solution)/shard_map/all_to_all | solution.py:25
  11.3 1.5 collective-permute-start.5
  12.8 80.1 %collective-permute-done.5 = bf16[4,896,256]{2,1,0:T(8,128)(2,1)} collective-permute-done((bf16[4,896,256]{2,1,0:T(8,128)(2,1)S(1)}, bf16[4,896,256]{2,1,0:T(8,128)(2,1)}, u32[]{:S(2)}, u32[]{:S(2)}) %collective-permute-start.5) | collective-permute-done | bytes 1835040 | tf_op jit(solution)/shard_map/ppermute | solution.py:26
  92.9 4.1 %gather_fusion.2 = bf16[8,896,256]{2,1,0:T(8,128)(2,1)} fusion(bf16[4,896,256]{2,1,0:T(8,128)(2,1)} %collective-permute-done.5, s32[1024]{0:T(1024)S(1)} %pad_clamp_fusion), kind=kCustom, calls=%fused_computation.2 | custom fusion | bytes 7340064 | tf_op jit(solution)/shard_map/jit(_take)/gather | solution.py:27
  97.0 5.8 %all-to-all-start.1 = ((bf16[8,896,256]{2,1,0:T(8,128)(2,1)}), bf16[8,896,256]{2,1,0:T(8,128)(2,1)}, u32[]{:S(2)}, u32[]{:S(2)}) async-start(bf16[8,896,256]{2,1,0:T(8,128)(2,1)} %gather_fusion.2), calls=%async_computation.1 | async-start | bytes 7340032 | tf_op jit(solution)/shard_map/all_to_all | solution.py:28
  102.8 1.4 collective-permute-start
  105.0 46.1 %collective-permute-done = bf16[32,4096]{1,0:T(8,128)(2,1)S(1)} collective-permute-done((bf16[32,4096]{1,0:T(8,128)(2,1)S(1)}, bf16[32,4096]{1,0:T(8,128)(2,1)S(1)}, u32[]{:S(2)}, u32[]{:S(2)}) %collective-permute-start) | collective-permute-done | bytes 262176 | tf_op jit(solution)/shard_map/ppermute | solution.py:19
  151.2 1.7 collective-permute-start.1
  152.8 2.9 collective-permute-start.2
  157.2 9.5 %collective-permute-done.1 = bf16[2,32,4096]{2,1,0:T(8,128)(2,1)S(1)} collective-permute-done((bf16[2,32,4096]{2,1,0:T(8,128)(2,1)S(1)}, bf16[2,32,4096]{2,1,0:T(8,128)(2,1)S(1)}, u32[]{:S(2)}, u32[]{:S(2)}) %collective-permute-start.1) | collective-permute-done | bytes 524320 | tf_op jit(solution)/shard_map/ppermute | solution.py:35
  166.7 7.1 %collective-permute-done.2 = bf16[2,32,4096]{2,1,0:T(8,128)(2,1)S(1)} collective-permute-done((bf16[2,32,4096]{2,1,0:T(8,128)(2,1)S(1)}, bf16[2,32,4096]{2,1,0:T(8,128)(2,1)S(1)}, u32[]{:S(2)}, u32[]{:S(2)}) %collective-permute-start.2) | collective-permute-done | bytes 524320 | tf_op jit(solution)/shard_map/ppermute | solution.py:35
  174.1 2.0 gather_fusion
  176.1 4.4 %collective-permute-done.4 = bf16[4,2,32,4096]{3,2,1,0:T(8,128)(2,1)S(1)} collective-permute-done((bf16[4,2,32,4096]{3,2,1,0:T(8,128)(2,1)}, bf16[4,2,32,4096]{3,2,1,0:T(8,128)(2,1)S(1)}, u32[]{:S(2)}, u32[]{:S(2)}) %collective-permute-start.4) | collective-permute-done | bytes 2097184 | tf_op jit(solution)/shard_map/ppermute | solution.py:39
  180.5 2.8 fusion.2
  185.3 4.5 %convolution_convert_fusion = bf16[896,4096]{1,0:T(8,128)(2,1)S(1)} fusion(bf16[512,4096]{1,0:T(8,128)(2,1)S(1)} %bitcast.44, bf16[512,896]{1,0:T(8,128)(2,1)S(1)} %copy-done.5, bf16[512,896]{1,0:T(8,128)(2,1)S(1)} %copy-done.4), kind=kOutput, calls=%fused_computation.6 | convolution fusion | flops 3765436416 | bytes 13369344 | tf_op jit(solution)/shard_map/dot_general | solution.py:59
  189.9 3.7 %copy.41 = bf16[112,16,8,256]{3,2,0,1:T(8,128)(2,1)} copy(bf16[112,16,8,256]{3,2,1,0:T(8,128)(2,1)S(1)} %bitcast.48) | data formatting | bytes 14680064 | tf_op jit(solution)/shard_map/reshape | solution.py:63
  193.6 9.7 %all-to-all-start.2 = ((bf16[896,16,256]{2,0,1:T(8,128)(2,1)}), bf16[896,16,256]{2,0,1:T(8,128)(2,1)}, u32[]{:S(2)}, u32[]{:S(2)}) async-start(bf16[896,16,256]{2,0,1:T(8,128)(2,1)} %bitcast.43), calls=%async_computation.2 | async-start | bytes 14680064 | tf_op jit(solution)/shard_map/all_to_all | solution.py:62
  203.3 3.6 copy.25
  207.2 4.4 %fusion.5 = f32[512,896,1]{1,0,2:T(8,128)S(1)} fusion(bf16[8,896,256]{2,1,0:T(8,128)(2,1)} %all-to-all-done, bf16[512,1,8,256]{3,2,1,0:T(8,128)(2,1)S(1)} %get-tuple-element.51), kind=kOutput, calls=%fused_computation.17 | convolution fusion | flops 1879048192 | bytes 7602176 | tf_op jit(solution)/shard_map/tsd,sfd->tf/dot_general | solution.py:51
  211.6 6.3 %multiply_convert_fusion = (bf16[512,896]{1,0:T(8,128)(2,1)}, bf16[512,896]{1,0:T(8,128)(2,1)}) fusion(bf16[512,896]{1,0:T(8,128)(2,1)S(1)} %copy-done.4, bf16[512,896]{1,0:T(8,128)(2,1)S(1)} %copy-done.5, bf16[8,896,256]{2,1,0:T(8,128)(2,1)} %all-to-all-done.1, bf16[512,1,8,256]{3,2,1,0:T(8,128)(2,1)S(1)} %get-tuple-element.50, f32[512,896,1]{1,0,2:T(8,128)S(1)} %fusion.5), kind=kOutput, calls=%fused_computation.30 | convolution fusion | flops 1886388224 | bytes 11272192 | tf_op jit(solution)/shard_map/tsd,sfd->tf/dot_general | solution.py:53
  217.9 144.1 %all-to-all-done.2 = bf16[896,16,256]{2,0,1:T(8,128)(2,1)} async-done(((bf16[896,16,256]{2,0,1:T(8,128)(2,1)}), bf16[896,16,256]{2,0,1:T(8,128)(2,1)}, u32[]{:S(2)}, u32[]{:S(2)}) %all-to-all-start.2) | async-done | bytes 7340064 | tf_op jit(solution)/shard_map/all_to_all | solution.py:62
  362.0 7.4 %fusion = f32[4,896,256]{2,0,1:T(4,128)S(1)} fusion(bf16[896,16,256]{2,0,1:T(8,128)(2,1)} %all-to-all-done.2, s32[16]{0:T(128)S(1)} %copy-done.3), kind=kOutput, calls=%fused_computation.4 | convolution fusion | flops 29360192 | bytes 11010112 | tf_op jit(solution)/shard_map/lg,fgd->lfd/dot_general | solution.py:69
  369.4 2.5 copy.23
  (29 shorter events, 5.6 us)
Async XLA Ops:
  5.5 5.8 %copy-start.1 = (bf16[4,896,256]{2,1,0:T(8,128)(2,1)S(1)}, bf16[4,896,256]{2,1,0:T(8,128)(2,1)}, u32[]{:S(2)}) copy-start(bf16[4,896,256]{2,1,0:T(8,128)(2,1)} %param.8) | copy-start | bytes 5505028
  5.5 91.5 %all-to-all-start = ((bf16[8,896,256]{2,1,0:T(8,128)(2,1)}), bf16[8,896,256]{2,1,0:T(8,128)(2,1)}, u32[]{:S(2)}, u32[]{:S(2)}) async-start(bf16[8,896,256]{2,1,0:T(8,128)(2,1)} %gather_fusion.1), calls=%async_computation | async-start | bytes 7340032 | tf_op jit(solution)/shard_map/all_to_all | solution.py:25
  11.3 81.6 %collective-permute-start.5 = (bf16[4,896,256]{2,1,0:T(8,128)(2,1)S(1)}, bf16[4,896,256]{2,1,0:T(8,128)(2,1)}, u32[]{:S(2)}, u32[]{:S(2)}) collective-permute-start(bf16[4,896,256]{2,1,0:T(8,128)(2,1)S(1)} %copy-done.1), channel_id=1, source_target_pairs={{0,128},{128,0},{1,129},{129,1},{2,130},{130,2},{3,131},{131,3},{4... | collective-permute-start | bytes 5505032 | tf_op jit(solution)/shard_map/ppermute | solution.py:26
  97.0 5.8 %copy-start.2 = (bf16[32,4096]{1,0:T(8,128)(2,1)S(1)}, bf16[32,4096]{1,0:T(8,128)(2,1)}, u32[]{:S(2)}) copy-start(bf16[32,4096]{1,0:T(8,128)(2,1)} %param.5) | copy-start | bytes 786436
  97.0 96.6 %all-to-all-start.1 = ((bf16[8,896,256]{2,1,0:T(8,128)(2,1)}), bf16[8,896,256]{2,1,0:T(8,128)(2,1)}, u32[]{:S(2)}, u32[]{:S(2)}) async-start(bf16[8,896,256]{2,1,0:T(8,128)(2,1)} %gather_fusion.2), calls=%async_computation.1 | async-start | bytes 7340032 | tf_op jit(solution)/shard_map/all_to_all | solution.py:28
  102.8 48.3 %collective-permute-start = (bf16[32,4096]{1,0:T(8,128)(2,1)S(1)}, bf16[32,4096]{1,0:T(8,128)(2,1)S(1)}, u32[]{:S(2)}, u32[]{:S(2)}) collective-permute-start(bf16[32,4096]{1,0:T(8,128)(2,1)S(1)} %copy-done.2), channel_id=1, source_target_pairs={{0,8},{8,0},{1,9},{9,1},{2,10},{10,2},{3,11},{11,3},{4,12},{12,4},... | collective-permute-start | bytes 786440 | tf_op jit(solution)/shard_map/ppermute | solution.py:19
  151.2 15.5 %collective-permute-start.1 = (bf16[2,32,4096]{2,1,0:T(8,128)(2,1)S(1)}, bf16[2,32,4096]{2,1,0:T(8,128)(2,1)S(1)}, u32[]{:S(2)}, u32[]{:S(2)}) collective-permute-start(bf16[2,32,4096]{2,1,0:T(8,128)(2,1)S(1)} %maximum_select_fusion.2), channel_id=1, source_target_pairs={{0,2},{2,4},{4,6},{6,0},{1,3},{3,5},{5,7},{7,1},{8,10},{10,12},{12... | collective-permute-start | bytes 1572872 | tf_op jit(solution)/shard_map/ppermute | solution.py:35
  152.8 21.0 %collective-permute-start.2 = (bf16[2,32,4096]{2,1,0:T(8,128)(2,1)S(1)}, bf16[2,32,4096]{2,1,0:T(8,128)(2,1)S(1)}, u32[]{:S(2)}, u32[]{:S(2)}) collective-permute-start(bf16[2,32,4096]{2,1,0:T(8,128)(2,1)S(1)} %maximum_select_fusion.2), channel_id=1, source_target_pairs={{0,4},{2,6},{4,0},{6,2},{1,5},{3,7},{5,1},{7,3},{8,12},{10,14},{12... | collective-permute-start | bytes 1572872 | tf_op jit(solution)/shard_map/ppermute | solution.py:35
  155.7 18.1 %collective-permute-start.3 = (bf16[2,32,4096]{2,1,0:T(8,128)(2,1)S(1)}, bf16[2,32,4096]{2,1,0:T(8,128)(2,1)S(1)}, u32[]{:S(2)}, u32[]{:S(2)}) collective-permute-start(bf16[2,32,4096]{2,1,0:T(8,128)(2,1)S(1)} %maximum_select_fusion.2), channel_id=1, source_target_pairs={{0,6},{2,0},{4,2},{6,4},{1,7},{3,1},{5,3},{7,5},{8,14},{10,8},{12,... | collective-permute-start | bytes 1572872 | tf_op jit(solution)/shard_map/ppermute | solution.py:35
  176.1 4.4 %collective-permute-start.4 = (bf16[4,2,32,4096]{3,2,1,0:T(8,128)(2,1)}, bf16[4,2,32,4096]{3,2,1,0:T(8,128)(2,1)S(1)}, u32[]{:S(2)}, u32[]{:S(2)}) collective-permute-start(bf16[4,2,32,4096]{3,2,1,0:T(8,128)(2,1)} %gather_fusion), channel_id=1, source_target_pairs={{0,1},{1,0},{2,3},{3,2},{4,5},{5,4},{6,7},{7,6},{8,9},{9,8},{10,11... | collective-permute-start | bytes 6291464 | tf_op jit(solution)/shard_map/ppermute | solution.py:39
  183.3 1.2 copy-start.4
  183.3 2.0 copy-start.5
  183.6 6.3 %copy-start = (bf16[2,4,2,32,4096]{4,3,2,1,0:T(8,128)(2,1)}, bf16[2,4,2,32,4096]{4,3,2,1,0:T(8,128)(2,1)S(1)}, u32[]{:S(2)}) copy-start(bf16[2,4,2,32,4096]{4,3,2,1,0:T(8,128)(2,1)S(1)} %copy.17) | copy-start | bytes 12582916
  193.6 168.3 %all-to-all-start.2 = ((bf16[896,16,256]{2,0,1:T(8,128)(2,1)}), bf16[896,16,256]{2,0,1:T(8,128)(2,1)}, u32[]{:S(2)}, u32[]{:S(2)}) async-start(bf16[896,16,256]{2,0,1:T(8,128)(2,1)} %bitcast.43), calls=%async_computation.2 | async-start | bytes 14680064 | tf_op jit(solution)/shard_map/all_to_all | solution.py:62
  211.6 150.4 %copy-start.3 = (s32[16]{0:T(128)S(1)}, s32[16]{0:T(128)}, u32[]{:S(2)}) copy-start(s32[16]{0:T(128)} %param.9) | copy-start | bytes 196

commit v9 on v8

--- a/solution.py
+++ b/solution.py
@@ -24,6 +24,7 @@
     own_slabs = jnp.take(w_down, own_langs, axis=0, mode="clip")
     near = lax.all_to_all(own_slabs, HALF, split_axis=0, concat_axis=0, tiled=True)
     block = lax.ppermute(w_down, "zh2", [(0, 1), (1, 0)])
+    partner, block = lax.optimization_barrier((partner, block))
     relay = jnp.take(block, own_langs, axis=0, mode="clip")
     far = lax.all_to_all(relay, HALF, split_axis=0, concat_axis=0, tiled=True)
     first = lax.axis_index("zh") == 0

time: 378 us -> 342 us (0.905)
  waiting for transfers between devices: 291 us -> 258 us
    ppermute x1, waiting for transfers between devices: 80.1 us -> 1.05 us  [shards(): block = lax.ppermute(w_down, 'zh2', [(0, 1), (1, 0)])]
    ppermute x1, waiting for transfers between devices: 46.1 us -> 90.1 us  [shards(): partner = lax.ppermute(cotangent, 'zh', [(0, 1), (1, 0)])]
  transfers between devices with their start and end apart: 9 -> 9, of which waited for: 6 -> 6; matrix products, arithmetic and copies ran while one was open for 9% -> 10% of each run, Pallas kernels for 0% -> 0%
where the time goes in v9:
time: 342 us; the launch traced here: 335 us
  waiting for transfers between devices  258 us (75%)
  starting transfers between devices  26.6 us (8%)
  local copies, waits for them, and re-layouts  23.1 us (7%)
  matrix products  22.6 us (7%)
  other arithmetic  4.01 us (1%)
    all_to_all x1, waiting for transfers between devices, shards(): lax.all_to_all(partial_term.reshape(ff_dev, groups, feat_dev), DP, split_...  144 us
    ppermute x1, waiting for transfers between devices, shards(): partner = lax.ppermute(cotangent, 'zh', [(0, 1), (1, 0)])  90.1 us
    ppermute x3, waiting for transfers between devices, shards(): lax.ppermute(pair, 'y', [(i, (i + shift) % ring) for i in range(ring)])  18.7 us
    unnamed x14, local copies, waits for them, and re-layouts  7.86 us
    all_to_all x1, starting transfers between devices, shards(): lax.all_to_all(partial_term.reshape(ff_dev, groups, feat_dev), DP, split_...  7.52 us
    dot_general x1, matrix products, shards(): jnp.einsum('lg,fgd->lfd', selector, pieces, preferred_element_type=jnp.fl...  7.39 us
  transfers between devices with their start and end apart: 9, of which 6 were waited for; matrix products, arithmetic and copies ran while one was open for 10% of the time, Pallas kernels for 0%

profile of v9, /device:TPU:228, one launch (start us, length us, event | category | flops | bytes accessed | tf_op | source)
XLA Modules:
  0.0 335.4 jit_solution(929742544070204121)
XLA Ops:
  1.4 4.1 %gather_fusion.1 = bf16[8,896,256]{2,1,0:T(8,128)(2,1)} fusion(bf16[4,896,256]{2,1,0:T(8,128)(2,1)} %param.8, s32[1024]{0:T(1024)S(1)} %pad_clamp_fusion), kind=kCustom, calls=%fused_computation.1 | custom fusion | bytes 7340064 | tf_op jit(solution)/shard_map/jit(_take)/gather | solution.py:24
  5.5 5.8 %all-to-all-start = ((bf16[8,896,256]{2,1,0:T(8,128)(2,1)}), bf16[8,896,256]{2,1,0:T(8,128)(2,1)}, u32[]{:S(2)}, u32[]{:S(2)}) async-start(bf16[8,896,256]{2,1,0:T(8,128)(2,1)} %gather_fusion.1), calls=%async_computation | async-start | bytes 7340032 | tf_op jit(solution)/shard_map/all_to_all | solution.py:25
  11.3 1.5 collective-permute-start.1
  12.9 90.1 %collective-permute-done = bf16[32,4096]{1,0:T(8,128)(2,1)S(1)} collective-permute-done((bf16[32,4096]{1,0:T(8,128)(2,1)S(1)}, bf16[32,4096]{1,0:T(8,128)(2,1)S(1)}, u32[]{:S(2)}, u32[]{:S(2)}) %collective-permute-start) | collective-permute-done | bytes 262176 | tf_op jit(solution)/shard_map/ppermute | solution.py:19
  103.1 1.1 collective-permute-done.1
  104.1 4.1 %gather_fusion.2 = bf16[8,896,256]{2,1,0:T(8,128)(2,1)} fusion(bf16[4,896,256]{2,1,0:T(8,128)(2,1)} %collective-permute-done.1, s32[1024]{0:T(1024)S(1)} %pad_clamp_fusion), kind=kCustom, calls=%fused_computation.2 | custom fusion | bytes 7340064 | tf_op jit(solution)/shard_map/jit(_take)/gather | solution.py:28
  108.2 5.7 %all-to-all-start.1 = ((bf16[8,896,256]{2,1,0:T(8,128)(2,1)}), bf16[8,896,256]{2,1,0:T(8,128)(2,1)}, u32[]{:S(2)}, u32[]{:S(2)}) async-start(bf16[8,896,256]{2,1,0:T(8,128)(2,1)} %gather_fusion.2), calls=%async_computation.1 | async-start | bytes 7340032 | tf_op jit(solution)/shard_map/all_to_all | solution.py:29
  114.8 1.7 collective-permute-start.2
  116.4 2.9 collective-permute-start.3
  119.3 1.3 collective-permute-start.4
  120.8 9.0 %collective-permute-done.2 = bf16[2,32,4096]{2,1,0:T(8,128)(2,1)S(1)} collective-permute-done((bf16[2,32,4096]{2,1,0:T(8,128)(2,1)S(1)}, bf16[2,32,4096]{2,1,0:T(8,128)(2,1)S(1)}, u32[]{:S(2)}, u32[]{:S(2)}) %collective-permute-start.2) | collective-permute-done | bytes 524320 | tf_op jit(solution)/shard_map/ppermute | solution.py:36
  129.8 9.7 %collective-permute-done.3 = bf16[2,32,4096]{2,1,0:T(8,128)(2,1)S(1)} collective-permute-done((bf16[2,32,4096]{2,1,0:T(8,128)(2,1)S(1)}, bf16[2,32,4096]{2,1,0:T(8,128)(2,1)S(1)}, u32[]{:S(2)}, u32[]{:S(2)}) %collective-permute-start.3) | collective-permute-done | bytes 524320 | tf_op jit(solution)/shard_map/ppermute | solution.py:36
  139.8 2.0 gather_fusion
  141.8 4.4 %collective-permute-done.5 = bf16[4,2,32,4096]{3,2,1,0:T(8,128)(2,1)S(1)} collective-permute-done((bf16[4,2,32,4096]{3,2,1,0:T(8,128)(2,1)}, bf16[4,2,32,4096]{3,2,1,0:T(8,128)(2,1)S(1)}, u32[]{:S(2)}, u32[]{:S(2)}) %collective-permute-start.5) | collective-permute-done | bytes 2097184 | tf_op jit(solution)/shard_map/ppermute | solution.py:40
  146.2 2.8 fusion.2
  151.0 4.5 %convolution_convert_fusion = bf16[896,4096]{1,0:T(8,128)(2,1)S(1)} fusion(bf16[512,4096]{1,0:T(8,128)(2,1)S(1)} %bitcast.44, bf16[512,896]{1,0:T(8,128)(2,1)S(1)} %copy-done.5, bf16[512,896]{1,0:T(8,128)(2,1)S(1)} %copy-done.4), kind=kOutput, calls=%fused_computation.6 | convolution fusion | flops 3765436416 | bytes 13369344 | tf_op jit(solution)/shard_map/dot_general | solution.py:60
  155.6 3.7 %copy.41 = bf16[112,16,8,256]{3,2,0,1:T(8,128)(2,1)} copy(bf16[112,16,8,256]{3,2,1,0:T(8,128)(2,1)S(1)} %bitcast.48) | data formatting | bytes 14680064 | tf_op jit(solution)/shard_map/reshape | solution.py:64
  159.3 7.5 %all-to-all-start.2 = ((bf16[896,16,256]{2,0,1:T(8,128)(2,1)}), bf16[896,16,256]{2,0,1:T(8,128)(2,1)}, u32[]{:S(2)}, u32[]{:S(2)}) async-start(bf16[896,16,256]{2,0,1:T(8,128)(2,1)} %bitcast.43), calls=%async_computation.2 | async-start | bytes 14680064 | tf_op jit(solution)/shard_map/all_to_all | solution.py:63
  166.9 3.6 %copy.25 = bf16[64,8,16,256]{3,2,1,0:T(8,128)(2,1)S(1)} copy(bf16[64,8,16,256]{3,1,2,0:T(8,128)(2,1)} %bitcast.45) | data formatting | bytes 8388608
  170.7 4.4 %fusion.3 = f32[512,896,1]{1,0,2:T(8,128)S(1)} fusion(bf16[8,896,256]{2,1,0:T(8,128)(2,1)} %all-to-all-done.1, bf16[512,1,8,256]{3,2,1,0:T(8,128)(2,1)S(1)} %get-tuple-element.55), kind=kOutput, calls=%fused_computation.15 | convolution fusion | flops 1879048192 | bytes 7602176 | tf_op jit(solution)/shard_map/tsd,sfd->tf/dot_general | solution.py:54
  175.2 6.3 %multiply_convert_fusion = (bf16[512,896]{1,0:T(8,128)(2,1)}, bf16[512,896]{1,0:T(8,128)(2,1)}) fusion(bf16[512,896]{1,0:T(8,128)(2,1)S(1)} %copy-done.4, bf16[512,896]{1,0:T(8,128)(2,1)S(1)} %copy-done.5, f32[512,896,1]{1,0,2:T(8,128)S(1)} %fusion.3, bf16[8,896,256]{2,1,0:T(8,128)(2,1)} %all-to-all-done, bf16[512,1,8,256]{3,2,1,0:T(8,128)(2,1)S(1)} %get-tuple-element.54), kind=kOutput, calls=%fused_computation.30 | convolution fusion | flops 1886388224 | bytes 11272192 | tf_op jit(solution)/shard_map/tsd,sfd->tf/dot_general | solution.py:52
  181.5 144.1 %all-to-all-done.2 = bf16[896,16,256]{2,0,1:T(8,128)(2,1)} async-done(((bf16[896,16,256]{2,0,1:T(8,128)(2,1)}), bf16[896,16,256]{2,0,1:T(8,128)(2,1)}, u32[]{:S(2)}, u32[]{:S(2)}) %all-to-all-start.2) | async-done | bytes 7340064 | tf_op jit(solution)/shard_map/all_to_all | solution.py:63
  325.5 7.4 %fusion = f32[4,896,256]{2,0,1:T(4,128)S(1)} fusion(bf16[896,16,256]{2,0,1:T(8,128)(2,1)} %all-to-all-done.2, s32[16]{0:T(128)S(1)} %copy-done.3), kind=kOutput, calls=%fused_computation.4 | convolution fusion | flops 29360192 | bytes 11010112 | tf_op jit(solution)/shard_map/lg,fgd->lfd/dot_general | solution.py:70
  332.9 2.5 copy.23
  (29 shorter events, 4.4 us)
Async XLA Ops:
  5.5 5.8 %copy-start.1 = (bf16[4,896,256]{2,1,0:T(8,128)(2,1)S(1)}, bf16[4,896,256]{2,1,0:T(8,128)(2,1)}, u32[]{:S(2)}) copy-start(bf16[4,896,256]{2,1,0:T(8,128)(2,1)} %param.8) | copy-start | bytes 5505028
  5.5 7.3 %copy-start.2 = (bf16[32,4096]{1,0:T(8,128)(2,1)S(1)}, bf16[32,4096]{1,0:T(8,128)(2,1)}, u32[]{:S(2)}) copy-start(bf16[32,4096]{1,0:T(8,128)(2,1)} %param.5) | copy-start | bytes 786436
  5.5 102.8 %all-to-all-start = ((bf16[8,896,256]{2,1,0:T(8,128)(2,1)}), bf16[8,896,256]{2,1,0:T(8,128)(2,1)}, u32[]{:S(2)}, u32[]{:S(2)}) async-start(bf16[8,896,256]{2,1,0:T(8,128)(2,1)} %gather_fusion.1), calls=%async_computation | async-start | bytes 7340032 | tf_op jit(solution)/shard_map/all_to_all | solution.py:25
  11.3 92.8 %collective-permute-start.1 = (bf16[4,896,256]{2,1,0:T(8,128)(2,1)S(1)}, bf16[4,896,256]{2,1,0:T(8,128)(2,1)}, u32[]{:S(2)}, u32[]{:S(2)}) collective-permute-start(bf16[4,896,256]{2,1,0:T(8,128)(2,1)S(1)} %copy-done.1), channel_id=1, source_target_pairs={{0,128},{128,0},{1,129},{129,1},{2,130},{130,2},{3,131},{131,3},{4... | collective-permute-start | bytes 5505032 | tf_op jit(solution)/shard_map/ppermute | solution.py:26
  12.8 90.3 %collective-permute-start = (bf16[32,4096]{1,0:T(8,128)(2,1)S(1)}, bf16[32,4096]{1,0:T(8,128)(2,1)S(1)}, u32[]{:S(2)}, u32[]{:S(2)}) collective-permute-start(bf16[32,4096]{1,0:T(8,128)(2,1)S(1)} %copy-done.2), channel_id=1, source_target_pairs={{0,8},{8,0},{1,9},{9,1},{2,10},{10,2},{3,11},{11,3},{4,12},{12,4},... | collective-permute-start | bytes 786440 | tf_op jit(solution)/shard_map/ppermute | solution.py:19
  108.2 51.1 %all-to-all-start.1 = ((bf16[8,896,256]{2,1,0:T(8,128)(2,1)}), bf16[8,896,256]{2,1,0:T(8,128)(2,1)}, u32[]{:S(2)}, u32[]{:S(2)}) async-start(bf16[8,896,256]{2,1,0:T(8,128)(2,1)} %gather_fusion.2), calls=%async_computation.1 | async-start | bytes 7340032 | tf_op jit(solution)/shard_map/all_to_all | solution.py:29
  114.8 15.0 %collective-permute-start.2 = (bf16[2,32,4096]{2,1,0:T(8,128)(2,1)S(1)}, bf16[2,32,4096]{2,1,0:T(8,128)(2,1)S(1)}, u32[]{:S(2)}, u32[]{:S(2)}) collective-permute-start(bf16[2,32,4096]{2,1,0:T(8,128)(2,1)S(1)} %maximum_select_fusion.2), channel_id=1, source_target_pairs={{0,2},{2,4},{4,6},{6,0},{1,3},{3,5},{5,7},{7,1},{8,10},{10,12},{12... | collective-permute-start | bytes 1572872 | tf_op jit(solution)/shard_map/ppermute | solution.py:36
  116.4 23.1 %collective-permute-start.3 = (bf16[2,32,4096]{2,1,0:T(8,128)(2,1)S(1)}, bf16[2,32,4096]{2,1,0:T(8,128)(2,1)S(1)}, u32[]{:S(2)}, u32[]{:S(2)}) collective-permute-start(bf16[2,32,4096]{2,1,0:T(8,128)(2,1)S(1)} %maximum_select_fusion.2), channel_id=1, source_target_pairs={{0,4},{2,6},{4,0},{6,2},{1,5},{3,7},{5,1},{7,3},{8,12},{10,14},{12... | collective-permute-start | bytes 1572872 | tf_op jit(solution)/shard_map/ppermute | solution.py:36
  119.3 20.2 %collective-permute-start.4 = (bf16[2,32,4096]{2,1,0:T(8,128)(2,1)S(1)}, bf16[2,32,4096]{2,1,0:T(8,128)(2,1)S(1)}, u32[]{:S(2)}, u32[]{:S(2)}) collective-permute-start(bf16[2,32,4096]{2,1,0:T(8,128)(2,1)S(1)} %maximum_select_fusion.2), channel_id=1, source_target_pairs={{0,6},{2,0},{4,2},{6,4},{1,7},{3,1},{5,3},{7,5},{8,14},{10,8},{12,... | collective-permute-start | bytes 1572872 | tf_op jit(solution)/shard_map/ppermute | solution.py:36
  141.8 4.4 %collective-permute-start.5 = (bf16[4,2,32,4096]{3,2,1,0:T(8,128)(2,1)}, bf16[4,2,32,4096]{3,2,1,0:T(8,128)(2,1)S(1)}, u32[]{:S(2)}, u32[]{:S(2)}) collective-permute-start(bf16[4,2,32,4096]{3,2,1,0:T(8,128)(2,1)} %gather_fusion), channel_id=1, source_target_pairs={{0,1},{1,0},{2,3},{3,2},{4,5},{5,4},{6,7},{7,6},{8,9},{9,8},{10,11... | collective-permute-start | bytes 6291464 | tf_op jit(solution)/shard_map/ppermute | solution.py:40
  149.0 1.2 copy-start.4
  149.0 2.0 copy-start.5
  149.3 6.3 %copy-start = (bf16[2,4,2,32,4096]{4,3,2,1,0:T(8,128)(2,1)}, bf16[2,4,2,32,4096]{4,3,2,1,0:T(8,128)(2,1)S(1)}, u32[]{:S(2)}) copy-start(bf16[2,4,2,32,4096]{4,3,2,1,0:T(8,128)(2,1)S(1)} %copy.17) | copy-start | bytes 12582916
  159.3 166.2 %all-to-all-start.2 = ((bf16[896,16,256]{2,0,1:T(8,128)(2,1)}), bf16[896,16,256]{2,0,1:T(8,128)(2,1)}, u32[]{:S(2)}, u32[]{:S(2)}) async-start(bf16[896,16,256]{2,0,1:T(8,128)(2,1)} %bitcast.43), calls=%async_computation.2 | async-start | bytes 14680064 | tf_op jit(solution)/shard_map/all_to_all | solution.py:63
  175.2 150.4 %copy-start.3 = (s32[16]{0:T(128)S(1)}, s32[16]{0:T(128)}, u32[]{:S(2)}) copy-start(s32[16]{0:T(128)} %param.9) | copy-start | bytes 196

commit v10 on v4

--- a/solution.py
+++ b/solution.py
@@ -26,7 +26,6 @@
     near = lax.all_to_all(own_slabs, HALF, split_axis=0, concat_axis=0, tiled=True)
     block = lax.ppermute(w_down, "zh2", [(0, 1), (1, 0)])
     relay = jnp.take(block, own_langs, axis=0, mode="clip")
-    far = lax.all_to_all(relay, HALF, split_axis=0, concat_axis=0, tiled=True)
     first = lax.axis_index("zh") == 0
     pair = jnp.where(first, jnp.stack([cotangent, partner]), jnp.stack([partner, cotangent]))
     ring = lax.axis_size("y")
@@ -46,6 +45,17 @@
     sig = jax.nn.sigmoid(gate_f)
     act = gate_f * sig
     hidden = (act * up_f).astype(jnp.bfloat16)
+    partial_term = lax.dot_general(
+        hidden, out_rows, (((0,), (0,)), ((), ())), preferred_element_type=jnp.float32
+    ).astype(jnp.bfloat16)
+    pieces = jnp.transpose(partial_term.reshape(ff_dev, groups, feat_dev), (1, 0, 2))
+    own_start = side * half
+    send = lax.dynamic_update_slice(pieces, relay, (own_start, 0, 0))
+    got = lax.all_to_all(send, DP, split_axis=0, concat_axis=0, tiled=True)
+    far = lax.dynamic_slice_in_dim(got, own_start, half, axis=0)
+    own_pieces = lax.dynamic_slice_in_dim(pieces, own_start, half, axis=0)
+    own_got = lax.all_to_all(own_pieces, HALF, split_axis=0, concat_axis=0, tiled=True)
+    by_group = lax.dynamic_update_slice(got, own_got, (own_start, 0, 0))
     rows3 = out_rows.reshape(out_rows.shape[0], 2, half, feat_dev)
     cot_near = jnp.take(rows3, side, axis=1, mode="clip")
     cot_far = jnp.take(rows3, 1 - side, axis=1, mode="clip")
@@ -57,17 +67,9 @@
     selector = (language[None, :] == jnp.arange(variants, dtype=jnp.int32)[:, None]).astype(
         jnp.bfloat16
     )
-    partial_term = lax.dot_general(
-        hidden, out_rows, (((0,), (0,)), ((), ())), preferred_element_type=jnp.float32
-    ).astype(jnp.bfloat16)
-    pieces = lax.all_to_all(
-        partial_term.reshape(ff_dev, groups, feat_dev),
-        DP,
-        split_axis=1,
-        concat_axis=1,
-        tiled=True,
+    d_weight = jnp.einsum(
+        "lg,gfd->lfd", selector, by_group, preferred_element_type=jnp.float32
     )
-    d_weight = jnp.einsum("lg,fgd->lfd", selector, pieces, preferred_element_type=jnp.float32)
     return (d_gate, d_up, d_weight)
 
 

time: 340 us -> 397 us (1.17)
  waiting for transfers between devices: 257 us -> 293 us
  local copies, waits for them, and re-layouts: 23.1 us -> 39.4 us
    all_to_all x2, waiting for transfers between devices: 144 us -> 179 us  [the longest x1 154 us: shards(): got = lax.all_to_all(send, DP, split_axis=0, concat_axis=0, tiled=True)]
    dynamic_update_slice x0 -> x2, local copies, waits for them, and re-layouts: none -> 6.2 us  [the longest x1 4.12 us: shards(): by_group = lax.dynamic_update_slice(got, own_got, (own_start, 0, 0))]
    unnamed x14 -> x19, local copies, waits for them, and re-layouts: 7.86 us -> 13.8 us
    ppermute x1, waiting for transfers between devices: 4.35 us -> 0.01 us  [shards(): other = lax.ppermute(by_y, 'c', [(0, 1), (1, 0)])]
    dynamic_slice x0 -> x1, local copies, waits for them, and re-layouts: none -> 4.11 us  [shards(): own_pieces = lax.dynamic_slice_in_dim(pieces, own_start, half, axis=0)]
  transfers between devices with their start and end apart: 9 -> 9, of which waited for: 6 -> 6; matrix products, arithmetic and copies ran while one was open for 11% -> 13% of each run, Pallas kernels for 0% -> 0%
where the time goes in v10:
time: 397 us; the launch traced here: 392 us
  waiting for transfers between devices  293 us (74%)
  local copies, waits for them, and re-layouts  39.4 us (10%)
  starting transfers between devices  30.4 us (8%)
  matrix products  24.5 us (6%)
  other arithmetic  4 us (1%)
    all_to_all x1, waiting for transfers between devices, shards(): got = lax.all_to_all(send, DP, split_axis=0, concat_axis=0, tiled=True)  154 us
    ppermute x1, waiting for transfers between devices, shards(): block = lax.ppermute(w_down, 'zh2', [(0, 1), (1, 0)])  81.5 us
    all_to_all x1, waiting for transfers between devices, shards(): lax.all_to_all(own_pieces, HALF, split_axis=0, concat_axis=0, tiled=True)  24.8 us
    ppermute x3, waiting for transfers between devices, shards(): lax.ppermute(pair, 'y', [(i, (i + shift) % ring) for i in range(ring)])  23.4 us
    unnamed x19, local copies, waits for them, and re-layouts  13.8 us
    ppermute x1, waiting for transfers between devices, shards(): partner = lax.ppermute(cotangent, 'zh', [(0, 1), (1, 0)])  8.97 us
  transfers between devices with their start and end apart: 9, of which 6 were waited for; matrix products, arithmetic and copies ran while one was open for 13% of the time, Pallas kernels for 0%

profile of v10, /device:TPU:228, one launch (start us, length us, event | category | flops | bytes accessed | tf_op | source)
XLA Modules:
  0.0 391.9 jit_solution(13913502415347445511)
XLA Ops:
  2.9 4.0 %gather_fusion = bf16[8,896,256]{2,1,0:T(8,128)(2,1)} fusion(bf16[4,896,256]{2,1,0:T(8,128)(2,1)} %param.8, s32[1024]{0:T(1024)S(1)} %pad_clamp_fusion.1), kind=kCustom, calls=%fused_computation | custom fusion | bytes 7340064 | tf_op jit(solution)/shard_map/jit(_take)/gather | solution.py:24
  7.0 9.0 %collective-permute-done = bf16[32,4096]{1,0:T(8,128)(2,1)S(1)} collective-permute-done((bf16[32,4096]{1,0:T(8,128)(2,1)}, bf16[32,4096]{1,0:T(8,128)(2,1)S(1)}, u32[]{:S(2)}, u32[]{:S(2)}) %collective-permute-start) | collective-permute-done | bytes 262176 | tf_op jit(solution)/shard_map/ppermute | solution.py:19
  15.9 7.9 %all-to-all-start = ((bf16[8,896,256]{2,1,0:T(8,128)(2,1)}), bf16[8,896,256]{2,1,0:T(8,128)(2,1)}, u32[]{:S(2)}, u32[]{:S(2)}) async-start(bf16[8,896,256]{2,1,0:T(8,128)(2,1)} %gather_fusion), calls=%async_computation | async-start | bytes 7340032 | tf_op jit(solution)/shard_map/all_to_all | solution.py:26
  24.6 3.1 collective-permute-start.3
  29.4 19.7 %collective-permute-done.3 = bf16[2,32,4096]{2,1,0:T(8,128)(2,1)S(1)} collective-permute-done((bf16[2,32,4096]{2,1,0:T(8,128)(2,1)S(1)}, bf16[2,32,4096]{2,1,0:T(8,128)(2,1)S(1)}, u32[]{:S(2)}, u32[]{:S(2)}) %collective-permute-start.3) | collective-permute-done | bytes 524320 | tf_op jit(solution)/shard_map/ppermute | solution.py:35
  49.2 3.7 collective-permute-done.1
  56.6 81.5 %collective-permute-done.5 = bf16[4,896,256]{2,1,0:T(8,128)(2,1)} collective-permute-done((bf16[4,896,256]{2,1,0:T(8,128)(2,1)}, bf16[4,896,256]{2,1,0:T(8,128)(2,1)}, u32[]{:S(2)}, u32[]{:S(2)}) %collective-permute-start.5) | collective-permute-done | bytes 1835040 | tf_op jit(solution)/shard_map/ppermute | solution.py:27
  138.2 4.1 %gather_fusion.2 = bf16[8,896,256]{2,1,0:T(8,128)(2,1)} fusion(bf16[4,896,256]{2,1,0:T(8,128)(2,1)} %collective-permute-done.5, s32[1024]{0:T(1024)S(1)} %pad_clamp_fusion.1), kind=kCustom, calls=%fused_computation.2 | custom fusion | bytes 7340064 | tf_op jit(solution)/shard_map/jit(_take)/gather | solution.py:28
  142.3 2.8 fusion.2
  147.2 6.4 %convolution_convert_fusion = bf16[896,4096]{1,0:T(8,128)(2,1)} fusion(bf16[512,4096]{1,0:T(8,128)(2,1)S(1)} %bitcast.50, bf16[512,896]{1,0:T(8,128)(2,1)S(1)} %copy-done.7, bf16[512,896]{1,0:T(8,128)(2,1)S(1)} %copy-done.6), kind=kOutput, calls=%fused_computation.6 | convolution fusion | flops 3765436416 | bytes 13369344 | tf_op jit(solution)/shard_map/dot_general | solution.py:48
  153.6 3.8 copy.45
  157.4 3.5 copy.46
  160.9 2.5 copy-done
  165.4 7.5 %all-to-all-start.1 = ((bf16[16,896,256]{2,1,0:T(8,128)(2,1)}), bf16[16,896,256]{2,1,0:T(8,128)(2,1)}, u32[]{:S(2)}, u32[]{:S(2)}) async-start(bf16[16,896,256]{2,1,0:T(8,128)(2,1)} %constant_dynamic-update-slice_fusion.1), calls=%async_computation.1 | async-start | bytes 14680064 | tf_op jit(solution)/shard_map/all_to_all | solution.py:54
  173.0 4.1 %dynamic-slice_bitcast_fusion = bf16[8,896,256]{2,1,0:T(8,128)(2,1)} fusion(bf16[896,16,256]{2,0,1:T(8,128)(2,1)} %bitcast.49, s32[]{:T(128)S(6)} %select_n.47), kind=kLoop, calls=%fused_computation.9 | loop fusion | bytes 7340036 | tf_op jit(solution)/shard_map/dynamic_slice | solution.py:56
  177.1 154.1 %all-to-all-done.1 = bf16[16,896,256]{2,1,0:T(8,128)(2,1)} async-done(((bf16[16,896,256]{2,1,0:T(8,128)(2,1)}), bf16[16,896,256]{2,1,0:T(8,128)(2,1)}, u32[]{:S(2)}, u32[]{:S(2)}) %all-to-all-start.1) | async-done | bytes 7340064 | tf_op jit(solution)/shard_map/all_to_all | solution.py:54
  331.2 7.3 %all-to-all-start.2 = ((bf16[8,896,256]{2,1,0:T(8,128)(2,1)}), bf16[8,896,256]{2,1,0:T(8,128)(2,1)}, u32[]{:S(2)}, u32[]{:S(2)}) async-start(bf16[8,896,256]{2,1,0:T(8,128)(2,1)} %dynamic-slice_bitcast_fusion), calls=%async_computation.2 | async-start | bytes 7340032 | tf_op jit(solution)/shard_map/all_to_all | solution.py:57
  338.6 3.6 copy.27
  342.5 4.4 %fusion.6 = f32[512,896,1]{1,0,2:T(8,128)S(1)} fusion(bf16[8,896,256]{2,1,0:T(8,128)(2,1)} %all-to-all-done, bf16[512,1,8,256]{3,2,1,0:T(8,128)(2,1)S(1)} %get-tuple-element.54), kind=kOutput, calls=%fused_computation.19 | convolution fusion | flops 1879048192 | bytes 7602176 | tf_op jit(solution)/shard_map/tsd,sfd->tf/dot_general | solution.py:62
  346.9 6.3 %multiply_convert_fusion = (bf16[512,896]{1,0:T(8,128)(2,1)}, bf16[512,896]{1,0:T(8,128)(2,1)}) fusion(bf16[512,896]{1,0:T(8,128)(2,1)S(1)} %copy-done.6, bf16[512,896]{1,0:T(8,128)(2,1)S(1)} %copy-done.7, bf16[16,896,256]{2,1,0:T(8,128)(2,1)} %all-to-all-done.1, s32[]{:T(128)S(6)} %select_n.47, bf16[512,1,8,256]{3,2,1,0:T(8,128)(2,1)S(1)} %get-tuple-element.53, ...), kind=kOutput, calls=%fused_computation.32 | convolution fusion | flops 1886388224 | bytes 11272196 | tf_op jit(solution)/shard_map/tsd,sfd->tf/dot_general | solution.py:64
  353.1 24.8 %all-to-all-done.2 = bf16[8,896,256]{2,1,0:T(8,128)(2,1)} async-done(((bf16[8,896,256]{2,1,0:T(8,128)(2,1)}), bf16[8,896,256]{2,1,0:T(8,128)(2,1)}, u32[]{:S(2)}, u32[]{:S(2)}) %all-to-all-start.2) | async-done | bytes 3670048 | tf_op jit(solution)/shard_map/all_to_all | solution.py:57
  377.9 4.1 %constant_dynamic-update-slice_fusion = bf16[16,896,256]{2,1,0:T(8,128)(2,1)} fusion(bf16[16,896,256]{2,1,0:T(8,128)(2,1)} %all-to-all-done.1, bf16[8,896,256]{2,1,0:T(8,128)(2,1)} %all-to-all-done.2, s32[]{:T(128)S(6)} %select_n.47), kind=kLoop, calls=%fused_computation.45 | loop fusion | bytes 7340036 | tf_op jit(solution)/shard_map/dynamic_update_slice | solution.py:58
  382.0 7.4 %fusion = f32[4,896,256]{2,0,1:T(4,128)S(1)} fusion(bf16[16,896,256]{2,1,0:T(8,128)(2,1)} %constant_dynamic-update-slice_fusion, s32[16]{0:T(128)S(1)} %copy-done.5), kind=kOutput, calls=%fused_computation.4 | convolution fusion | flops 29360192 | bytes 11010112 | tf_op jit(solution)/shard_map/lg,gfd->lfd/dot_general | solution.py:70
  389.4 2.5 copy.25
  (37 shorter events, 13.0 us)
Async XLA Ops:
  0.6 15.3 %collective-permute-start = (bf16[32,4096]{1,0:T(8,128)(2,1)}, bf16[32,4096]{1,0:T(8,128)(2,1)S(1)}, u32[]{:S(2)}, u32[]{:S(2)}) collective-permute-start(bf16[32,4096]{1,0:T(8,128)(2,1)} %param.5), channel_id=1, source_target_pairs={{0,8},{8,0},{1,9},{9,1},{2,10},{10,2},{3,11},{11,3},{4,12},{12,4},... | collective-permute-start | bytes 786440 | tf_op jit(solution)/shard_map/ppermute | solution.py:19
  7.0 17.6 %copy-start.4 = (bf16[32,4096]{1,0:T(8,128)(2,1)S(1)}, bf16[32,4096]{1,0:T(8,128)(2,1)}, u32[]{:S(2)}) copy-start(bf16[32,4096]{1,0:T(8,128)(2,1)} %param.5) | copy-start | bytes 786436
  15.9 149.5 %all-to-all-start = ((bf16[8,896,256]{2,1,0:T(8,128)(2,1)}), bf16[8,896,256]{2,1,0:T(8,128)(2,1)}, u32[]{:S(2)}, u32[]{:S(2)}) async-start(bf16[8,896,256]{2,1,0:T(8,128)(2,1)} %gather_fusion), calls=%async_computation | async-start | bytes 7340032 | tf_op jit(solution)/shard_map/all_to_all | solution.py:26
  24.6 24.5 %collective-permute-start.3 = (bf16[2,32,4096]{2,1,0:T(8,128)(2,1)S(1)}, bf16[2,32,4096]{2,1,0:T(8,128)(2,1)S(1)}, u32[]{:S(2)}, u32[]{:S(2)}) collective-permute-start(bf16[2,32,4096]{2,1,0:T(8,128)(2,1)S(1)} %maximum_select_fusion.2), channel_id=1, source_target_pairs={{0,6},{2,0},{4,2},{6,4},{1,7},{3,1},{5,3},{7,5},{8,14},{10,8},{12,... | collective-permute-start | bytes 1572872 | tf_op jit(solution)/shard_map/ppermute | solution.py:35
  27.7 21.4 %collective-permute-start.2 = (bf16[2,32,4096]{2,1,0:T(8,128)(2,1)S(1)}, bf16[2,32,4096]{2,1,0:T(8,128)(2,1)S(1)}, u32[]{:S(2)}, u32[]{:S(2)}) collective-permute-start(bf16[2,32,4096]{2,1,0:T(8,128)(2,1)S(1)} %maximum_select_fusion.2), channel_id=1, source_target_pairs={{0,4},{2,6},{4,0},{6,2},{1,5},{3,7},{5,1},{7,3},{8,12},{10,14},{12... | collective-permute-start | bytes 1572872 | tf_op jit(solution)/shard_map/ppermute | solution.py:35
  28.4 24.5 %collective-permute-start.1 = (bf16[2,32,4096]{2,1,0:T(8,128)(2,1)S(1)}, bf16[2,32,4096]{2,1,0:T(8,128)(2,1)S(1)}, u32[]{:S(2)}, u32[]{:S(2)}) collective-permute-start(bf16[2,32,4096]{2,1,0:T(8,128)(2,1)S(1)} %maximum_select_fusion.2), channel_id=1, source_target_pairs={{0,2},{2,4},{4,6},{6,0},{1,3},{3,5},{5,7},{7,1},{8,10},{10,12},{12... | collective-permute-start | bytes 1572872 | tf_op jit(solution)/shard_map/ppermute | solution.py:35
  55.1 87.1 %collective-permute-start.4 = (bf16[4,2,32,4096]{3,2,1,0:T(8,128)(2,1)}, bf16[4,2,32,4096]{3,2,1,0:T(8,128)(2,1)}, u32[]{:S(2)}, u32[]{:S(2)}) collective-permute-start(bf16[4,2,32,4096]{3,2,1,0:T(8,128)(2,1)} %gather_fusion.1), channel_id=1, source_target_pairs={{0,1},{1,0},{2,3},{3,2},{4,5},{5,4},{6,7},{7,6},{8,9},{9,8},{10,11... | collective-permute-start | bytes 6291464 | tf_op jit(solution)/shard_map/ppermute | solution.py:39
  55.2 83.0 %collective-permute-start.5 = (bf16[4,896,256]{2,1,0:T(8,128)(2,1)}, bf16[4,896,256]{2,1,0:T(8,128)(2,1)}, u32[]{:S(2)}, u32[]{:S(2)}) collective-permute-start(bf16[4,896,256]{2,1,0:T(8,128)(2,1)} %param.8), channel_id=1, source_target_pairs={{0,128},{128,0},{1,129},{129,1},{2,130},{130,2},{3,131},{131,3},{4... | collective-permute-start | bytes 5505032 | tf_op jit(solution)/shard_map/ppermute | solution.py:27
  56.6 85.7 %copy-start.3 = (bf16[4,2,32,4096]{3,2,1,0:T(8,128)(2,1)S(1)}, bf16[4,2,32,4096]{3,2,1,0:T(8,128)(2,1)}, u32[]{:S(2)}) copy-start(bf16[4,2,32,4096]{3,2,1,0:T(8,128)(2,1)} %gather_fusion.1) | copy-start | bytes 6291460
  145.1 1.2 copy-start.6
  145.1 2.0 copy-start.7
  145.4 8.1 %copy-start.1 = (bf16[2,4,2,32,4096]{4,3,2,1,0:T(8,128)(2,1)}, bf16[2,4,2,32,4096]{4,3,2,1,0:T(8,128)(2,1)S(1)}, u32[]{:S(2)}) copy-start(bf16[2,4,2,32,4096]{4,3,2,1,0:T(8,128)(2,1)S(1)} %copy.18) | copy-start | bytes 12582916
  157.4 6.0 %copy-start = (bf16[112,16,8,256]{3,2,0,1:T(8,128)(2,1)}, bf16[112,16,8,256]{3,2,0,1:T(8,128)(2,1)S(1)}, u32[]{:S(2)}) copy-start(bf16[112,16,8,256]{3,2,0,1:T(8,128)(2,1)S(1)} %copy.45) | copy-start | bytes 22020100
  157.4 6.0 %copy-start.2 = (bf16[8,896,256]{2,1,0:T(8,128)(2,1)S(1)}, bf16[8,896,256]{2,1,0:T(8,128)(2,1)}, u32[]{:S(2)}) copy-start(bf16[8,896,256]{2,1,0:T(8,128)(2,1)} %gather_fusion.2) | copy-start | bytes 11010052
  165.4 165.8 %all-to-all-start.1 = ((bf16[16,896,256]{2,1,0:T(8,128)(2,1)}), bf16[16,896,256]{2,1,0:T(8,128)(2,1)}, u32[]{:S(2)}, u32[]{:S(2)}) async-start(bf16[16,896,256]{2,1,0:T(8,128)(2,1)} %constant_dynamic-update-slice_fusion.1), calls=%async_computation.1 | async-start | bytes 14680064 | tf_op jit(solution)/shard_map/all_to_all | solution.py:54
  331.2 46.7 %all-to-all-start.2 = ((bf16[8,896,256]{2,1,0:T(8,128)(2,1)}), bf16[8,896,256]{2,1,0:T(8,128)(2,1)}, u32[]{:S(2)}, u32[]{:S(2)}) async-start(bf16[8,896,256]{2,1,0:T(8,128)(2,1)} %dynamic-slice_bitcast_fusion), calls=%async_computation.2 | async-start | bytes 7340032 | tf_op jit(solution)/shard_map/all_to_all | solution.py:57
  353.1 28.9 %copy-start.5 = (s32[16]{0:T(128)S(1)}, s32[16]{0:T(128)}, u32[]{:S(2)}) copy-start(s32[16]{0:T(128)} %param.9) | copy-start | bytes 196

commit v11 on v4

--- a/solution.py
+++ b/solution.py
@@ -57,17 +57,13 @@
     selector = (language[None, :] == jnp.arange(variants, dtype=jnp.int32)[:, None]).astype(
         jnp.bfloat16
     )
-    partial_term = lax.dot_general(
-        hidden, out_rows, (((0,), (0,)), ((), ())), preferred_element_type=jnp.float32
+    partial_t = lax.dot_general(
+        out_rows, hidden, (((0,), (0,)), ((), ())), preferred_element_type=jnp.float32
     ).astype(jnp.bfloat16)
     pieces = lax.all_to_all(
-        partial_term.reshape(ff_dev, groups, feat_dev),
-        DP,
-        split_axis=1,
-        concat_axis=1,
-        tiled=True,
+        partial_t.reshape(groups, feat_dev, ff_dev), DP, split_axis=0, concat_axis=0, tiled=True
     )
-    d_weight = jnp.einsum("lg,fgd->lfd", selector, pieces, preferred_element_type=jnp.float32)
+    d_weight = jnp.einsum("lg,gdf->lfd", selector, pieces, preferred_element_type=jnp.float32)
     return (d_gate, d_up, d_weight)
 
 

time: 340 us -> 343 us (level)
  matrix products: 22.6 us -> 26.9 us
    dot_general x2, matrix products: 11.9 us -> 16.2 us  [the longest x1 9.31 us: shards(): jnp.einsum('lg,gdf->lfd', selector, pieces, preferred_element_type=jnp.fl...]
    reshape x1 -> x0, local copies, waits for them, and re-layouts: 3.74 us -> none  [shards(): partial_term.reshape(ff_dev, groups, feat_dev)]
where the time goes in v11:
time: 343 us; the launch traced here: 340 us
  waiting for transfers between devices  257 us (75%)
  starting transfers between devices  29.3 us (9%)
  matrix products  26.9 us (8%)
  local copies, waits for them, and re-layouts  22.1 us (6%)
  other arithmetic  4.01 us (1%)
    all_to_all x1, waiting for transfers between devices, shards(): lax.all_to_all(partial_t.reshape(groups, feat_dev, ff_dev), DP, split_axi...  144 us
    ppermute x1, waiting for transfers between devices, shards(): block = lax.ppermute(w_down, 'zh2', [(0, 1), (1, 0)])  79.3 us
    ppermute x3, waiting for transfers between devices, shards(): lax.ppermute(pair, 'y', [(i, (i + shift) % ring) for i in range(ring)])  20.5 us
    unnamed x14, local copies, waits for them, and re-layouts  10.6 us
    dot_general x1, matrix products, shards(): jnp.einsum('lg,gdf->lfd', selector, pieces, preferred_element_type=jnp.fl...  9.31 us
    ppermute x1, waiting for transfers between devices, shards(): partner = lax.ppermute(cotangent, 'zh', [(0, 1), (1, 0)])  8.94 us
    all_to_all x1, starting transfers between devices, shards(): lax.all_to_all(own_slabs, HALF, split_axis=0, concat_axis=0, tiled=True)  7.86 us
    all_to_all x1, starting transfers between devices, shards(): lax.all_to_all(partial_t.reshape(groups, feat_dev, ff_dev), DP, split_axi...  7.52 us
  transfers between devices with their start and end apart: 9, of which 6 were waited for; matrix products, arithmetic and copies ran while one was open for 11% of the time, Pallas kernels for 0%

profile of v11, /device:TPU:228, one launch (start us, length us, event | category | flops | bytes accessed | tf_op | source)
XLA Modules:
  0.0 340.2 jit_solution(11781564985994894289)
XLA Ops:
  0.6 1.5 collective-permute-start
  2.9 4.1 %gather_fusion = bf16[8,896,256]{2,1,0:T(8,128)(2,1)} fusion(bf16[4,896,256]{2,1,0:T(8,128)(2,1)} %param.8, s32[1024]{0:T(1024)S(1)} %pad_clamp_fusion.1), kind=kCustom, calls=%fused_computation | custom fusion | bytes 7340064 | tf_op jit(solution)/shard_map/jit(_take)/gather | solution.py:24
  7.0 8.9 %collective-permute-done = bf16[32,4096]{1,0:T(8,128)(2,1)S(1)} collective-permute-done((bf16[32,4096]{1,0:T(8,128)(2,1)}, bf16[32,4096]{1,0:T(8,128)(2,1)S(1)}, u32[]{:S(2)}, u32[]{:S(2)}) %collective-permute-start) | collective-permute-done | bytes 262176 | tf_op jit(solution)/shard_map/ppermute | solution.py:19
  15.9 7.9 %all-to-all-start = ((bf16[8,896,256]{2,1,0:T(8,128)(2,1)}), bf16[8,896,256]{2,1,0:T(8,128)(2,1)}, u32[]{:S(2)}, u32[]{:S(2)}) async-start(bf16[8,896,256]{2,1,0:T(8,128)(2,1)} %gather_fusion), calls=%async_computation | async-start | bytes 7340032 | tf_op jit(solution)/shard_map/all_to_all | solution.py:26
  23.8 1.9 collective-permute-start.5
  25.7 79.3 %collective-permute-done.5 = bf16[4,896,256]{2,1,0:T(8,128)(2,1)} collective-permute-done((bf16[4,896,256]{2,1,0:T(8,128)(2,1)S(1)}, bf16[4,896,256]{2,1,0:T(8,128)(2,1)}, u32[]{:S(2)}, u32[]{:S(2)}) %collective-permute-start.5) | collective-permute-done | bytes 1835040 | tf_op jit(solution)/shard_map/ppermute | solution.py:27
  104.9 4.1 %gather_fusion.2 = bf16[8,896,256]{2,1,0:T(8,128)(2,1)} fusion(bf16[4,896,256]{2,1,0:T(8,128)(2,1)} %collective-permute-done.5, s32[1024]{0:T(1024)S(1)} %pad_clamp_fusion.1), kind=kCustom, calls=%fused_computation.2 | custom fusion | bytes 7340064 | tf_op jit(solution)/shard_map/jit(_take)/gather | solution.py:28
  109.0 5.8 %all-to-all-start.1 = ((bf16[8,896,256]{2,1,0:T(8,128)(2,1)}), bf16[8,896,256]{2,1,0:T(8,128)(2,1)}, u32[]{:S(2)}, u32[]{:S(2)}) async-start(bf16[8,896,256]{2,1,0:T(8,128)(2,1)} %gather_fusion.2), calls=%async_computation.1 | async-start | bytes 7340032 | tf_op jit(solution)/shard_map/all_to_all | solution.py:29
  115.7 3.1 collective-permute-start.3
  119.4 1.0 collective-permute-start.1
  120.5 16.8 %collective-permute-done.3 = bf16[2,32,4096]{2,1,0:T(8,128)(2,1)S(1)} collective-permute-done((bf16[2,32,4096]{2,1,0:T(8,128)(2,1)S(1)}, bf16[2,32,4096]{2,1,0:T(8,128)(2,1)S(1)}, u32[]{:S(2)}, u32[]{:S(2)}) %collective-permute-start.3) | collective-permute-done | bytes 524320 | tf_op jit(solution)/shard_map/ppermute | solution.py:36
  137.3 3.7 %collective-permute-done.1 = bf16[2,32,4096]{2,1,0:T(8,128)(2,1)S(1)} collective-permute-done((bf16[2,32,4096]{2,1,0:T(8,128)(2,1)S(1)}, bf16[2,32,4096]{2,1,0:T(8,128)(2,1)S(1)}, u32[]{:S(2)}, u32[]{:S(2)}) %collective-permute-start.1) | collective-permute-done | bytes 524320 | tf_op jit(solution)/shard_map/ppermute | solution.py:36
  141.3 2.0 gather_fusion.1
  143.3 4.4 %collective-permute-done.4 = bf16[4,2,32,4096]{3,2,1,0:T(8,128)(2,1)S(1)} collective-permute-done((bf16[4,2,32,4096]{3,2,1,0:T(8,128)(2,1)}, bf16[4,2,32,4096]{3,2,1,0:T(8,128)(2,1)S(1)}, u32[]{:S(2)}, u32[]{:S(2)}) %collective-permute-start.4) | collective-permute-done | bytes 2097184 | tf_op jit(solution)/shard_map/ppermute | solution.py:40
  147.6 2.8 fusion.2
  150.8 1.9 copy-done
  152.7 6.9 %convolution_convert_fusion = bf16[4096,896]{1,0:T(8,128)(2,1)} fusion(bf16[512,4096]{1,0:T(8,128)(2,1)S(1)} %bitcast.42, bf16[512,896]{1,0:T(8,128)(2,1)S(1)} %copy-done.5, bf16[512,896]{1,0:T(8,128)(2,1)S(1)} %copy-done.4), kind=kOutput, calls=%fused_computation.5 | convolution fusion | flops 3765436416 | bytes 13369344 | tf_op jit(solution)/shard_map/dot_general | solution.py:60
  159.7 7.5 %all-to-all-start.2 = ((bf16[16,256,896]{2,1,0:T(8,128)(2,1)}), bf16[16,256,896]{2,1,0:T(8,128)(2,1)}, u32[]{:S(2)}, u32[]{:S(2)}) async-start(bf16[16,256,896]{2,1,0:T(8,128)(2,1)} %bitcast.46), calls=%async_computation.2 | async-start | bytes 14680064 | tf_op jit(solution)/shard_map/all_to_all | solution.py:63
  167.2 3.6 %copy.26 = bf16[64,8,16,256]{3,2,1,0:T(8,128)(2,1)S(1)} copy(bf16[64,8,16,256]{3,1,2,0:T(8,128)(2,1)} %bitcast.43) | data formatting | bytes 8388608
  171.1 4.4 %fusion.5 = f32[512,896,1]{1,0,2:T(8,128)S(1)} fusion(bf16[8,896,256]{2,1,0:T(8,128)(2,1)} %all-to-all-done, bf16[512,1,8,256]{3,2,1,0:T(8,128)(2,1)S(1)} %get-tuple-element.55), kind=kOutput, calls=%fused_computation.16 | convolution fusion | flops 1879048192 | bytes 7602176 | tf_op jit(solution)/shard_map/tsd,sfd->tf/dot_general | solution.py:52
  175.5 6.3 %multiply_convert_fusion = (bf16[512,896]{1,0:T(8,128)(2,1)}, bf16[512,896]{1,0:T(8,128)(2,1)}) fusion(bf16[512,896]{1,0:T(8,128)(2,1)S(1)} %copy-done.4, bf16[512,896]{1,0:T(8,128)(2,1)S(1)} %copy-done.5, bf16[8,896,256]{2,1,0:T(8,128)(2,1)} %all-to-all-done.1, bf16[512,1,8,256]{3,2,1,0:T(8,128)(2,1)S(1)} %get-tuple-element.54, f32[512,896,1]{1,0,2:T(8,128)S(1)} %fusion.5), kind=kOutput, calls=%fused_computation.30 | convolution fusion | flops 1886388224 | bytes 11272192 | tf_op jit(solution)/shard_map/tsd,sfd->tf/dot_general | solution.py:54
  181.8 144.1 %all-to-all-done.2 = bf16[16,256,896]{2,1,0:T(8,128)(2,1)} async-done(((bf16[16,256,896]{2,1,0:T(8,128)(2,1)}), bf16[16,256,896]{2,1,0:T(8,128)(2,1)}, u32[]{:S(2)}, u32[]{:S(2)}) %all-to-all-start.2) | async-done | bytes 7340064 | tf_op jit(solution)/shard_map/all_to_all | solution.py:63
  325.9 9.3 %fusion.9 = f32[4,896,256]{1,0,2:T(4,128)} fusion(bf16[16,256,896]{2,1,0:T(8,128)(2,1)} %all-to-all-done.2, s32[16]{0:T(128)S(1)} %copy-done.3), kind=kOutput, calls=%fused_computation.20 | convolution fusion | flops 29360192 | bytes 11010112 | tf_op jit(solution)/shard_map/lg,gdf->lfd/dot_general | solution.py:66
  335.2 5.1 %copy.25 = f32[4,896,256]{2,1,0:T(8,128)} copy(f32[4,896,256]{1,0,2:T(4,128)} %fusion.9) | data formatting | bytes 7340032
  (28 shorter events, 3.2 us)
Async XLA Ops:
  0.6 15.3 %collective-permute-start = (bf16[32,4096]{1,0:T(8,128)(2,1)}, bf16[32,4096]{1,0:T(8,128)(2,1)S(1)}, u32[]{:S(2)}, u32[]{:S(2)}) collective-permute-start(bf16[32,4096]{1,0:T(8,128)(2,1)} %param.5), channel_id=1, source_target_pairs={{0,8},{8,0},{1,9},{9,1},{2,10},{10,2},{3,11},{11,3},{4,12},{12,4},... | collective-permute-start | bytes 786440 | tf_op jit(solution)/shard_map/ppermute | solution.py:19
  7.0 16.8 %copy-start.1 = (bf16[4,896,256]{2,1,0:T(8,128)(2,1)S(1)}, bf16[4,896,256]{2,1,0:T(8,128)(2,1)}, u32[]{:S(2)}) copy-start(bf16[4,896,256]{2,1,0:T(8,128)(2,1)} %param.8) | copy-start | bytes 5505028
  15.9 93.1 %all-to-all-start = ((bf16[8,896,256]{2,1,0:T(8,128)(2,1)}), bf16[8,896,256]{2,1,0:T(8,128)(2,1)}, u32[]{:S(2)}, u32[]{:S(2)}) async-start(bf16[8,896,256]{2,1,0:T(8,128)(2,1)} %gather_fusion), calls=%async_computation | async-start | bytes 7340032 | tf_op jit(solution)/shard_map/all_to_all | solution.py:26
  23.8 81.1 %collective-permute-start.5 = (bf16[4,896,256]{2,1,0:T(8,128)(2,1)S(1)}, bf16[4,896,256]{2,1,0:T(8,128)(2,1)}, u32[]{:S(2)}, u32[]{:S(2)}) collective-permute-start(bf16[4,896,256]{2,1,0:T(8,128)(2,1)S(1)} %copy-done.1), channel_id=1, source_target_pairs={{0,128},{128,0},{1,129},{129,1},{2,130},{130,2},{3,131},{131,3},{4... | collective-permute-start | bytes 5505032 | tf_op jit(solution)/shard_map/ppermute | solution.py:27
  109.0 6.6 %copy-start.2 = (bf16[32,4096]{1,0:T(8,128)(2,1)S(1)}, bf16[32,4096]{1,0:T(8,128)(2,1)}, u32[]{:S(2)}) copy-start(bf16[32,4096]{1,0:T(8,128)(2,1)} %param.5) | copy-start | bytes 786436
  109.0 50.6 %all-to-all-start.1 = ((bf16[8,896,256]{2,1,0:T(8,128)(2,1)}), bf16[8,896,256]{2,1,0:T(8,128)(2,1)}, u32[]{:S(2)}, u32[]{:S(2)}) async-start(bf16[8,896,256]{2,1,0:T(8,128)(2,1)} %gather_fusion.2), calls=%async_computation.1 | async-start | bytes 7340032 | tf_op jit(solution)/shard_map/all_to_all | solution.py:29
  115.7 21.6 %collective-permute-start.3 = (bf16[2,32,4096]{2,1,0:T(8,128)(2,1)S(1)}, bf16[2,32,4096]{2,1,0:T(8,128)(2,1)S(1)}, u32[]{:S(2)}, u32[]{:S(2)}) collective-permute-start(bf16[2,32,4096]{2,1,0:T(8,128)(2,1)S(1)} %maximum_select_fusion.2), channel_id=1, source_target_pairs={{0,6},{2,0},{4,2},{6,4},{1,7},{3,1},{5,3},{7,5},{8,14},{10,8},{12,... | collective-permute-start | bytes 1572872 | tf_op jit(solution)/shard_map/ppermute | solution.py:36
  118.8 18.5 %collective-permute-start.2 = (bf16[2,32,4096]{2,1,0:T(8,128)(2,1)S(1)}, bf16[2,32,4096]{2,1,0:T(8,128)(2,1)S(1)}, u32[]{:S(2)}, u32[]{:S(2)}) collective-permute-start(bf16[2,32,4096]{2,1,0:T(8,128)(2,1)S(1)} %maximum_select_fusion.2), channel_id=1, source_target_pairs={{0,4},{2,6},{4,0},{6,2},{1,5},{3,7},{5,1},{7,3},{8,12},{10,14},{12... | collective-permute-start | bytes 1572872 | tf_op jit(solution)/shard_map/ppermute | solution.py:36
  119.4 21.5 %collective-permute-start.1 = (bf16[2,32,4096]{2,1,0:T(8,128)(2,1)S(1)}, bf16[2,32,4096]{2,1,0:T(8,128)(2,1)S(1)}, u32[]{:S(2)}, u32[]{:S(2)}) collective-permute-start(bf16[2,32,4096]{2,1,0:T(8,128)(2,1)S(1)} %maximum_select_fusion.2), channel_id=1, source_target_pairs={{0,2},{2,4},{4,6},{6,0},{1,3},{3,5},{5,7},{7,1},{8,10},{10,12},{12... | collective-permute-start | bytes 1572872 | tf_op jit(solution)/shard_map/ppermute | solution.py:36
  143.3 4.4 %collective-permute-start.4 = (bf16[4,2,32,4096]{3,2,1,0:T(8,128)(2,1)}, bf16[4,2,32,4096]{3,2,1,0:T(8,128)(2,1)S(1)}, u32[]{:S(2)}, u32[]{:S(2)}) collective-permute-start(bf16[4,2,32,4096]{3,2,1,0:T(8,128)(2,1)} %gather_fusion.1), channel_id=1, source_target_pairs={{0,1},{1,0},{2,3},{3,2},{4,5},{5,4},{6,7},{7,6},{8,9},{9,8},{10,11... | collective-permute-start | bytes 6291464 | tf_op jit(solution)/shard_map/ppermute | solution.py:40
  150.5 2.3 copy-start.4
  150.5 2.3 copy-start.5
  150.8 2.0 copy-start
  159.7 166.2 %all-to-all-start.2 = ((bf16[16,256,896]{2,1,0:T(8,128)(2,1)}), bf16[16,256,896]{2,1,0:T(8,128)(2,1)}, u32[]{:S(2)}, u32[]{:S(2)}) async-start(bf16[16,256,896]{2,1,0:T(8,128)(2,1)} %bitcast.46), calls=%async_computation.2 | async-start | bytes 14680064 | tf_op jit(solution)/shard_map/all_to_all | solution.py:63
  175.5 150.4 %copy-start.3 = (s32[16]{0:T(128)S(1)}, s32[16]{0:T(128)}, u32[]{:S(2)}) copy-start(s32[16]{0:T(128)} %param.9) | copy-start | bytes 196

commit v12 on v4

--- a/solution.py
+++ b/solution.py
@@ -67,7 +67,8 @@
         concat_axis=1,
         tiled=True,
     )
-    d_weight = jnp.einsum("lg,fgd->lfd", selector, pieces, preferred_element_type=jnp.float32)
+    by_group = jnp.transpose(pieces, (1, 0, 2))
+    d_weight = jnp.sum(selector[:, :, None, None] * by_group[None], axis=1, dtype=jnp.float32)
     return (d_gate, d_up, d_weight)
 
 

time: 340 us -> 339 us (level)
  other arithmetic: 4.01 us -> 13.1 us
  matrix products: 22.6 us -> 15.2 us
    reduce_sum x0 -> x1, other arithmetic: none -> 9.1 us  [shards(): jnp.sum(selector[:, :, None, None] * by_group[None], axis=1, dtype=jnp.fl...]
    dot_general x1 -> x0, matrix products: 7.39 us -> none  [shards(): jnp.einsum('lg,fgd->lfd', selector, pieces, preferred_element_type=jnp.fl...]
    unnamed x14 -> x13, local copies, waits for them, and re-layouts: 7.86 us -> 5.36 us
where the time goes in v12:
time: 339 us; the launch traced here: 336 us
  waiting for transfers between devices  257 us (76%)
  starting transfers between devices  29.4 us (9%)
  local copies, waits for them, and re-layouts  20.6 us (6%)
  matrix products  15.2 us (4%)
  other arithmetic  13.1 us (4%)
    all_to_all x1, waiting for transfers between devices, shards(): lax.all_to_all(partial_term.reshape(ff_dev, groups, feat_dev), DP, split_...  144 us
    ppermute x1, waiting for transfers between devices, shards(): block = lax.ppermute(w_down, 'zh2', [(0, 1), (1, 0)])  79.3 us
    ppermute x3, waiting for transfers between devices, shards(): lax.ppermute(pair, 'y', [(i, (i + shift) % ring) for i in range(ring)])  20.5 us
    reduce_sum x1, other arithmetic, shards(): jnp.sum(selector[:, :, None, None] * by_group[None], axis=1, dtype=jnp.fl...  9.1 us
    ppermute x1, waiting for transfers between devices, shards(): partner = lax.ppermute(cotangent, 'zh', [(0, 1), (1, 0)])  8.95 us
    all_to_all x1, starting transfers between devices, shards(): lax.all_to_all(own_slabs, HALF, split_axis=0, concat_axis=0, tiled=True)  7.85 us
    all_to_all x1, starting transfers between devices, shards(): lax.all_to_all(partial_term.reshape(ff_dev, groups, feat_dev), DP, split_...  7.65 us
  transfers between devices with their start and end apart: 9, of which 6 were waited for; matrix products, arithmetic and copies ran while one was open for 11% of the time, Pallas kernels for 0%

profile of v12, /device:TPU:228, one launch (start us, length us, event | category | flops | bytes accessed | tf_op | source)
XLA Modules:
  0.0 336.3 jit_solution(9179407645504107547)
XLA Ops:
  0.6 1.5 collective-permute-start
  2.9 4.1 %gather_fusion = bf16[8,896,256]{2,1,0:T(8,128)(2,1)} fusion(bf16[4,896,256]{2,1,0:T(8,128)(2,1)} %param.8, s32[1024]{0:T(1024)S(1)} %pad_clamp_fusion.1), kind=kCustom, calls=%fused_computation | custom fusion | bytes 7340064 | tf_op jit(solution)/shard_map/jit(_take)/gather | solution.py:24
  7.0 8.9 %collective-permute-done = bf16[32,4096]{1,0:T(8,128)(2,1)S(1)} collective-permute-done((bf16[32,4096]{1,0:T(8,128)(2,1)}, bf16[32,4096]{1,0:T(8,128)(2,1)S(1)}, u32[]{:S(2)}, u32[]{:S(2)}) %collective-permute-start) | collective-permute-done | bytes 262176 | tf_op jit(solution)/shard_map/ppermute | solution.py:19
  15.9 7.8 %all-to-all-start = ((bf16[8,896,256]{2,1,0:T(8,128)(2,1)}), bf16[8,896,256]{2,1,0:T(8,128)(2,1)}, u32[]{:S(2)}, u32[]{:S(2)}) async-start(bf16[8,896,256]{2,1,0:T(8,128)(2,1)} %gather_fusion), calls=%async_computation | async-start | bytes 7340032 | tf_op jit(solution)/shard_map/all_to_all | solution.py:26
  23.8 1.9 collective-permute-start.5
  25.7 79.3 %collective-permute-done.5 = bf16[4,896,256]{2,1,0:T(8,128)(2,1)} collective-permute-done((bf16[4,896,256]{2,1,0:T(8,128)(2,1)S(1)}, bf16[4,896,256]{2,1,0:T(8,128)(2,1)}, u32[]{:S(2)}, u32[]{:S(2)}) %collective-permute-start.5) | collective-permute-done | bytes 1835040 | tf_op jit(solution)/shard_map/ppermute | solution.py:27
  104.9 4.1 %gather_fusion.2 = bf16[8,896,256]{2,1,0:T(8,128)(2,1)} fusion(bf16[4,896,256]{2,1,0:T(8,128)(2,1)} %collective-permute-done.5, s32[1024]{0:T(1024)S(1)} %pad_clamp_fusion.1), kind=kCustom, calls=%fused_computation.2 | custom fusion | bytes 7340064 | tf_op jit(solution)/shard_map/jit(_take)/gather | solution.py:28
  109.0 5.8 %all-to-all-start.1 = ((bf16[8,896,256]{2,1,0:T(8,128)(2,1)}), bf16[8,896,256]{2,1,0:T(8,128)(2,1)}, u32[]{:S(2)}, u32[]{:S(2)}) async-start(bf16[8,896,256]{2,1,0:T(8,128)(2,1)} %gather_fusion.2), calls=%async_computation.1 | async-start | bytes 7340032 | tf_op jit(solution)/shard_map/all_to_all | solution.py:29
  115.7 3.1 collective-permute-start.3
  119.4 1.0 collective-permute-start.1
  120.5 16.8 %collective-permute-done.3 = bf16[2,32,4096]{2,1,0:T(8,128)(2,1)S(1)} collective-permute-done((bf16[2,32,4096]{2,1,0:T(8,128)(2,1)S(1)}, bf16[2,32,4096]{2,1,0:T(8,128)(2,1)S(1)}, u32[]{:S(2)}, u32[]{:S(2)}) %collective-permute-start.3) | collective-permute-done | bytes 524320 | tf_op jit(solution)/shard_map/ppermute | solution.py:36
  137.3 3.7 %collective-permute-done.1 = bf16[2,32,4096]{2,1,0:T(8,128)(2,1)S(1)} collective-permute-done((bf16[2,32,4096]{2,1,0:T(8,128)(2,1)S(1)}, bf16[2,32,4096]{2,1,0:T(8,128)(2,1)S(1)}, u32[]{:S(2)}, u32[]{:S(2)}) %collective-permute-start.1) | collective-permute-done | bytes 524320 | tf_op jit(solution)/shard_map/ppermute | solution.py:36
  141.3 2.0 gather_fusion.1
  143.3 4.4 %collective-permute-done.4 = bf16[4,2,32,4096]{3,2,1,0:T(8,128)(2,1)S(1)} collective-permute-done((bf16[4,2,32,4096]{3,2,1,0:T(8,128)(2,1)}, bf16[4,2,32,4096]{3,2,1,0:T(8,128)(2,1)S(1)}, u32[]{:S(2)}, u32[]{:S(2)}) %collective-permute-start.4) | collective-permute-done | bytes 2097184 | tf_op jit(solution)/shard_map/ppermute | solution.py:40
  147.6 2.8 fusion
  151.6 0.9 copy-done.4
  152.5 4.5 %convolution_convert_fusion = bf16[896,4096]{1,0:T(8,128)(2,1)S(1)} fusion(bf16[512,4096]{1,0:T(8,128)(2,1)S(1)} %bitcast.42, bf16[512,896]{1,0:T(8,128)(2,1)S(1)} %copy-done.4, bf16[512,896]{1,0:T(8,128)(2,1)S(1)} %copy-done.3), kind=kOutput, calls=%fused_computation.5 | convolution fusion | flops 3765436416 | bytes 13369344 | tf_op jit(solution)/shard_map/dot_general | solution.py:60
  157.1 3.8 %copy.42 = bf16[112,16,8,256]{3,2,0,1:T(8,128)(2,1)} copy(bf16[112,16,8,256]{3,2,1,0:T(8,128)(2,1)S(1)} %bitcast.46) | data formatting | bytes 14680064 | tf_op jit(solution)/shard_map/reshape | solution.py:64
  160.8 7.7 %all-to-all-start.2 = ((bf16[896,16,256]{2,0,1:T(8,128)(2,1)}), bf16[896,16,256]{2,0,1:T(8,128)(2,1)}, u32[]{:S(2)}, u32[]{:S(2)}) async-start(bf16[896,16,256]{2,0,1:T(8,128)(2,1)} %bitcast.41), calls=%async_computation.2 | async-start | bytes 14680064 | tf_op jit(solution)/shard_map/all_to_all | solution.py:63
  168.5 3.6 %copy.28 = bf16[64,8,16,256]{3,2,1,0:T(8,128)(2,1)S(1)} copy(bf16[64,8,16,256]{3,1,2,0:T(8,128)(2,1)} %bitcast.43) | data formatting | bytes 8388608
  172.4 4.4 %fusion.3 = f32[512,896,1]{1,0,2:T(8,128)S(1)} fusion(bf16[8,896,256]{2,1,0:T(8,128)(2,1)} %all-to-all-done, bf16[512,1,8,256]{3,2,1,0:T(8,128)(2,1)S(1)} %get-tuple-element.43), kind=kOutput, calls=%fused_computation.16 | convolution fusion | flops 1879048192 | bytes 7602176 | tf_op jit(solution)/shard_map/tsd,sfd->tf/dot_general | solution.py:52
  176.8 6.3 %multiply_convert_fusion = (bf16[512,896]{1,0:T(8,128)(2,1)}, bf16[512,896]{1,0:T(8,128)(2,1)}) fusion(bf16[512,896]{1,0:T(8,128)(2,1)S(1)} %copy-done.3, bf16[512,896]{1,0:T(8,128)(2,1)S(1)} %copy-done.4, bf16[8,896,256]{2,1,0:T(8,128)(2,1)} %all-to-all-done.1, bf16[512,1,8,256]{3,2,1,0:T(8,128)(2,1)S(1)} %get-tuple-element.42, f32[512,896,1]{1,0,2:T(8,128)S(1)} %fusion.3), kind=kOutput, calls=%fused_computation.29 | convolution fusion | flops 1886388224 | bytes 11272192 | tf_op jit(solution)/shard_map/tsd,sfd->tf/dot_general | solution.py:54
  183.1 144.1 %all-to-all-done.2 = bf16[896,16,256]{2,0,1:T(8,128)(2,1)} async-done(((bf16[896,16,256]{2,0,1:T(8,128)(2,1)}), bf16[896,16,256]{2,0,1:T(8,128)(2,1)}, u32[]{:S(2)}, u32[]{:S(2)}) %all-to-all-start.2) | async-done | bytes 7340064 | tf_op jit(solution)/shard_map/all_to_all | solution.py:63
  327.2 9.1 %convert_reduce_fusion = f32[4,896,256]{2,1,0:T(8,128)} fusion(bf16[16,896,256]{2,1,0:T(8,128)(2,1)} %bitcast.16, bf16[4,16]{1,0:T(4,128)(2,1)S(1)} %fusion.18), kind=kLoop, calls=%fused_computation.3 | loop fusion | flops 43122688 | bytes 11010176 | tf_op jit(solution)/shard_map/reduce_sum | solution.py:71
  (29 shorter events, 4.0 us)
Async XLA Ops:
  0.6 15.3 %collective-permute-start = (bf16[32,4096]{1,0:T(8,128)(2,1)}, bf16[32,4096]{1,0:T(8,128)(2,1)S(1)}, u32[]{:S(2)}, u32[]{:S(2)}) collective-permute-start(bf16[32,4096]{1,0:T(8,128)(2,1)} %param.5), channel_id=1, source_target_pairs={{0,8},{8,0},{1,9},{9,1},{2,10},{10,2},{3,11},{11,3},{4,12},{12,4},... | collective-permute-start | bytes 786440 | tf_op jit(solution)/shard_map/ppermute | solution.py:19
  7.0 16.8 %copy-start.1 = (bf16[4,896,256]{2,1,0:T(8,128)(2,1)S(1)}, bf16[4,896,256]{2,1,0:T(8,128)(2,1)}, u32[]{:S(2)}) copy-start(bf16[4,896,256]{2,1,0:T(8,128)(2,1)} %param.8) | copy-start | bytes 5505028
  15.9 93.1 %all-to-all-start = ((bf16[8,896,256]{2,1,0:T(8,128)(2,1)}), bf16[8,896,256]{2,1,0:T(8,128)(2,1)}, u32[]{:S(2)}, u32[]{:S(2)}) async-start(bf16[8,896,256]{2,1,0:T(8,128)(2,1)} %gather_fusion), calls=%async_computation | async-start | bytes 7340032 | tf_op jit(solution)/shard_map/all_to_all | solution.py:26
  23.8 81.1 %collective-permute-start.5 = (bf16[4,896,256]{2,1,0:T(8,128)(2,1)S(1)}, bf16[4,896,256]{2,1,0:T(8,128)(2,1)}, u32[]{:S(2)}, u32[]{:S(2)}) collective-permute-start(bf16[4,896,256]{2,1,0:T(8,128)(2,1)S(1)} %copy-done.1), channel_id=1, source_target_pairs={{0,128},{128,0},{1,129},{129,1},{2,130},{130,2},{3,131},{131,3},{4... | collective-permute-start | bytes 5505032 | tf_op jit(solution)/shard_map/ppermute | solution.py:27
  109.0 6.6 %copy-start.2 = (bf16[32,4096]{1,0:T(8,128)(2,1)S(1)}, bf16[32,4096]{1,0:T(8,128)(2,1)}, u32[]{:S(2)}) copy-start(bf16[32,4096]{1,0:T(8,128)(2,1)} %param.5) | copy-start | bytes 786436
  109.0 51.8 %all-to-all-start.1 = ((bf16[8,896,256]{2,1,0:T(8,128)(2,1)}), bf16[8,896,256]{2,1,0:T(8,128)(2,1)}, u32[]{:S(2)}, u32[]{:S(2)}) async-start(bf16[8,896,256]{2,1,0:T(8,128)(2,1)} %gather_fusion.2), calls=%async_computation.1 | async-start | bytes 7340032 | tf_op jit(solution)/shard_map/all_to_all | solution.py:29
  115.7 21.6 %collective-permute-start.3 = (bf16[2,32,4096]{2,1,0:T(8,128)(2,1)S(1)}, bf16[2,32,4096]{2,1,0:T(8,128)(2,1)S(1)}, u32[]{:S(2)}, u32[]{:S(2)}) collective-permute-start(bf16[2,32,4096]{2,1,0:T(8,128)(2,1)S(1)} %maximum_select_fusion.2), channel_id=1, source_target_pairs={{0,6},{2,0},{4,2},{6,4},{1,7},{3,1},{5,3},{7,5},{8,14},{10,8},{12,... | collective-permute-start | bytes 1572872 | tf_op jit(solution)/shard_map/ppermute | solution.py:36
  118.8 18.5 %collective-permute-start.2 = (bf16[2,32,4096]{2,1,0:T(8,128)(2,1)S(1)}, bf16[2,32,4096]{2,1,0:T(8,128)(2,1)S(1)}, u32[]{:S(2)}, u32[]{:S(2)}) collective-permute-start(bf16[2,32,4096]{2,1,0:T(8,128)(2,1)S(1)} %maximum_select_fusion.2), channel_id=1, source_target_pairs={{0,4},{2,6},{4,0},{6,2},{1,5},{3,7},{5,1},{7,3},{8,12},{10,14},{12... | collective-permute-start | bytes 1572872 | tf_op jit(solution)/shard_map/ppermute | solution.py:36
  119.4 21.6 %collective-permute-start.1 = (bf16[2,32,4096]{2,1,0:T(8,128)(2,1)S(1)}, bf16[2,32,4096]{2,1,0:T(8,128)(2,1)S(1)}, u32[]{:S(2)}, u32[]{:S(2)}) collective-permute-start(bf16[2,32,4096]{2,1,0:T(8,128)(2,1)S(1)} %maximum_select_fusion.2), channel_id=1, source_target_pairs={{0,2},{2,4},{4,6},{6,0},{1,3},{3,5},{5,7},{7,1},{8,10},{10,12},{12... | collective-permute-start | bytes 1572872 | tf_op jit(solution)/shard_map/ppermute | solution.py:36
  143.3 4.4 %collective-permute-start.4 = (bf16[4,2,32,4096]{3,2,1,0:T(8,128)(2,1)}, bf16[4,2,32,4096]{3,2,1,0:T(8,128)(2,1)S(1)}, u32[]{:S(2)}, u32[]{:S(2)}) collective-permute-start(bf16[4,2,32,4096]{3,2,1,0:T(8,128)(2,1)} %gather_fusion.1), channel_id=1, source_target_pairs={{0,1},{1,0},{2,3},{3,2},{4,5},{5,4},{6,7},{7,6},{8,9},{9,8},{10,11... | collective-permute-start | bytes 6291464 | tf_op jit(solution)/shard_map/ppermute | solution.py:40
  150.5 1.2 copy-start.3
  150.5 2.0 copy-start.4
  150.8 6.3 %copy-start = (bf16[2,4,2,32,4096]{4,3,2,1,0:T(8,128)(2,1)}, bf16[2,4,2,32,4096]{4,3,2,1,0:T(8,128)(2,1)S(1)}, u32[]{:S(2)}) copy-start(bf16[2,4,2,32,4096]{4,3,2,1,0:T(8,128)(2,1)S(1)} %copy.22) | copy-start | bytes 12582916
  160.8 7.7 %copy-start.5 = (s32[16]{0:T(128)S(1)}, s32[16]{0:T(128)}, u32[]{:S(2)}) copy-start(s32[16]{0:T(128)} %param.9) | copy-start | bytes 196
  160.8 166.3 %all-to-all-start.2 = ((bf16[896,16,256]{2,0,1:T(8,128)(2,1)}), bf16[896,16,256]{2,0,1:T(8,128)(2,1)}, u32[]{:S(2)}, u32[]{:S(2)}) async-start(bf16[896,16,256]{2,0,1:T(8,128)(2,1)} %bitcast.41), calls=%async_computation.2 | async-start | bytes 14680064 | tf_op jit(solution)/shard_map/all_to_all | solution.py:63

commit v13 on v4

--- a/solution.py
+++ b/solution.py
@@ -67,7 +67,8 @@
         concat_axis=1,
         tiled=True,
     )
-    d_weight = jnp.einsum("lg,fgd->lfd", selector, pieces, preferred_element_type=jnp.float32)
+    d_fld = jnp.sum(selector[None, :, :, None] * pieces[:, None], axis=2, dtype=jnp.float32)
+    d_weight = jnp.transpose(d_fld, (1, 0, 2))
     return (d_gate, d_up, d_weight)
 
 

time: 340 us -> 375 us (1.10)
  other arithmetic: 4.01 us -> 36.6 us
  local copies, waits for them, and re-layouts: 23.1 us -> 33.4 us
  matrix products: 22.6 us -> 15.2 us
    reduce_sum x0 -> x1, other arithmetic: none -> 32.6 us  [shards(): jnp.sum(selector[None, :, :, None] * pieces[:, None], axis=2, dtype=jnp.f...]
    all_to_all x0 -> x1, local copies, waits for them, and re-layouts: none -> 10.3 us  [shards(): lax.all_to_all(partial_term.reshape(ff_dev, groups, feat_dev), DP, split_...]
    dot_general x1 -> x0, matrix products: 7.39 us -> none  [shards(): jnp.einsum('lg,fgd->lfd', selector, pieces, preferred_element_type=jnp.fl...]
  transfers between devices with their start and end apart: 9 -> 9, of which waited for: 6 -> 6; matrix products, arithmetic and copies ran while one was open for 11% -> 10% of each run, Pallas kernels for 0% -> 0%
where the time goes in v13:
time: 375 us; the launch traced here: 372 us
  waiting for transfers between devices  257 us (69%)
  other arithmetic  36.6 us (10%)
  local copies, waits for them, and re-layouts  33.4 us (9%)
  starting transfers between devices  29.4 us (8%)
  matrix products  15.2 us (4%)
    all_to_all x1, waiting for transfers between devices, shards(): lax.all_to_all(partial_term.reshape(ff_dev, groups, feat_dev), DP, split_...  144 us
    ppermute x1, waiting for transfers between devices, shards(): block = lax.ppermute(w_down, 'zh2', [(0, 1), (1, 0)])  79.3 us
    reduce_sum x1, other arithmetic, shards(): jnp.sum(selector[None, :, :, None] * pieces[:, None], axis=2, dtype=jnp.f...  32.6 us
    ppermute x3, waiting for transfers between devices, shards(): lax.ppermute(pair, 'y', [(i, (i + shift) % ring) for i in range(ring)])  20.5 us
    all_to_all x1, local copies, waits for them, and re-layouts, shards(): lax.all_to_all(partial_term.reshape(ff_dev, groups, feat_dev), DP, split_...  10.3 us
    ppermute x1, waiting for transfers between devices, shards(): partner = lax.ppermute(cotangent, 'zh', [(0, 1), (1, 0)])  8.95 us
    unnamed x14, local copies, waits for them, and re-layouts  7.86 us
    all_to_all x1, starting transfers between devices, shards(): lax.all_to_all(own_slabs, HALF, split_axis=0, concat_axis=0, tiled=True)  7.85 us
  transfers between devices with their start and end apart: 9, of which 6 were waited for; matrix products, arithmetic and copies ran while one was open for 10% of the time, Pallas kernels for 0%

profile of v13, /device:TPU:228, one launch (start us, length us, event | category | flops | bytes accessed | tf_op | source)
XLA Modules:
  0.0 372.5 jit_solution(8322771173629188144)
XLA Ops:
  0.6 1.5 collective-permute-start
  2.9 4.1 %gather_fusion = bf16[8,896,256]{2,1,0:T(8,128)(2,1)} fusion(bf16[4,896,256]{2,1,0:T(8,128)(2,1)} %param.8, s32[1024]{0:T(1024)S(1)} %pad_clamp_fusion.1), kind=kCustom, calls=%fused_computation | custom fusion | bytes 7340064 | tf_op jit(solution)/shard_map/jit(_take)/gather | solution.py:24
  7.0 8.9 %collective-permute-done = bf16[32,4096]{1,0:T(8,128)(2,1)S(1)} collective-permute-done((bf16[32,4096]{1,0:T(8,128)(2,1)}, bf16[32,4096]{1,0:T(8,128)(2,1)S(1)}, u32[]{:S(2)}, u32[]{:S(2)}) %collective-permute-start) | collective-permute-done | bytes 262176 | tf_op jit(solution)/shard_map/ppermute | solution.py:19
  15.9 7.8 %all-to-all-start = ((bf16[8,896,256]{2,1,0:T(8,128)(2,1)}), bf16[8,896,256]{2,1,0:T(8,128)(2,1)}, u32[]{:S(2)}, u32[]{:S(2)}) async-start(bf16[8,896,256]{2,1,0:T(8,128)(2,1)} %gather_fusion), calls=%async_computation | async-start | bytes 7340032 | tf_op jit(solution)/shard_map/all_to_all | solution.py:26
  23.8 1.9 collective-permute-start.5
  25.7 79.3 %collective-permute-done.5 = bf16[4,896,256]{2,1,0:T(8,128)(2,1)} collective-permute-done((bf16[4,896,256]{2,1,0:T(8,128)(2,1)S(1)}, bf16[4,896,256]{2,1,0:T(8,128)(2,1)}, u32[]{:S(2)}, u32[]{:S(2)}) %collective-permute-start.5) | collective-permute-done | bytes 1835040 | tf_op jit(solution)/shard_map/ppermute | solution.py:27
  104.9 4.1 %gather_fusion.2 = bf16[8,896,256]{2,1,0:T(8,128)(2,1)} fusion(bf16[4,896,256]{2,1,0:T(8,128)(2,1)} %collective-permute-done.5, s32[1024]{0:T(1024)S(1)} %pad_clamp_fusion.1), kind=kCustom, calls=%fused_computation.2 | custom fusion | bytes 7340064 | tf_op jit(solution)/shard_map/jit(_take)/gather | solution.py:28
  109.0 5.8 %all-to-all-start.1 = ((bf16[8,896,256]{2,1,0:T(8,128)(2,1)}), bf16[8,896,256]{2,1,0:T(8,128)(2,1)}, u32[]{:S(2)}, u32[]{:S(2)}) async-start(bf16[8,896,256]{2,1,0:T(8,128)(2,1)} %gather_fusion.2), calls=%async_computation.1 | async-start | bytes 7340032 | tf_op jit(solution)/shard_map/all_to_all | solution.py:29
  115.7 3.1 collective-permute-start.3
  120.5 16.8 %collective-permute-done.3 = bf16[2,32,4096]{2,1,0:T(8,128)(2,1)S(1)} collective-permute-done((bf16[2,32,4096]{2,1,0:T(8,128)(2,1)S(1)}, bf16[2,32,4096]{2,1,0:T(8,128)(2,1)S(1)}, u32[]{:S(2)}, u32[]{:S(2)}) %collective-permute-start.3) | collective-permute-done | bytes 524320 | tf_op jit(solution)/shard_map/ppermute | solution.py:36
  137.3 3.7 collective-permute-done.1
  141.3 2.0 gather_fusion.1
  143.3 4.4 %collective-permute-done.4 = bf16[4,2,32,4096]{3,2,1,0:T(8,128)(2,1)S(1)} collective-permute-done((bf16[4,2,32,4096]{3,2,1,0:T(8,128)(2,1)}, bf16[4,2,32,4096]{3,2,1,0:T(8,128)(2,1)S(1)}, u32[]{:S(2)}, u32[]{:S(2)}) %collective-permute-start.4) | collective-permute-done | bytes 2097184 | tf_op jit(solution)/shard_map/ppermute | solution.py:40
  147.6 2.8 fusion
  152.5 4.5 %convolution_convert_fusion = bf16[896,4096]{1,0:T(8,128)(2,1)S(1)} fusion(bf16[512,4096]{1,0:T(8,128)(2,1)S(1)} %bitcast.42, bf16[512,896]{1,0:T(8,128)(2,1)S(1)} %copy-done.4, bf16[512,896]{1,0:T(8,128)(2,1)S(1)} %copy-done.3), kind=kOutput, calls=%fused_computation.5 | convolution fusion | flops 3765436416 | bytes 13369344 | tf_op jit(solution)/shard_map/dot_general | solution.py:60
  157.0 3.8 %copy.42 = bf16[112,16,8,256]{3,2,0,1:T(8,128)(2,1)} copy(bf16[112,16,8,256]{3,2,1,0:T(8,128)(2,1)S(1)} %bitcast.47) | data formatting | bytes 14680064 | tf_op jit(solution)/shard_map/reshape | solution.py:64
  160.8 7.7 %all-to-all-start.2 = ((bf16[896,16,256]{2,0,1:T(8,128)(2,1)}), bf16[896,16,256]{2,0,1:T(8,128)(2,1)}, u32[]{:S(2)}, u32[]{:S(2)}) async-start(bf16[896,16,256]{2,0,1:T(8,128)(2,1)} %bitcast.41), calls=%async_computation.2 | async-start | bytes 14680064 | tf_op jit(solution)/shard_map/all_to_all | solution.py:63
  168.5 3.6 copy.28
  172.4 4.4 %fusion.3 = f32[512,896,1]{1,0,2:T(8,128)S(1)} fusion(bf16[8,896,256]{2,1,0:T(8,128)(2,1)} %all-to-all-done, bf16[512,1,8,256]{3,2,1,0:T(8,128)(2,1)S(1)} %get-tuple-element.46), kind=kOutput, calls=%fused_computation.16 | convolution fusion | flops 1879048192 | bytes 7602176 | tf_op jit(solution)/shard_map/tsd,sfd->tf/dot_general | solution.py:52
  176.8 6.3 %multiply_convert_fusion = (bf16[512,896]{1,0:T(8,128)(2,1)}, bf16[512,896]{1,0:T(8,128)(2,1)}) fusion(bf16[512,896]{1,0:T(8,128)(2,1)S(1)} %copy-done.3, bf16[512,896]{1,0:T(8,128)(2,1)S(1)} %copy-done.4, bf16[8,896,256]{2,1,0:T(8,128)(2,1)} %all-to-all-done.1, bf16[512,1,8,256]{3,2,1,0:T(8,128)(2,1)S(1)} %get-tuple-element.45, f32[512,896,1]{1,0,2:T(8,128)S(1)} %fusion.3), kind=kOutput, calls=%fused_computation.29 | convolution fusion | flops 1886388224 | bytes 11272192 | tf_op jit(solution)/shard_map/tsd,sfd->tf/dot_general | solution.py:54
  183.1 144.1 %all-to-all-done.2 = bf16[896,16,256]{2,0,1:T(8,128)(2,1)} async-done(((bf16[896,16,256]{2,0,1:T(8,128)(2,1)}), bf16[896,16,256]{2,0,1:T(8,128)(2,1)}, u32[]{:S(2)}, u32[]{:S(2)}) %all-to-all-start.2) | async-done | bytes 7340064 | tf_op jit(solution)/shard_map/all_to_all | solution.py:63
  327.1 10.3 %copy.25 = bf16[896,16,256]{2,1,0:T(8,128)(2,1)} copy(bf16[896,16,256]{2,0,1:T(8,128)(2,1)} %all-to-all-done.2) | data formatting | bytes 14680064 | tf_op jit(solution)/shard_map/all_to_all | solution.py:63
  337.4 32.6 %convert_reduce_fusion = f32[896,4,256]{2,1,0:T(4,128)S(1)} fusion(bf16[896,16,256]{2,1,0:T(8,128)(2,1)} %copy.25, bf16[4,16]{1,0:T(4,128)(2,1)S(1)} %fusion.18), kind=kLoop, calls=%fused_computation.3 | loop fusion | flops 43122688 | bytes 11010176 | tf_op jit(solution)/shard_map/reduce_sum | solution.py:70
  370.0 2.5 copy.26
  (31 shorter events, 5.9 us)
Async XLA Ops:
  0.6 15.3 %collective-permute-start = (bf16[32,4096]{1,0:T(8,128)(2,1)}, bf16[32,4096]{1,0:T(8,128)(2,1)S(1)}, u32[]{:S(2)}, u32[]{:S(2)}) collective-permute-start(bf16[32,4096]{1,0:T(8,128)(2,1)} %param.5), channel_id=1, source_target_pairs={{0,8},{8,0},{1,9},{9,1},{2,10},{10,2},{3,11},{11,3},{4,12},{12,4},... | collective-permute-start | bytes 786440 | tf_op jit(solution)/shard_map/ppermute | solution.py:19
  7.0 16.8 %copy-start.1 = (bf16[4,896,256]{2,1,0:T(8,128)(2,1)S(1)}, bf16[4,896,256]{2,1,0:T(8,128)(2,1)}, u32[]{:S(2)}) copy-start(bf16[4,896,256]{2,1,0:T(8,128)(2,1)} %param.8) | copy-start | bytes 5505028
  15.9 93.1 %all-to-all-start = ((bf16[8,896,256]{2,1,0:T(8,128)(2,1)}), bf16[8,896,256]{2,1,0:T(8,128)(2,1)}, u32[]{:S(2)}, u32[]{:S(2)}) async-start(bf16[8,896,256]{2,1,0:T(8,128)(2,1)} %gather_fusion), calls=%async_computation | async-start | bytes 7340032 | tf_op jit(solution)/shard_map/all_to_all | solution.py:26
  23.8 81.1 %collective-permute-start.5 = (bf16[4,896,256]{2,1,0:T(8,128)(2,1)S(1)}, bf16[4,896,256]{2,1,0:T(8,128)(2,1)}, u32[]{:S(2)}, u32[]{:S(2)}) collective-permute-start(bf16[4,896,256]{2,1,0:T(8,128)(2,1)S(1)} %copy-done.1), channel_id=1, source_target_pairs={{0,128},{128,0},{1,129},{129,1},{2,130},{130,2},{3,131},{131,3},{4... | collective-permute-start | bytes 5505032 | tf_op jit(solution)/shard_map/ppermute | solution.py:27
  109.0 6.6 %copy-start.2 = (bf16[32,4096]{1,0:T(8,128)(2,1)S(1)}, bf16[32,4096]{1,0:T(8,128)(2,1)}, u32[]{:S(2)}) copy-start(bf16[32,4096]{1,0:T(8,128)(2,1)} %param.5) | copy-start | bytes 786436
  109.0 51.8 %all-to-all-start.1 = ((bf16[8,896,256]{2,1,0:T(8,128)(2,1)}), bf16[8,896,256]{2,1,0:T(8,128)(2,1)}, u32[]{:S(2)}, u32[]{:S(2)}) async-start(bf16[8,896,256]{2,1,0:T(8,128)(2,1)} %gather_fusion.2), calls=%async_computation.1 | async-start | bytes 7340032 | tf_op jit(solution)/shard_map/all_to_all | solution.py:29
  115.7 21.6 %collective-permute-start.3 = (bf16[2,32,4096]{2,1,0:T(8,128)(2,1)S(1)}, bf16[2,32,4096]{2,1,0:T(8,128)(2,1)S(1)}, u32[]{:S(2)}, u32[]{:S(2)}) collective-permute-start(bf16[2,32,4096]{2,1,0:T(8,128)(2,1)S(1)} %maximum_select_fusion.2), channel_id=1, source_target_pairs={{0,6},{2,0},{4,2},{6,4},{1,7},{3,1},{5,3},{7,5},{8,14},{10,8},{12,... | collective-permute-start | bytes 1572872 | tf_op jit(solution)/shard_map/ppermute | solution.py:36
  118.8 18.5 %collective-permute-start.2 = (bf16[2,32,4096]{2,1,0:T(8,128)(2,1)S(1)}, bf16[2,32,4096]{2,1,0:T(8,128)(2,1)S(1)}, u32[]{:S(2)}, u32[]{:S(2)}) collective-permute-start(bf16[2,32,4096]{2,1,0:T(8,128)(2,1)S(1)} %maximum_select_fusion.2), channel_id=1, source_target_pairs={{0,4},{2,6},{4,0},{6,2},{1,5},{3,7},{5,1},{7,3},{8,12},{10,14},{12... | collective-permute-start | bytes 1572872 | tf_op jit(solution)/shard_map/ppermute | solution.py:36
  119.4 21.6 %collective-permute-start.1 = (bf16[2,32,4096]{2,1,0:T(8,128)(2,1)S(1)}, bf16[2,32,4096]{2,1,0:T(8,128)(2,1)S(1)}, u32[]{:S(2)}, u32[]{:S(2)}) collective-permute-start(bf16[2,32,4096]{2,1,0:T(8,128)(2,1)S(1)} %maximum_select_fusion.2), channel_id=1, source_target_pairs={{0,2},{2,4},{4,6},{6,0},{1,3},{3,5},{5,7},{7,1},{8,10},{10,12},{12... | collective-permute-start | bytes 1572872 | tf_op jit(solution)/shard_map/ppermute | solution.py:36
  143.3 4.4 %collective-permute-start.4 = (bf16[4,2,32,4096]{3,2,1,0:T(8,128)(2,1)}, bf16[4,2,32,4096]{3,2,1,0:T(8,128)(2,1)S(1)}, u32[]{:S(2)}, u32[]{:S(2)}) collective-permute-start(bf16[4,2,32,4096]{3,2,1,0:T(8,128)(2,1)} %gather_fusion.1), channel_id=1, source_target_pairs={{0,1},{1,0},{2,3},{3,2},{4,5},{5,4},{6,7},{7,6},{8,9},{9,8},{10,11... | collective-permute-start | bytes 6291464 | tf_op jit(solution)/shard_map/ppermute | solution.py:40
  150.5 1.2 copy-start.3
  150.5 2.0 copy-start.4
  150.8 6.3 %copy-start = (bf16[2,4,2,32,4096]{4,3,2,1,0:T(8,128)(2,1)}, bf16[2,4,2,32,4096]{4,3,2,1,0:T(8,128)(2,1)S(1)}, u32[]{:S(2)}) copy-start(bf16[2,4,2,32,4096]{4,3,2,1,0:T(8,128)(2,1)S(1)} %copy.20) | copy-start | bytes 12582916
  160.8 7.7 %copy-start.5 = (s32[16]{0:T(128)S(1)}, s32[16]{0:T(128)}, u32[]{:S(2)}) copy-start(s32[16]{0:T(128)} %param.9) | copy-start | bytes 196
  160.8 166.3 %all-to-all-start.2 = ((bf16[896,16,256]{2,0,1:T(8,128)(2,1)}), bf16[896,16,256]{2,0,1:T(8,128)(2,1)}, u32[]{:S(2)}, u32[]{:S(2)}) async-start(bf16[896,16,256]{2,0,1:T(8,128)(2,1)} %bitcast.41), calls=%async_computation.2 | async-start | bytes 14680064 | tf_op jit(solution)/shard_map/all_to_all | solution.py:63
